TPU v7x, 32 devices: a whole 2x2x4 slice. The times are simulated.
32 devices in a mesh: fsdp: 16 (over z, x, core), dp: 2 (over y).
Axes of the slice: x: 2, y: 2, z: 4, core: 2. Of those that a mesh axis runs over, the one named last changes fastest.
Arguments:
- tokens: bfloat16 [16384, 768], P(('fsdp', 'dp')), may hold values from -6 to 6
- cotangent: float32 [16384, 768], P(('fsdp', 'dp')), may hold values from -6 to 6
- lengths: int32 [32], P(('fsdp', 'dp')), may hold values from 128 to 512, as said below
- step_count: int32 [1], replicated, may hold values from 1 to 3
- attention_master: float32 [3072, 768], P(('fsdp', 'dp')), may hold values from -0.4330127 to 0.4330127
- attention_first: float32 [3072, 768], P(('fsdp', 'dp')), may hold values from -224 to 224
- attention_second: float32 [3072, 768], P(('fsdp', 'dp')), may hold values from 589.824 to 9584.64
- feed_master: float32 [6144, 768], P(('fsdp', 'dp')), may hold values from -0.14433757 to 0.14433757
- feed_first: float32 [6144, 768], P(('fsdp', 'dp')), may hold values from -320 to 320
- feed_second: float32 [6144, 768], P(('fsdp', 'dp')), may hold values from 1048.576 to 17039.36
- small_master: float32 [9216], P(('fsdp', 'dp')), may hold values from -2 to 2
- small_first: float32 [9216], P(('fsdp', 'dp')), may hold values from -640 to 640
- small_second: float32 [9216], P(('fsdp', 'dp')), may hold values from 4194.304 to 68157.44
Outputs:
- layer_out: bfloat16 [16384, 768], P(('fsdp', 'dp'))
- tokens_grad: float32 [16384, 768], P(('fsdp', 'dp'))
- attention_new: float32 [3072, 768], P(('fsdp', 'dp'))
- attention_first_new: float32 [3072, 768], P(('fsdp', 'dp'))
- attention_second_new: float32 [3072, 768], P(('fsdp', 'dp'))
- attention_copy: bfloat16 [3072, 768], P(('fsdp', 'dp'))
- feed_new: float32 [6144, 768], P(('fsdp', 'dp'))
- feed_first_new: float32 [6144, 768], P(('fsdp', 'dp'))
- feed_second_new: float32 [6144, 768], P(('fsdp', 'dp'))
- feed_copy: bfloat16 [6144, 768], P(('fsdp', 'dp'))
- small_new: float32 [9216], P(('fsdp', 'dp'))
- small_first_new: float32 [9216], P(('fsdp', 'dp'))
- small_second_new: float32 [9216], P(('fsdp', 'dp'))
- small_copy: bfloat16 [9216], P(('fsdp', 'dp'))
- rms_values: float32 [3], replicated
Inputs may be any that keep to these rules, and one draw needn't show every extreme that they name: `lengths`: one sequence has exactly 512 valid tokens and one exactly 128.
All inputs are finite; a program needn't handle non-finite values.
Results may differ from a plain program's by a relative error of at most 0.011.
The roundings to bfloat16 on the way count: a program that leaves them out, or rounds other values in their place, can miss the bound.
Values may be sent and summed in bfloat16 or wider, within the bound.
No kernel may reach another device: no remote copies, remote signals or barrier semaphores. Data moves between devices by JAX's collectives and lax.ppermute only.
A program may use at most 192 MiB of HBM per device.

v0:
```python
import math

import jax
import jax.numpy as jnp
from jax import lax
from jax.sharding import PartitionSpec as P

D = 768
HEADS = 12
HDIM = 64
FF = 3072
SEQ = 512


ln_epsilon = 1e-12
beta_first = 0.5
beta_second = 0.55
adam_epsilon = 1e-06
rate_matrix = 0.04
rate_small = 0.25
weight_decay = 0.01


def product(left_side, right_side):
    return jnp.dot(left_side, right_side, preferred_element_type=jnp.float32)


def product_rows(left_side, right_side):
    return lax.dot_general(
        left_side, right_side, (((0,), (0,)), ((), ())), preferred_element_type=jnp.float32
    )


def product_cols(left_side, right_side):
    return lax.dot_general(
        left_side, right_side, (((1,), (1,)), ((), ())), preferred_element_type=jnp.float32
    )


def column_total(entries):
    return jnp.sum(entries, axis=0, dtype=jnp.float32)


def layer_norm(entries, norm_gain, norm_shift):
    center = jnp.mean(entries, axis=-1, keepdims=True)
    offset = entries - center
    spread = jnp.mean(offset * offset, axis=-1, keepdims=True)
    return offset * lax.rsqrt(spread + ln_epsilon) * norm_gain + norm_shift


def gelu_exact(entries):
    return jax.nn.gelu(entries, approximate=False)


def split_small(small_full):
    pieces = []
    position = 0
    for length in (D, D, D, FF, D, D, D, D, D):
        pieces.append(small_full[position : position + length].astype(jnp.float32))
        position = position + length
    return pieces


def head_view(entries):
    return entries.reshape(SEQ, HEADS, HDIM)


def masked_scores(queries, key_vectors, key_valid):
    scores = jnp.einsum(
        "qhd,khd->hqk",
        head_view(queries),
        head_view(key_vectors),
        preferred_element_type=jnp.float32,
    ) * (1.0 / math.sqrt(HDIM))
    return jnp.where(key_valid[None, None, :] > 0, scores, -1e30)


def attend_forward(pieces):
    queries, key_vectors, values, key_valid = pieces
    scores = masked_scores(queries, key_vectors, key_valid)
    row_max = jnp.max(scores, axis=-1, keepdims=True)
    exponent = jnp.exp(scores - row_max)
    row_total = jnp.sum(exponent, axis=-1, keepdims=True)
    probability = (exponent / row_total).astype(jnp.bfloat16)
    attended = jnp.einsum(
        "hqk,khd->qhd", probability, head_view(values), preferred_element_type=jnp.float32
    )
    return (attended.reshape(SEQ, D).astype(jnp.bfloat16), (row_max + jnp.log(row_total))[:, :, 0])


def attend_backward(pieces):
    queries, key_vectors, values, key_valid, log_total, attended_grad = pieces
    scores = masked_scores(queries, key_vectors, key_valid)
    probability = jnp.exp(scores - log_total[:, :, None])
    probability_low = probability.astype(jnp.bfloat16)
    grad_heads = head_view(attended_grad)
    value_grad = jnp.einsum(
        "hqk,qhd->khd", probability_low, grad_heads, preferred_element_type=jnp.float32
    )
    probability_grad = jnp.einsum(
        "qhd,khd->hqk", grad_heads, head_view(values), preferred_element_type=jnp.float32
    )
    inner_total = jnp.sum(probability * probability_grad, axis=-1, keepdims=True)
    score_grad = (probability * (probability_grad - inner_total)).astype(jnp.bfloat16)
    score_scale = 1.0 / math.sqrt(HDIM)
    query_grad = (
        jnp.einsum(
            "hqk,khd->qhd", score_grad, head_view(key_vectors), preferred_element_type=jnp.float32
        )
        * score_scale
    )
    key_grad = (
        jnp.einsum(
            "hqk,qhd->khd", score_grad, head_view(queries), preferred_element_type=jnp.float32
        )
        * score_scale
    )
    return (
        query_grad.reshape(SEQ, D).astype(jnp.bfloat16),
        key_grad.reshape(SEQ, D).astype(jnp.bfloat16),
        value_grad.reshape(SEQ, D).astype(jnp.bfloat16),
    )


def adam_step(master, first_moment, second, gradient, step_rate, decay_rate, step_float):
    first_new = beta_first * first_moment + (1.0 - beta_first) * gradient
    second_new = beta_second * second + (1.0 - beta_second) * gradient * gradient
    first_hat = first_new / (1.0 - beta_first**step_float)
    second_hat = second_new / (1.0 - beta_second**step_float)
    master_new = master - step_rate * (
        first_hat / (jnp.sqrt(second_hat) + adam_epsilon) + decay_rate * master
    )
    return (master_new, first_new, second_new)


def on_device(
    tokens,
    cotangent,
    lengths,
    step_count,
    attention_master,
    attention_first,
    attention_second,
    feed_master,
    feed_first,
    feed_second,
    small_master,
    small_first,
    small_second,
):
    row_count = tokens.shape[0]
    sequence_count = row_count // SEQ
    attention_work = attention_master.astype(jnp.bfloat16)
    feed_work = feed_master.astype(jnp.bfloat16)
    small_work = small_master.astype(jnp.bfloat16)
    attention_full, feed_full, small_full = (
        lax.all_gather(attention_work, ("fsdp", "dp"), axis=0, tiled=True),
        lax.all_gather(feed_work, ("fsdp", "dp"), axis=0, tiled=True),
        lax.all_gather(small_work, ("fsdp", "dp"), axis=0, tiled=True),
    )
    key_valid = (
        lax.broadcasted_iota(jnp.int32, (sequence_count, SEQ), 1) < lengths[:, None]
    ).astype(jnp.float32)
    token_valid = key_valid.reshape(row_count)
    (
        query_bias,
        value_bias,
        output_bias,
        inner_bias,
        outer_bias,
        first_gain,
        first_shift,
        second_gain,
        second_shift,
    ) = split_small(small_full)
    queries = (product(tokens, attention_full[0:D]) + query_bias).astype(jnp.bfloat16)
    key_vectors = product(tokens, attention_full[D : 2 * D]).astype(jnp.bfloat16)
    values = (product(tokens, attention_full[2 * D : 3 * D]) + value_bias).astype(jnp.bfloat16)
    seq_shape = (sequence_count, SEQ, D)
    attended, log_total = lax.map(
        attend_forward,
        (
            queries.reshape(seq_shape),
            key_vectors.reshape(seq_shape),
            values.reshape(seq_shape),
            key_valid,
        ),
    )
    attended = attended.reshape(row_count, D)
    branch_attention = product(attended, attention_full[3 * D : 4 * D]) + output_bias
    first_sum = tokens.astype(jnp.float32) + branch_attention
    normed = layer_norm(first_sum, first_gain, first_shift)
    normed_low = normed.astype(jnp.bfloat16)
    inner_sum = product_cols(normed_low, feed_full[0:FF]) + inner_bias
    active = gelu_exact(inner_sum).astype(jnp.bfloat16)
    branch_feed = product(active, feed_full[FF : 2 * FF]) + outer_bias
    residual = normed + branch_feed
    layer_out = layer_norm(residual, second_gain, second_shift).astype(jnp.bfloat16)
    column = token_valid[:, None]
    local_squares = jnp.stack(
        [
            jnp.sum(residual * residual * column),
            jnp.sum(branch_attention * branch_attention * column),
            jnp.sum(branch_feed * branch_feed * column),
        ]
    )
    square_totals, counted = lax.psum((local_squares, jnp.sum(token_valid)), ("fsdp", "dp"))
    rms_values = jnp.sqrt(square_totals / (counted * D))
    attention_back, feed_back, small_back = (
        lax.all_gather(attention_work, ("fsdp", "dp"), axis=0, tiled=True),
        lax.all_gather(feed_work, ("fsdp", "dp"), axis=0, tiled=True),
        lax.all_gather(small_work, ("fsdp", "dp"), axis=0, tiled=True),
    )
    back_pieces = split_small(small_back)
    first_gain_back = back_pieces[5]
    first_shift_back = back_pieces[6]
    second_gain_back = back_pieces[7]
    second_shift_back = back_pieces[8]
    query_weight = attention_back[0:D]
    key_weight = attention_back[D : 2 * D]
    value_weight = attention_back[2 * D : 3 * D]
    output_weight = attention_back[3 * D : 4 * D]
    inner_weight = feed_back[0:FF]
    outer_weight = feed_back[FF : 2 * FF]
    second_pull = jax.vjp(layer_norm, residual, second_gain_back, second_shift_back)[1]
    residual_grad, second_gain_grad, second_shift_grad = second_pull(cotangent)
    feed_out_grad = residual_grad.astype(jnp.bfloat16)
    outer_bias_grad = column_total(feed_out_grad)
    outer_weight_grad = product_rows(active, feed_out_grad)
    active_grad = product_cols(feed_out_grad, outer_weight)
    inner_grad = jax.vjp(gelu_exact, inner_sum)[1](active_grad)[0].astype(jnp.bfloat16)
    inner_bias_grad = column_total(inner_grad)
    inner_weight_grad = product_rows(inner_grad, normed_low)
    normed_grad = residual_grad + product(inner_grad, inner_weight)
    feed_grad_all = jnp.concatenate([inner_weight_grad, outer_weight_grad], axis=0)
    first_pull = jax.vjp(layer_norm, first_sum, first_gain_back, first_shift_back)[1]
    first_sum_grad, first_gain_grad, first_shift_grad = first_pull(normed_grad)
    branch_grad_low = first_sum_grad.astype(jnp.bfloat16)
    output_bias_grad = column_total(branch_grad_low)
    output_weight_grad = product_rows(attended, branch_grad_low)
    attended_grad = product_cols(branch_grad_low, output_weight).astype(jnp.bfloat16)
    query_grad, key_grad, value_grad = lax.map(
        attend_backward,
        (
            queries.reshape(seq_shape),
            key_vectors.reshape(seq_shape),
            values.reshape(seq_shape),
            key_valid,
            log_total,
            attended_grad.reshape(seq_shape),
        ),
    )
    query_grad = query_grad.reshape(row_count, D)
    key_grad = key_grad.reshape(row_count, D)
    value_grad = value_grad.reshape(row_count, D)
    query_weight_grad = product_rows(tokens, query_grad)
    key_weight_grad = product_rows(tokens, key_grad)
    value_weight_grad = product_rows(tokens, value_grad)
    query_bias_grad = column_total(query_grad)
    value_bias_grad = column_total(value_grad)
    tokens_grad = (
        first_sum_grad
        + product_cols(query_grad, query_weight)
        + product_cols(key_grad, key_weight)
        + product_cols(value_grad, value_weight)
    )
    attention_grad_all = jnp.concatenate(
        [query_weight_grad, key_weight_grad, value_weight_grad, output_weight_grad], axis=0
    )
    small_grad_all = jnp.concatenate(
        [
            query_bias_grad,
            value_bias_grad,
            output_bias_grad,
            inner_bias_grad,
            outer_bias_grad,
            first_gain_grad,
            first_shift_grad,
            second_gain_grad,
            second_shift_grad,
        ]
    )
    attention_owned, feed_owned, small_owned = (
        lax.psum_scatter(attention_grad_all, ("fsdp", "dp"), scatter_dimension=0, tiled=True),
        lax.psum_scatter(feed_grad_all, ("fsdp", "dp"), scatter_dimension=0, tiled=True),
        lax.psum_scatter(small_grad_all, ("fsdp", "dp"), scatter_dimension=0, tiled=True),
    )
    step_float = step_count[0].astype(jnp.float32)
    attention_new, attention_first_new, attention_second_new = adam_step(
        attention_master,
        attention_first,
        attention_second,
        attention_owned,
        rate_matrix,
        weight_decay,
        step_float,
    )
    feed_new, feed_first_new, feed_second_new = adam_step(
        feed_master, feed_first, feed_second, feed_owned, rate_matrix, weight_decay, step_float
    )
    small_new, small_first_new, small_second_new = adam_step(
        small_master, small_first, small_second, small_owned, rate_small, 0.0, step_float
    )
    return (
        layer_out,
        tokens_grad,
        attention_new,
        attention_first_new,
        attention_second_new,
        attention_new.astype(jnp.bfloat16),
        feed_new,
        feed_first_new,
        feed_second_new,
        feed_new.astype(jnp.bfloat16),
        small_new,
        small_first_new,
        small_second_new,
        small_new.astype(jnp.bfloat16),
        rms_values,
    )


def solution(mesh):
    placed = (
        P(("fsdp", "dp"), None),
        P(("fsdp", "dp"), None),
        P(("fsdp", "dp")),
        P(),
        P(("fsdp", "dp"), None),
        P(("fsdp", "dp"), None),
        P(("fsdp", "dp"), None),
        P(("fsdp", "dp"), None),
        P(("fsdp", "dp"), None),
        P(("fsdp", "dp"), None),
        P(("fsdp", "dp")),
        P(("fsdp", "dp")),
        P(("fsdp", "dp")),
    )
    return jax.shard_map(
        on_device,
        mesh=mesh,
        in_specs=placed,
        out_specs=(
            P(("fsdp", "dp"), None),
            P(("fsdp", "dp"), None),
            P(("fsdp", "dp"), None),
            P(("fsdp", "dp"), None),
            P(("fsdp", "dp"), None),
            P(("fsdp", "dp"), None),
            P(("fsdp", "dp"), None),
            P(("fsdp", "dp"), None),
            P(("fsdp", "dp"), None),
            P(("fsdp", "dp"), None),
            P(("fsdp", "dp")),
            P(("fsdp", "dp")),
            P(("fsdp", "dp")),
            P(("fsdp", "dp")),
            P(),
        ),
        check_vma=False,
    )
```

profile of v0, /device:TPU:0, one launch (start us, length us, event | category | flops | bytes accessed | tf_op | source)
XLA Modules:
  0.0 595.2 jit_solution(15256771966233240500)
XLA Ops:
  12.5 42.4 %all-reduce = bf16[9216]{0:T(1024)(128)(2,1)S(1)} all-reduce(bf16[9216]{0:T(1024)(128)(2,1)S(1)} %dynamic-update-slice), channel_id=1, replica_groups=mesh['fsdp'=16,'dp'=2] {'fsdp','dp'}, use_global_device_ids=true, to_apply=%add | all-reduce | flops 9216 | bytes 36864
  54.9 23.0 %all-gather.3.cloned.1.call-done = bf16[3072,768]{1,0:T(8,128)(2,1)} async-done(((bf16[96,768]{1,0:T(8,128)(2,1)}), bf16[3072,768]{1,0:T(8,128)(2,1)}) %all-gather.3.cloned.1.call-update) | async-done | bytes 4718608 | tf_op jit(solution)/shard_map/all_gather | solution.py:157
  77.9 2.3 add_convert_fusion.3
  80.5 2.3 add_convert_fusion.2
  83.2 3.2 convolution_convert_fusion.1
  87.8 3.0 fusion.61
  92.8 2.7 copy-done
  95.5 2.5 fusion.27
  98.0 3.6 fusion.60
  101.9 59.4 %all-gather.5.cloned.1.call-done = bf16[6144,768]{1,0:T(8,128)(2,1)} async-done(((bf16[192,768]{1,0:T(8,128)(2,1)}), bf16[6144,768]{1,0:T(8,128)(2,1)}) %all-gather.5.cloned.1.call-update) | async-done | bytes 9437200 | tf_op jit(solution)/shard_map/all_gather | solution.py:158
  161.3 20.0 %multiply_convert_fusion.1 = (bf16[512,3072]{1,0:T(8,128)(2,1)S(1)}, f32[512,3072]{1,0:T(8,128)S(1)}, f32[512,3072]{1,0:T(8,128)}) fusion(f32[3072]{0:T(1024)S(1)} %slice_convert_fusion, bf16[6144,768]{1,0:T(8,128)(2,1)} %all-gather.5.cloned.1.call-done, f32[512,768]{1,0:T(8,128)S(1)} %get-tuple-element.103, f32[768]{0:T(1024)S(1)} %get-tuple-element.109, ...), kind=kOutput, calls=%fused_computation.16 | convolution fusion | flops 2521694208 | bytes 22042624 | tf_op jit(solution)/shard_map/dot_general | solution.py:35
  181.3 3.6 multiply_reduce_fusion.2
  188.6 7.1 %convert_reduce_fusion = (f32[3072]{0:T(1024)S(1)}, bf16[512,3072]{1,0:T(8,128)(2,1)S(1)}) fusion(f32[512,3072]{1,0:T(8,128)S(1)} %get-tuple-element.101, bf16[512,768]{1,0:T(8,128)(2,1)S(1)} %get-tuple-element.83, bf16[6144,768]{1,0:T(8,128)(2,1)S(1)} %copy-done.26, f32[512,3072]{1,0:T(8,128)} %get-tuple-element.118, f32[3072]{0:T(1024)S(1)} %slice_convert_fusion), kind=kOutput, calls=%fused_computation.13 | convolution fusion | flops 2442654720 | bytes 21258240 | tf_op jit(solution)/shard_map/dot_general | solution.py:35
  195.7 3.0 multiply_reduce_fusion.5
  200.5 3.0 convolution_convert_fusion
  203.5 2.3 copy.52
  205.8 12.1 %multiply_reduce_fusion = (f32[12,512]{1,0:T(8,128)S(1)}, f32[12,512,512]{1,2,0:T(8,128)}) fusion(f32[12,512,512]{1,2,0:T(8,128)} %copy-done, f32[12,512]{1,0:T(8,128)S(1)} %log_add_fusion, bf16[512,12,64]{0,2,1:T(8,128)(2,1)} %bitcast.67, bf16[512,12,64]{0,2,1:T(8,128)(2,1)} %bitcast.76), kind=kOutput, calls=%fused_computation.2 | convolution fusion | flops 412084224 | bytes 26787840 | tf_op jit(solution)/shard_map/while/body/eval_jaxpr/qhd,khd->hqk/dot_general | solution.py:100
  218.0 7.2 %multiply_convert_fusion = bf16[12,512,512]{1,2,0:T(8,128)(2,1)S(1)} fusion(f32[12,512,512]{1,2,0:T(8,128)} %get-tuple-element.121, f32[12,512,512]{1,2,0:T(8,128)S(1)} %bitcast.64, f32[12,512]{1,0:T(8,128)S(1)} %get-tuple-element.120, f32[12,512]{1,0:T(8,128)S(1)} %log_add_fusion), kind=kLoop, calls=%fused_computation.1 | loop fusion | flops 12582912 | bytes 31506432 | tf_op jit(solution)/shard_map/while/body/eval_jaxpr/convert_element_type | solution.py:104
  228.6 2.1 convert_reduce_fusion.3
  234.1 4.1 pad_maximum_fusion.1
  238.6 4.9 fusion.63
  243.5 2.8 fusion.47
  246.3 10.4 %pad_maximum_fusion = f32[6144,768]{1,0:T(8,128)} fusion(f32[3072,768]{1,0:T(8,128)S(1)} %fusion.63, f32[3072,768]{1,0:T(8,128)S(1)} %fusion.47), kind=kLoop, calls=%fused_computation | loop fusion | flops 4718592 | bytes 37748736 | tf_op jit(solution)/shard_map/concatenate | solution.py:235
  258.4 2.0 pad_maximum_fusion.2
  260.5 40.3 %all-reduce.2 = (f32[9216]{0:T(1024)S(1)}, f32[3]{0:T(128)S(1)}, f32[]{:T(128)}) all-reduce(f32[9216]{0:T(1024)S(1)} %constant_dynamic-update-slice_fusion, f32[3]{0:T(128)S(1)} %pad_maximum_fusion.2, f32[]{:T(128)} %fusion.43), channel_id=4, replica_groups=mesh['fsdp'=16,'dp'=2] {'fsdp','dp'}, use_global_device_ids=true, to_apply=%region_22.23.clone | all-reduce | flops 9220 | bytes 73760
  302.7 2.4 fusion.31
  305.0 2.1 fusion.34
  307.2 3.6 add_add_fusion.2
  310.9 62.2 %reduce-scatter.3.cloned.1.call-done = f32[96,768]{1,0:T(8,128)} async-done(((f32[3072,768]{1,0:T(8,128)}), f32[96,768]{1,0:T(8,128)}) %reduce-scatter.3.cloned.1.call-update) | async-done | bytes 294928 | tf_op jit(solution)/shard_map/reduce_scatter | solution.py:284
  373.1 2.2 fusion.54
  375.3 209.8 %reduce-scatter.5.cloned.1.call-done = f32[192,768]{1,0:T(8,128)} async-done(((f32[6144,768]{1,0:T(8,128)}), f32[192,768]{1,0:T(8,128)}) %reduce-scatter.5.cloned.1.call-update) | async-done | bytes 589840 | tf_op jit(solution)/shard_map/reduce_scatter | solution.py:285
  585.2 3.0 fusion.52
  (124 shorter events, 23.4 us)
Async XLA Ops:
  7.2 73.4 %copy-start.1 = (bf16[512,768]{1,0:T(8,128)(2,1)S(1)}, bf16[512,768]{1,0:T(8,128)(2,1)}, u32[]{:S(2)}) copy-start(bf16[512,768]{1,0:T(8,128)(2,1)} %param.13) | copy-start | bytes 2359300
  7.2 70.8 %all-gather.3.cloned.1.call-start = ((), (), s32[]{:S(2)}) async-start(), calls=%async_computation.2 | async-start | bytes 4866048 | tf_op jit(solution)/shard_map/all_gather | solution.py:157
  9.0 152.3 %all-gather.5.cloned.1.call-start = ((), (), s32[]{:S(2)}) async-start(), calls=%async_computation.3 | async-start | bytes 9732096 | tf_op jit(solution)/shard_map/all_gather | solution.py:158
  10.8 362.2 %reduce-scatter.3.cloned.1.call-start = ((), (), s32[]{:S(2)}) async-start(), calls=%async_computation.4 | async-start | bytes 9732096 | tf_op jit(solution)/shard_map/reduce_scatter | solution.py:284
  80.5 12.3 %copy-start.13 = (bf16[512,768]{0,1:T(8,128)(2,1)}, bf16[512,768]{0,1:T(8,128)(2,1)S(1)}, u32[]{:S(2)}) copy-start(bf16[512,768]{0,1:T(8,128)(2,1)S(1)} %copy.48) | copy-start | bytes 2359300
  83.2 7.7 %copy-start.8 = (bf16[512,768]{0,1:T(8,128)(2,1)}, bf16[512,768]{0,1:T(8,128)(2,1)S(1)}, u32[]{:S(2)}) copy-start(bf16[512,768]{0,1:T(8,128)(2,1)S(1)} %copy.49) | copy-start | bytes 2359300
  87.8 3.1 copy-start.3
  90.9 4.6 copy-start
  97.9 83.3 %copy-start.14 = (bf16[12,64,512]{2,1,0:T(8,128)(2,1)}, bf16[12,64,512]{2,1,0:T(8,128)(2,1)S(1)}, u32[]{:S(2)}) copy-start(bf16[12,64,512]{2,1,0:T(8,128)(2,1)S(1)} %fusion.27) | copy-start | bytes 2359300
  161.3 20.0 %copy-start.20 = (f32[512,768]{1,0:T(8,128)S(1)}, f32[512,768]{1,0:T(8,128)}, u32[]{:S(2)}) copy-start(f32[512,768]{1,0:T(8,128)} %get-tuple-element.117) | copy-start | bytes 4718596
  161.3 20.0 %copy-start.26 = (bf16[6144,768]{1,0:T(8,128)(2,1)S(1)}, bf16[6144,768]{1,0:T(8,128)(2,1)}, u32[]{:S(2)}) copy-start(bf16[6144,768]{1,0:T(8,128)(2,1)} %all-gather.5.cloned.1.call-done) | copy-start | bytes 28311556
  181.3 3.6 copy-start.27
  181.3 3.9 copy-start.12
  188.6 7.1 %copy-start.22 = (bf16[512,768]{1,0:T(8,128)(2,1)}, bf16[512,768]{1,0:T(8,128)(2,1)S(1)}, u32[]{:S(2)}) copy-start(bf16[512,768]{1,0:T(8,128)(2,1)S(1)} %get-tuple-element.83) | copy-start | bytes 2359300
  195.7 3.0 copy-start.28
  205.8 12.1 %slice-start = ((s8[12582912]{0:T(1024)(128)(4,1)}), s8[4194304]{0:T(1024)(128)(4,1)S(1)}, s32[]{:S(2)}) async-start(s8[12582912]{0:T(1024)(128)(4,1)} %bitcast.63), calls=%async_computation.6 | async-start | bytes 8388608
  205.8 12.1 %slice-start.1 = ((s8[12582912]{0:T(1024)(128)(4,1)}), s8[4194304]{0:T(1024)(128)(4,1)S(1)}, s32[]{:S(2)}) async-start(s8[12582912]{0:T(1024)(128)(4,1)} %bitcast.63), calls=%async_computation.7 | async-start | bytes 8388608
  205.8 12.1 %slice-start.2 = ((s8[12582912]{0:T(1024)(128)(4,1)}), s8[4194304]{0:T(1024)(128)(4,1)S(1)}, s32[]{:S(2)}) async-start(s8[12582912]{0:T(1024)(128)(4,1)} %bitcast.63), calls=%async_computation.8 | async-start | bytes 8388608
  218.0 7.2 %copy-start.9 = (bf16[512,768]{0,1:T(8,128)(2,1)S(1)}, bf16[512,768]{0,1:T(8,128)(2,1)}, u32[]{:S(2)}) copy-start(bf16[512,768]{0,1:T(8,128)(2,1)} %copy-done.8) | copy-start | bytes 2359300
  227.2 5.2 copy-start.18
  228.6 4.7 copy-start.10
  228.6 2.9 copy-start.2
  230.7 2.5 copy-start.6
  238.2 346.9 %reduce-scatter.5.cloned.1.call-start = ((), (), s32[]{:S(2)}) async-start(), calls=%async_computation.5 | async-start | bytes 19464192 | tf_op jit(solution)/shard_map/reduce_scatter | solution.py:285
  238.6 4.9 copy-start.29
  256.7 45.2 %copy-start.23 = (f32[288]{0:T(512)S(1)}, f32[288]{0:T(512)}, u32[]{:S(2)}) copy-start(f32[288]{0:T(512)} %param.23) | copy-start | bytes 3460
  256.7 45.2 %copy-start.24 = (f32[288]{0:T(512)S(1)}, f32[288]{0:T(512)}, u32[]{:S(2)}) copy-start(f32[288]{0:T(512)} %param.25) | copy-start | bytes 3460
  256.7 45.2 %copy-start.25 = (f32[288]{0:T(512)S(1)}, f32[288]{0:T(512)}, u32[]{:S(2)}) copy-start(f32[288]{0:T(512)} %param.24) | copy-start | bytes 3460
  256.7 48.3 %copy-start.11 = (bf16[12,64,512]{2,1,0:T(8,128)(2,1)S(1)}, bf16[12,64,512]{2,1,0:T(8,128)(2,1)}, u32[]{:S(2)}) copy-start(bf16[12,64,512]{2,1,0:T(8,128)(2,1)} %copy-done.10) | copy-start | bytes 2359300
  256.8 50.4 %copy-start.7 = (bf16[12,64,512]{2,1,0:T(8,128)(2,1)S(1)}, bf16[12,64,512]{2,1,0:T(8,128)(2,1)}, u32[]{:S(2)}) copy-start(bf16[12,64,512]{2,1,0:T(8,128)(2,1)} %copy-done.6) | copy-start | bytes 2359300
  307.2 65.9 %copy-start.21 = (f32[96,768]{1,0:T(8,128)S(1)}, f32[96,768]{1,0:T(8,128)}, u32[]{:S(2)}) copy-start(f32[96,768]{1,0:T(8,128)} %param.17) | copy-start | bytes 884740
  307.2 277.9 %copy-start.19 = (f32[192,768]{1,0:T(8,128)S(1)}, f32[192,768]{1,0:T(8,128)}, u32[]{:S(2)}) copy-start(f32[192,768]{1,0:T(8,128)} %param.20) | copy-start | bytes 1769476
  (5 other events, 8.7 us)
Sparse Core Ops, SparseCore 0:
  11.5 66.4 all-gather.2
  81.4 79.7 all-gather.4
  238.3 134.7 reduce-scatter.2
  379.4 205.7 reduce-scatter.4
where the time goes:
time: 604 us; the launch traced here: 595 us
  waiting for transfers between devices  355 us (59%)
  matrix products  90.1 us (15%)
  blocking collectives  82.7 us (14%)
  other arithmetic  41.6 us (7%)
  between operations  17.1 us (3%)
  local copies, waits for them, and re-layouts  8.73 us (1%)
    reduce_scatter x1, waiting for transfers between devices, on_device(): lax.psum_scatter(feed_grad_all, ('fsdp', 'dp'), scatter_dimension=0, tile...  210 us
    unnamed x2, blocking collectives  82.7 us
    reduce_scatter x1, waiting for transfers between devices, on_device(): lax.psum_scatter(attention_grad_all, ('fsdp', 'dp'), scatter_dimension=0,...  62.2 us
    all_gather x1, waiting for transfers between devices, on_device(): lax.all_gather(feed_work, ('fsdp', 'dp'), axis=0, tiled=True)  59.4 us
    dot_general x6, matrix products, product_cols(): lax.dot_general(left_side, right_side, (((1,), (1,)), ((), ())), preferre...  38.2 us
    all_gather x1, waiting for transfers between devices, on_device(): lax.all_gather(attention_work, ('fsdp', 'dp'), axis=0, tiled=True)  23 us
    dot_general x6, matrix products, product(): return jnp.dot(left_side, right_side, preferred_element_type=jnp.float32)  18 us
    dot_general x1, matrix products, attend_backward(): jnp.einsum('qhd,khd->hqk', grad_heads, head_view(values), preferred_eleme...  12.1 us
  transfers between devices with their start and end apart: 4, of which 4 were waited for; matrix products, arithmetic and copies ran while one was open for 9% of the time, Pallas kernels for 0%

commit v1 on v0

--- a/solution.py
+++ b/solution.py
@@ -131,6 +131,74 @@
         first_hat / (jnp.sqrt(second_hat) + adam_epsilon) + decay_rate * master
     )
     return (master_new, first_new, second_new)
+
+
+def padded_rows(rows, multiple):
+    return -(-rows // multiple) * multiple
+
+
+def gather_working(attention_master, feed_master, small_master):
+    attention_rows = attention_master.shape[0]
+    feed_rows = feed_master.shape[0]
+    small_count = small_master.shape[0]
+    main_rows = attention_rows + feed_rows
+    extra_rows = padded_rows(main_rows + padded_rows(small_count, D) // D, 16) - main_rows
+    small_flat = jnp.zeros((extra_rows * D,), jnp.bfloat16)
+    small_flat = small_flat.at[:small_count].set(small_master.astype(jnp.bfloat16))
+    block = jnp.concatenate(
+        [
+            attention_master.astype(jnp.bfloat16),
+            feed_master.astype(jnp.bfloat16),
+            small_flat.reshape(extra_rows, D),
+        ],
+        axis=0,
+    )
+    gathered = lax.all_gather(block, ("fsdp", "dp"), axis=0, tiled=False)
+    owners = gathered.shape[0]
+    attention_full = gathered[:, :attention_rows].reshape(owners * attention_rows, D)
+    feed_full = gathered[:, attention_rows:main_rows].reshape(owners * feed_rows, D)
+    small_full = gathered[:, main_rows:].reshape(owners, extra_rows * D)[:, :small_count]
+    return attention_full, feed_full, small_full.reshape(owners * small_count)
+
+
+def scatter_gradients(attention_grad_all, feed_grad_all, small_grad_all, partials):
+    owners = lax.psum(1, ("fsdp", "dp"))
+    me = lax.axis_index(("fsdp", "dp"))
+    attention_rows = attention_grad_all.shape[0] // owners
+    feed_rows = feed_grad_all.shape[0] // owners
+    small_count = small_grad_all.shape[0] // owners
+    main_rows = attention_rows + feed_rows
+    slots = partials.shape[0]
+    extra_count = small_count + owners * slots
+    extra_rows = padded_rows(main_rows + padded_rows(extra_count, D) // D, 8) - main_rows
+    slot_row = jnp.zeros((owners * slots,), jnp.float32)
+    slot_row = lax.dynamic_update_slice(slot_row, partials, (me * slots,))
+    extra = jnp.concatenate(
+        [
+            small_grad_all.reshape(owners, small_count),
+            jnp.broadcast_to(slot_row[None], (owners, owners * slots)),
+            jnp.zeros((owners, extra_rows * D - extra_count), jnp.float32),
+        ],
+        axis=1,
+    ).reshape(owners, extra_rows, D)
+    packed = jnp.concatenate(
+        [
+            attention_grad_all.reshape(owners, attention_rows, D),
+            feed_grad_all.reshape(owners, feed_rows, D),
+            extra,
+        ],
+        axis=1,
+    ).reshape(owners * (main_rows + extra_rows), D)
+    owned = lax.psum_scatter(packed, ("fsdp", "dp"), scatter_dimension=0, tiled=True)
+    attention_owned = owned[:attention_rows]
+    feed_owned = owned[attention_rows:main_rows]
+    extra_owned = owned[main_rows:].reshape(extra_rows * D)
+    small_owned = extra_owned[:small_count]
+    gathered_partials = extra_owned[small_count:extra_count].reshape(owners, slots)
+    totals = gathered_partials[0]
+    for index in range(1, owners):
+        totals = totals + gathered_partials[index]
+    return attention_owned, feed_owned, small_owned, totals
 
 
 def on_device(
@@ -150,14 +218,7 @@
 ):
     row_count = tokens.shape[0]
     sequence_count = row_count // SEQ
-    attention_work = attention_master.astype(jnp.bfloat16)
-    feed_work = feed_master.astype(jnp.bfloat16)
-    small_work = small_master.astype(jnp.bfloat16)
-    attention_full, feed_full, small_full = (
-        lax.all_gather(attention_work, ("fsdp", "dp"), axis=0, tiled=True),
-        lax.all_gather(feed_work, ("fsdp", "dp"), axis=0, tiled=True),
-        lax.all_gather(small_work, ("fsdp", "dp"), axis=0, tiled=True),
-    )
+    attention_full, feed_full, small_full = gather_working(attention_master, feed_master, small_master)
     key_valid = (
         lax.broadcasted_iota(jnp.int32, (sequence_count, SEQ), 1) < lengths[:, None]
     ).astype(jnp.float32)
@@ -197,32 +258,21 @@
     residual = normed + branch_feed
     layer_out = layer_norm(residual, second_gain, second_shift).astype(jnp.bfloat16)
     column = token_valid[:, None]
-    local_squares = jnp.stack(
+    partials = jnp.stack(
         [
             jnp.sum(residual * residual * column),
             jnp.sum(branch_attention * branch_attention * column),
             jnp.sum(branch_feed * branch_feed * column),
+            jnp.sum(token_valid),
         ]
     )
-    square_totals, counted = lax.psum((local_squares, jnp.sum(token_valid)), ("fsdp", "dp"))
-    rms_values = jnp.sqrt(square_totals / (counted * D))
-    attention_back, feed_back, small_back = (
-        lax.all_gather(attention_work, ("fsdp", "dp"), axis=0, tiled=True),
-        lax.all_gather(feed_work, ("fsdp", "dp"), axis=0, tiled=True),
-        lax.all_gather(small_work, ("fsdp", "dp"), axis=0, tiled=True),
-    )
-    back_pieces = split_small(small_back)
-    first_gain_back = back_pieces[5]
-    first_shift_back = back_pieces[6]
-    second_gain_back = back_pieces[7]
-    second_shift_back = back_pieces[8]
-    query_weight = attention_back[0:D]
-    key_weight = attention_back[D : 2 * D]
-    value_weight = attention_back[2 * D : 3 * D]
-    output_weight = attention_back[3 * D : 4 * D]
-    inner_weight = feed_back[0:FF]
-    outer_weight = feed_back[FF : 2 * FF]
-    second_pull = jax.vjp(layer_norm, residual, second_gain_back, second_shift_back)[1]
+    query_weight = attention_full[0:D]
+    key_weight = attention_full[D : 2 * D]
+    value_weight = attention_full[2 * D : 3 * D]
+    output_weight = attention_full[3 * D : 4 * D]
+    outer_weight = feed_full[FF : 2 * FF]
+    inner_weight = feed_full[0:FF]
+    second_pull = jax.vjp(layer_norm, residual, second_gain, second_shift)[1]
     residual_grad, second_gain_grad, second_shift_grad = second_pull(cotangent)
     feed_out_grad = residual_grad.astype(jnp.bfloat16)
     outer_bias_grad = column_total(feed_out_grad)
@@ -233,7 +283,7 @@
     inner_weight_grad = product_rows(inner_grad, normed_low)
     normed_grad = residual_grad + product(inner_grad, inner_weight)
     feed_grad_all = jnp.concatenate([inner_weight_grad, outer_weight_grad], axis=0)
-    first_pull = jax.vjp(layer_norm, first_sum, first_gain_back, first_shift_back)[1]
+    first_pull = jax.vjp(layer_norm, first_sum, first_gain, first_shift)[1]
     first_sum_grad, first_gain_grad, first_shift_grad = first_pull(normed_grad)
     branch_grad_low = first_sum_grad.astype(jnp.bfloat16)
     output_bias_grad = column_total(branch_grad_low)
@@ -280,11 +330,10 @@
             second_shift_grad,
         ]
     )
-    attention_owned, feed_owned, small_owned = (
-        lax.psum_scatter(attention_grad_all, ("fsdp", "dp"), scatter_dimension=0, tiled=True),
-        lax.psum_scatter(feed_grad_all, ("fsdp", "dp"), scatter_dimension=0, tiled=True),
-        lax.psum_scatter(small_grad_all, ("fsdp", "dp"), scatter_dimension=0, tiled=True),
-    )
+    attention_owned, feed_owned, small_owned, totals = scatter_gradients(
+        attention_grad_all, feed_grad_all, small_grad_all, partials
+    )
+    rms_values = jnp.sqrt(totals[:3] / (totals[3] * D))
     step_float = step_count[0].astype(jnp.float32)
     attention_new, attention_first_new, attention_second_new = adam_step(
         attention_master,

time: 604 us -> 563 us (0.932)
  blocking collectives: 82.7 us -> 0 us
  local copies, waits for them, and re-layouts: 8.73 us -> 28.5 us
  waiting for transfers between devices: 355 us -> 370 us
  other arithmetic: 41.6 us -> 50.1 us
    unnamed x2 -> x0, blocking collectives: 82.7 us -> none
    all_gather x2 -> x1, waiting for transfers between devices: 82.4 us -> 107 us  [gather_working(): gathered = lax.all_gather(block, ('fsdp', 'dp'), axis=0, tiled=False)]
    slice x0 -> x6, local copies, waits for them, and re-layouts: none -> 15.6 us  [the longest x1 8.43 us: on_device(): branch_feed = product(active, feed_full[FF:2 * FF]) + outer_bias]
    concatenate x0 -> x2, other arithmetic: none -> 10.6 us  [the longest x1 9.8 us: scatter_gradients(): jnp.concatenate([attention_grad_all.reshape(owners, attention_rows, D), f...]
    reduce_scatter x2 -> x1, waiting for transfers between devices: 272 us -> 262 us  [scatter_gradients(): lax.psum_scatter(packed, ('fsdp', 'dp'), scatter_dimension=0, tiled=True)]
    dot_general x6, matrix products: 11 us -> 19.4 us  [product_rows(): lax.dot_general(left_side, right_side, (((0,), (0,)), ((), ())), preferre...]
    dot_general x6, matrix products: 18 us -> 10.2 us  [product(): return jnp.dot(left_side, right_side, preferred_element_type=jnp.float32)]
  transfers between devices with their start and end apart: 4 -> 2, of which waited for: 4 -> 2; matrix products, arithmetic and copies ran while one was open for 9% -> 1% of each run, Pallas kernels for 0% -> 0%
where the time goes in v1:
time: 563 us; the launch traced here: 556 us
  waiting for transfers between devices  370 us (66%)
  matrix products  90.1 us (16%)
  other arithmetic  50.1 us (9%)
  local copies, waits for them, and re-layouts  28.5 us (5%)
  between operations  17.5 us (3%)
    reduce_scatter x1, waiting for transfers between devices, scatter_gradients(): lax.psum_scatter(packed, ('fsdp', 'dp'), scatter_dimension=0, tiled=True)  262 us
    all_gather x1, waiting for transfers between devices, gather_working(): gathered = lax.all_gather(block, ('fsdp', 'dp'), axis=0, tiled=False)  107 us
    dot_general x6, matrix products, product_cols(): lax.dot_general(left_side, right_side, (((1,), (1,)), ((), ())), preferre...  34.8 us
    dot_general x6, matrix products, product_rows(): lax.dot_general(left_side, right_side, (((0,), (0,)), ((), ())), preferre...  19.4 us
    dot_general x1, matrix products, attend_backward(): jnp.einsum('qhd,khd->hqk', grad_heads, head_view(values), preferred_eleme...  12.1 us
  transfers between devices with their start and end apart: 2, of which 2 were waited for; matrix products, arithmetic and copies ran while one was open for 1% of the time, Pallas kernels for 0%

profile of v1, /device:TPU:0, one launch (start us, length us, event | category | flops | bytes accessed | tf_op | source)
XLA Modules:
  0.0 555.8 jit_solution(227521700923529953)
XLA Ops:
  12.8 107.4 %all-gather.3.cloned.1.call-done = bf16[9728,768]{1,0:T(8,128)(2,1)} async-done(((bf16[304,768]{1,0:T(8,128)(2,1)}), bf16[9728,768]{1,0:T(8,128)(2,1)}) %all-gather.3.cloned.1.call-update) | async-done | bytes 14942224 | tf_op jit(solution)/shard_map/all_gather | solution.py:156
  121.3 3.8 fusion.41
  130.4 8.4 %fusion.40 = (bf16[16,192,768]{2,1,0:T(8,128)(2,1)}, bf16[16,192,768]{2,1,0:T(8,128)(2,1)}) fusion(bf16[32,304,768]{2,1,0:T(8,128)(2,1)} %bitcast.105), kind=kLoop, calls=%fused_computation.156 | loop fusion | bytes 18874368 | tf_op jit(solution)/shard_map/slice | solution.py:257
  140.6 3.0 fusion.42
  146.4 2.7 copy-done
  149.0 2.7 fusion.15
  153.1 19.5 %multiply_convert_fusion.1 = (bf16[512,3072]{1,0:T(8,128)(2,1)S(1)}, f32[512,3072]{1,0:T(8,128)}, f32[512,3072]{1,0:T(8,128)}) fusion(f32[3072]{0:T(1024)S(1)} %copy-done.32, bf16[3072,768]{1,0:T(8,128)(2,1)S(1)} %bitcast.120, f32[512,768]{1,0:T(8,128)S(1)} %get-tuple-element.114, f32[768]{0:T(1024)S(1)} %copy-done.35, f32[768]{0:T(1024)S(1)} %get-tuple-element.128, ...), kind=kOutput, calls=%fused_computation.17 | convolution fusion | flops 2521694208 | bytes 22042624 | tf_op jit(solution)/shard_map/dot_general | solution.py:35
  172.7 3.6 multiply_reduce_fusion.2
  180.0 8.1 %convert_reduce_fusion = (f32[3072]{0:T(1024)S(1)}, bf16[512,3072]{1,0:T(8,128)(2,1)S(1)}) fusion(f32[512,3072]{1,0:T(8,128)} %get-tuple-element.112, f32[512,3072]{1,0:T(8,128)} %get-tuple-element.135, f32[3072]{0:T(1024)S(1)} %copy-done.32, bf16[512,768]{1,0:T(8,128)(2,1)S(1)} %get-tuple-element.100, bf16[3072,768]{1,0:T(8,128)(2,1)S(1)} %bitcast.127), kind=kOutput, calls=%fused_computation.14 | convolution fusion | flops 2442654720 | bytes 21258240 | tf_op jit(solution)/shard_map/dot_general | solution.py:35
  188.2 3.1 multiply_reduce_fusion.5
  194.7 2.4 copy.35
  197.1 12.1 %multiply_reduce_fusion = (f32[12,512]{1,0:T(8,128)S(1)}, f32[12,512,512]{1,2,0:T(8,128)}) fusion(f32[12,512,512]{1,2,0:T(8,128)} %copy-done, f32[12,512]{1,0:T(8,128)S(1)} %log_add_fusion, bf16[512,12,64]{0,2,1:T(8,128)(2,1)} %bitcast.106, bf16[512,12,64]{0,2,1:T(8,128)(2,1)} %bitcast.143), kind=kOutput, calls=%fused_computation.3 | convolution fusion | flops 412084224 | bytes 26787840 | tf_op jit(solution)/shard_map/while/body/eval_jaxpr/qhd,khd->hqk/dot_general | solution.py:100
  209.3 7.2 %multiply_convert_fusion = bf16[12,512,512]{1,2,0:T(8,128)(2,1)S(1)} fusion(f32[12,512,512]{1,2,0:T(8,128)} %get-tuple-element.138, f32[12,512,512]{1,2,0:T(8,128)S(1)} %bitcast.99, f32[12,512]{1,0:T(8,128)S(1)} %get-tuple-element.137, f32[12,512]{1,0:T(8,128)S(1)} %log_add_fusion), kind=kLoop, calls=%fused_computation.2 | loop fusion | flops 12582912 | bytes 31506432 | tf_op jit(solution)/shard_map/while/body/eval_jaxpr/convert_element_type | solution.py:104
  216.5 2.9 multiply_convert_fusion.2
  219.4 2.0 convert_reduce_fusion.4
  221.4 2.9 convert_reduce_fusion.3
  224.3 5.1 fusion.46
  229.4 5.4 fusion.25
  234.8 2.2 fusion.45
  237.3 2.8 maximum_dynamic-update-slice_fusion
  241.1 2.3 concatenate.24
  244.9 2.3 convolution_bitcast_fusion
  247.1 2.3 convolution_bitcast_fusion.1
  249.5 2.2 convolution_bitcast_fusion.2
  251.7 6.1 %pad_maximum_fusion.1 = f32[6144,768]{1,0:T(8,128)S(1)} fusion(f32[3072,768]{1,0:T(8,128)S(1)} %copy-done.4, f32[3072,768]{1,0:T(8,128)} %fusion.25), kind=kLoop, calls=%fused_computation.1 | loop fusion | flops 4718592 | bytes 37748736 | tf_op jit(solution)/shard_map/concatenate | solution.py:285
  257.8 3.8 pad_maximum_fusion.2
  261.6 9.8 %pad_maximum_fusion = f32[32,296,768]{2,1,0:T(8,128)} fusion(f32[32,8,768]{2,1,0:T(8,128)S(1)} %bitcast.128, f32[32,192,768]{2,1,0:T(8,128)S(1)} %bitcast.101, f32[32,96,768]{2,1,0:T(8,128)S(1)} %bitcast.102), kind=kLoop, calls=%fused_computation | loop fusion | flops 14548992 | bytes 58195968 | tf_op jit(solution)/shard_map/concatenate | solution.py:184
  272.3 2.4 fusion.44
  275.7 2.3 add_add_fusion.2
  277.9 262.1 %reduce-scatter.2.cloned.1.call-done = f32[296,768]{1,0:T(8,128)} async-done(((f32[9472,768]{1,0:T(8,128)}), f32[296,768]{1,0:T(8,128)}) %reduce-scatter.2.cloned.1.call-update) | async-done | bytes 909328 | tf_op jit(solution)/shard_map/reduce_scatter | solution.py:192
  543.3 2.2 fusion.33
  545.5 3.0 fusion.31
  (173 shorter events, 30.3 us)
Async XLA Ops:
  7.2 113.0 %all-gather.3.cloned.1.call-start = ((), (), s32[]{:S(2)}) async-start(), calls=%async_computation.2 | async-start | bytes 15409152 | tf_op jit(solution)/shard_map/all_gather | solution.py:156
  10.9 529.2 %reduce-scatter.2.cloned.1.call-start = ((), (), s32[]{:S(2)}) async-start(), calls=%async_computation.1 | async-start | bytes 30007296 | tf_op jit(solution)/shard_map/reduce_scatter | solution.py:192
  125.1 13.7 %copy-start.26 = (bf16[8,96,768]{2,1,0:T(8,128)(2,1)}, bf16[8,96,768]{2,1,0:T(8,128)(2,1)S(1)}, u32[]{:S(2)}) copy-start(bf16[8,96,768]{2,1,0:T(8,128)(2,1)S(1)} %get-tuple-element.118) | copy-start | bytes 3538948
  125.1 14.5 %copy-start.24 = (bf16[8,96,768]{2,1,0:T(8,128)(2,1)}, bf16[8,96,768]{2,1,0:T(8,128)(2,1)S(1)}, u32[]{:S(2)}) copy-start(bf16[8,96,768]{2,1,0:T(8,128)(2,1)S(1)} %get-tuple-element.119) | copy-start | bytes 3538948
  125.1 20.3 %copy-start.12 = (bf16[8,96,768]{2,1,0:T(8,128)(2,1)}, bf16[8,96,768]{2,1,0:T(8,128)(2,1)S(1)}, u32[]{:S(2)}) copy-start(bf16[8,96,768]{2,1,0:T(8,128)(2,1)S(1)} %get-tuple-element.120) | copy-start | bytes 3538948
  130.4 8.4 %copy-start.1 = (bf16[512,768]{1,0:T(8,128)(2,1)S(1)}, bf16[512,768]{1,0:T(8,128)(2,1)}, u32[]{:S(2)}) copy-start(bf16[512,768]{1,0:T(8,128)(2,1)} %param.15) | copy-start | bytes 2359300
  143.6 5.4 copy-start
  145.5 7.6 %slice-start.3 = ((s8[4718592]{0:T(1024)(128)(4,1)}), s8[4194304]{0:T(1024)(128)(4,1)S(1)}, s32[]{:S(2)}) async-start(s8[4718592]{0:T(1024)(128)(4,1)} %bitcast.118), calls=%async_computation.6 | async-start | bytes 8388608
  146.4 5.3 copy-start.28
  151.7 20.9 %slice-start.7 = ((s8[4718592]{0:T(1024)(128)(4,1)}), s8[4194304]{0:T(1024)(128)(4,1)S(1)}, s32[]{:S(2)}) async-start(s8[4718592]{0:T(1024)(128)(4,1)} %bitcast.124), calls=%async_computation.10 | async-start | bytes 8388608
  153.1 19.5 %slice-start.8 = ((s8[4718592]{0:T(1024)(128)(4,1)}), s8[524288]{0:T(1024)(128)(4,1)S(1)}, s32[]{:S(2)}) async-start(s8[4718592]{0:T(1024)(128)(4,1)} %bitcast.124), calls=%async_computation.11 | async-start | bytes 1048576
  153.1 19.5 %copy-start.34 = (f32[512]{0:T(512)S(1)}, f32[512]{0:T(512)}, u32[]{:S(2)}) copy-start(f32[512]{0:T(512)} %get-tuple-element.143) | copy-start | bytes 6148
  153.1 19.5 %copy-start.36 = (f32[768]{0:T(1024)S(1)}, f32[768]{0:T(1024)}, u32[]{:S(2)}) copy-start(f32[768]{0:T(1024)} %get-tuple-element.126) | copy-start | bytes 9220
  178.2 10.0 %slice-start.5 = ((s8[4718592]{0:T(1024)(128)(4,1)}), s8[4194304]{0:T(1024)(128)(4,1)S(1)}, s32[]{:S(2)}) async-start(s8[4718592]{0:T(1024)(128)(4,1)} %bitcast.121), calls=%async_computation.8 | async-start | bytes 8388608
  180.0 8.1 %copy-start.29 = (bf16[512,768]{1,0:T(8,128)(2,1)}, bf16[512,768]{1,0:T(8,128)(2,1)S(1)}, u32[]{:S(2)}) copy-start(bf16[512,768]{1,0:T(8,128)(2,1)S(1)} %get-tuple-element.100) | copy-start | bytes 2359300
  180.0 8.2 %slice-start.6 = ((s8[4718592]{0:T(1024)(128)(4,1)}), s8[524288]{0:T(1024)(128)(4,1)S(1)}, s32[]{:S(2)}) async-start(s8[4718592]{0:T(1024)(128)(4,1)} %bitcast.121), calls=%async_computation.9 | async-start | bytes 1048576
  197.1 12.2 %slice-start = ((s8[12582912]{0:T(1024)(128)(4,1)}), s8[4194304]{0:T(1024)(128)(4,1)S(1)}, s32[]{:S(2)}) async-start(s8[12582912]{0:T(1024)(128)(4,1)} %bitcast.98), calls=%async_computation.3 | async-start | bytes 8388608
  197.1 12.2 %slice-start.1 = ((s8[12582912]{0:T(1024)(128)(4,1)}), s8[4194304]{0:T(1024)(128)(4,1)S(1)}, s32[]{:S(2)}) async-start(s8[12582912]{0:T(1024)(128)(4,1)} %bitcast.98), calls=%async_computation.4 | async-start | bytes 8388608
  197.1 12.2 %slice-start.2 = ((s8[12582912]{0:T(1024)(128)(4,1)}), s8[4194304]{0:T(1024)(128)(4,1)S(1)}, s32[]{:S(2)}) async-start(s8[12582912]{0:T(1024)(128)(4,1)} %bitcast.98), calls=%async_computation.5 | async-start | bytes 8388608
  209.3 7.2 %copy-start.21 = (bf16[768,512]{1,0:T(8,128)(2,1)S(1)}, bf16[768,512]{1,0:T(8,128)(2,1)}, u32[]{:S(2)}) copy-start(bf16[768,512]{1,0:T(8,128)(2,1)} %copy-done.20) | copy-start | bytes 2359300
  224.3 5.1 copy-start.43
  229.4 5.4 copy-start.17
  229.4 5.4 copy-start.19
  234.8 10.0 %copy-start.2 = (bf16[512,768]{1,0:T(8,128)(2,1)S(1)}, bf16[512,768]{1,0:T(8,128)(2,1)}, u32[]{:S(2)}) copy-start(bf16[512,768]{1,0:T(8,128)(2,1)} %param.15) | copy-start | bytes 2359300
  234.8 10.0 %copy-start.6 = (bf16[12,64,512]{2,1,0:T(8,128)(2,1)S(1)}, bf16[12,64,512]{2,1,0:T(8,128)(2,1)}, u32[]{:S(2)}) copy-start(bf16[12,64,512]{2,1,0:T(8,128)(2,1)} %get-tuple-element.142) | copy-start | bytes 2359300
  244.9 6.8 %copy-start.4 = (f32[3072,768]{1,0:T(8,128)S(1)}, f32[3072,768]{1,0:T(8,128)}, u32[]{:S(2)}) copy-start(f32[3072,768]{1,0:T(8,128)} %fusion.46) | copy-start | bytes 28311556
  251.7 6.1 %copy-start.3 = (f32[768,768]{1,0:T(8,128)S(1)}, f32[768,768]{1,0:T(8,128)}, u32[]{:S(2)}) copy-start(f32[768,768]{1,0:T(8,128)} %fusion.45) | copy-start | bytes 7077892
  275.6 267.1 %copy-start.33 = (f32[288]{0:T(512)S(1)}, f32[288]{0:T(512)}, u32[]{:S(2)}) copy-start(f32[288]{0:T(512)} %param.25) | copy-start | bytes 3460
  275.6 267.1 %copy-start.38 = (f32[288]{0:T(512)S(1)}, f32[288]{0:T(512)}, u32[]{:S(2)}) copy-start(f32[288]{0:T(512)} %param.27) | copy-start | bytes 3460
  275.6 267.1 %copy-start.39 = (f32[288]{0:T(512)S(1)}, f32[288]{0:T(512)}, u32[]{:S(2)}) copy-start(f32[288]{0:T(512)} %param.26) | copy-start | bytes 3460
  275.7 267.7 %copy-start.27 = (f32[96,768]{1,0:T(8,128)S(1)}, f32[96,768]{1,0:T(8,128)}, u32[]{:S(2)}) copy-start(f32[96,768]{1,0:T(8,128)} %param.19) | copy-start | bytes 884740
  275.7 269.9 %copy-start.23 = (f32[192,768]{1,0:T(8,128)S(1)}, f32[192,768]{1,0:T(8,128)}, u32[]{:S(2)}) copy-start(f32[192,768]{1,0:T(8,128)} %param.22) | copy-start | bytes 1769476
  (23 other events, 63.7 us)
Sparse Core Ops, SparseCore 0:
  11.5 108.6 all-gather.2
  271.5 268.4 reduce-scatter.1

commit v2 on v1

--- a/solution.py
+++ b/solution.py
@@ -161,23 +161,28 @@
     return attention_full, feed_full, small_full.reshape(owners * small_count)
 
 
-def scatter_gradients(attention_grad_all, feed_grad_all, small_grad_all, partials):
+def scatter_gradients(attention_pieces, feed_pieces, small_grad_all, partials):
     owners = lax.psum(1, ("fsdp", "dp"))
     me = lax.axis_index(("fsdp", "dp"))
+    attention_grad_all = jnp.concatenate(attention_pieces, axis=0).astype(jnp.bfloat16)
+    feed_grad_all = jnp.concatenate(feed_pieces, axis=0).astype(jnp.bfloat16)
     attention_rows = attention_grad_all.shape[0] // owners
     feed_rows = feed_grad_all.shape[0] // owners
     small_count = small_grad_all.shape[0] // owners
     main_rows = attention_rows + feed_rows
-    slots = partials.shape[0]
+    partials_high = partials.astype(jnp.bfloat16)
+    partials_low = (partials - partials_high.astype(jnp.float32)).astype(jnp.bfloat16)
+    split_partials = jnp.concatenate([partials_high, partials_low])
+    slots = split_partials.shape[0]
     extra_count = small_count + owners * slots
-    extra_rows = padded_rows(main_rows + padded_rows(extra_count, D) // D, 8) - main_rows
-    slot_row = jnp.zeros((owners * slots,), jnp.float32)
-    slot_row = lax.dynamic_update_slice(slot_row, partials, (me * slots,))
+    extra_rows = padded_rows(main_rows + padded_rows(extra_count, D) // D, 16) - main_rows
+    slot_row = jnp.zeros((owners * slots,), jnp.bfloat16)
+    slot_row = lax.dynamic_update_slice(slot_row, split_partials, (me * slots,))
     extra = jnp.concatenate(
         [
-            small_grad_all.reshape(owners, small_count),
+            small_grad_all.astype(jnp.bfloat16).reshape(owners, small_count),
             jnp.broadcast_to(slot_row[None], (owners, owners * slots)),
-            jnp.zeros((owners, extra_rows * D - extra_count), jnp.float32),
+            jnp.zeros((owners, extra_rows * D - extra_count), jnp.bfloat16),
         ],
         axis=1,
     ).reshape(owners, extra_rows, D)
@@ -190,14 +195,15 @@
         axis=1,
     ).reshape(owners * (main_rows + extra_rows), D)
     owned = lax.psum_scatter(packed, ("fsdp", "dp"), scatter_dimension=0, tiled=True)
-    attention_owned = owned[:attention_rows]
-    feed_owned = owned[attention_rows:main_rows]
-    extra_owned = owned[main_rows:].reshape(extra_rows * D)
+    attention_owned = owned[:attention_rows].astype(jnp.float32)
+    feed_owned = owned[attention_rows:main_rows].astype(jnp.float32)
+    extra_owned = owned[main_rows:].reshape(extra_rows * D).astype(jnp.float32)
     small_owned = extra_owned[:small_count]
     gathered_partials = extra_owned[small_count:extra_count].reshape(owners, slots)
-    totals = gathered_partials[0]
+    half = slots // 2
+    totals = gathered_partials[0, :half] + gathered_partials[0, half:]
     for index in range(1, owners):
-        totals = totals + gathered_partials[index]
+        totals = totals + (gathered_partials[index, :half] + gathered_partials[index, half:])
     return attention_owned, feed_owned, small_owned, totals
 
 
@@ -282,7 +288,6 @@
     inner_bias_grad = column_total(inner_grad)
     inner_weight_grad = product_rows(inner_grad, normed_low)
     normed_grad = residual_grad + product(inner_grad, inner_weight)
-    feed_grad_all = jnp.concatenate([inner_weight_grad, outer_weight_grad], axis=0)
     first_pull = jax.vjp(layer_norm, first_sum, first_gain, first_shift)[1]
     first_sum_grad, first_gain_grad, first_shift_grad = first_pull(normed_grad)
     branch_grad_low = first_sum_grad.astype(jnp.bfloat16)
@@ -314,9 +319,6 @@
         + product_cols(key_grad, key_weight)
         + product_cols(value_grad, value_weight)
     )
-    attention_grad_all = jnp.concatenate(
-        [query_weight_grad, key_weight_grad, value_weight_grad, output_weight_grad], axis=0
-    )
     small_grad_all = jnp.concatenate(
         [
             query_bias_grad,
@@ -331,7 +333,10 @@
         ]
     )
     attention_owned, feed_owned, small_owned, totals = scatter_gradients(
-        attention_grad_all, feed_grad_all, small_grad_all, partials
+        [query_weight_grad, key_weight_grad, value_weight_grad, output_weight_grad],
+        [inner_weight_grad, outer_weight_grad],
+        small_grad_all,
+        partials,
     )
     rms_values = jnp.sqrt(totals[:3] / (totals[3] * D))
     step_float = step_count[0].astype(jnp.float32)

time: 563 us -> 450 us (0.80)
  waiting for transfers between devices: 370 us -> 266 us
  other arithmetic: 50.1 us -> 43.7 us
    reduce_scatter x1, waiting for transfers between devices: 262 us -> 159 us  [scatter_gradients(): lax.psum_scatter(packed, ('fsdp', 'dp'), scatter_dimension=0, tiled=True)]
  transfers between devices with their start and end apart: 2 -> 2, of which waited for: 2 -> 2; matrix products, arithmetic and copies ran while one was open for 1% -> 2% of each run, Pallas kernels for 0% -> 0%
where the time goes in v2:
time: 450 us; the launch traced here: 442 us
  waiting for transfers between devices  266 us (59%)
  matrix products  87 us (19%)
  other arithmetic  43.7 us (10%)
  local copies, waits for them, and re-layouts  28.2 us (6%)
  between operations  17.4 us (4%)
    reduce_scatter x1, waiting for transfers between devices, scatter_gradients(): lax.psum_scatter(packed, ('fsdp', 'dp'), scatter_dimension=0, tiled=True)  159 us
    all_gather x1, waiting for transfers between devices, gather_working(): gathered = lax.all_gather(block, ('fsdp', 'dp'), axis=0, tiled=False)  107 us
    dot_general x6, matrix products, product_cols(): lax.dot_general(left_side, right_side, (((1,), (1,)), ((), ())), preferre...  36.2 us
    dot_general x6, matrix products, product_rows(): lax.dot_general(left_side, right_side, (((0,), (0,)), ((), ())), preferre...  14.6 us
    dot_general x1, matrix products, attend_backward(): jnp.einsum('qhd,khd->hqk', grad_heads, head_view(values), preferred_eleme...  12.1 us
    dot_general x6, matrix products, product(): return jnp.dot(left_side, right_side, preferred_element_type=jnp.float32)  10.2 us
  transfers between devices with their start and end apart: 2, of which 2 were waited for; matrix products, arithmetic and copies ran while one was open for 2% of the time, Pallas kernels for 0%

profile of v2, /device:TPU:0, one launch (start us, length us, event | category | flops | bytes accessed | tf_op | source)
XLA Modules:
  0.0 442.4 jit_solution(3498045729577218092)
XLA Ops:
  12.8 107.4 %all-gather.3.cloned.1.call-done = bf16[9728,768]{1,0:T(8,128)(2,1)} async-done(((bf16[304,768]{1,0:T(8,128)(2,1)}), bf16[9728,768]{1,0:T(8,128)(2,1)}) %all-gather.3.cloned.1.call-update) | async-done | bytes 14942224 | tf_op jit(solution)/shard_map/all_gather | solution.py:156
  121.3 3.8 fusion.100
  130.4 8.4 %fusion.99 = (bf16[16,192,768]{2,1,0:T(8,128)(2,1)}, bf16[16,192,768]{2,1,0:T(8,128)(2,1)}) fusion(bf16[32,304,768]{2,1,0:T(8,128)(2,1)} %bitcast.201), kind=kLoop, calls=%fused_computation.207 | loop fusion | bytes 18874368 | tf_op jit(solution)/shard_map/slice | solution.py:263
  140.6 3.0 fusion.101
  143.7 1.9 fusion
  146.4 2.1 copy-done
  148.6 2.9 fusion.18
  152.9 19.5 %multiply_convert_fusion.1 = (bf16[512,3072]{1,0:T(8,128)(2,1)S(1)}, f32[512,3072]{1,0:T(8,128)}, f32[512,3072]{1,0:T(8,128)}) fusion(f32[3072]{0:T(1024)S(1)} %copy-done.30, bf16[3072,768]{1,0:T(8,128)(2,1)S(1)} %bitcast.212, f32[512,768]{1,0:T(8,128)S(1)} %get-tuple-element.116, f32[768]{0:T(1024)S(1)} %copy-done.33, f32[768]{0:T(1024)S(1)} %get-tuple-element.132, ...), kind=kOutput, calls=%fused_computation.15 | convolution fusion | flops 2521694208 | bytes 22042624 | tf_op jit(solution)/shard_map/dot_general | solution.py:35
  172.5 3.6 multiply_reduce_fusion.2
  179.8 8.2 %fusion.92 = (bf16[3072]{0:T(1024)(128)(2,1)S(1)}, bf16[512,3072]{1,0:T(8,128)(2,1)S(1)}) fusion(f32[512,3072]{1,0:T(8,128)} %get-tuple-element.114, f32[512,3072]{1,0:T(8,128)} %get-tuple-element.139, f32[3072]{0:T(1024)S(1)} %copy-done.30, bf16[512,768]{1,0:T(8,128)(2,1)S(1)} %get-tuple-element.102, bf16[3072,768]{1,0:T(8,128)(2,1)S(1)} %bitcast.219), kind=kOutput, calls=%fused_computation.201 | convolution fusion | flops 2441081856 | bytes 21252096 | tf_op jit(solution)/shard_map/dot_general | solution.py:35
  188.1 3.1 multiply_reduce_fusion.5
  193.0 1.7 convolution_convert_fusion.6
  194.7 2.3 copy.35
  197.0 12.1 %multiply_reduce_fusion = (f32[12,512]{1,0:T(8,128)S(1)}, f32[12,512,512]{1,2,0:T(8,128)}) fusion(f32[12,512,512]{1,2,0:T(8,128)} %copy-done, f32[12,512]{1,0:T(8,128)S(1)} %log_add_fusion, bf16[512,12,64]{0,2,1:T(8,128)(2,1)} %bitcast.202, bf16[512,12,64]{0,2,1:T(8,128)(2,1)} %bitcast.235), kind=kOutput, calls=%fused_computation.2 | convolution fusion | flops 412084224 | bytes 26787840 | tf_op jit(solution)/shard_map/while/body/eval_jaxpr/qhd,khd->hqk/dot_general | solution.py:100
  209.2 7.1 %multiply_convert_fusion = bf16[12,512,512]{1,2,0:T(8,128)(2,1)S(1)} fusion(f32[12,512,512]{1,2,0:T(8,128)} %get-tuple-element.142, f32[12,512,512]{1,2,0:T(8,128)S(1)} %bitcast.195, f32[12,512]{1,0:T(8,128)S(1)} %get-tuple-element.141, f32[12,512]{1,0:T(8,128)S(1)} %log_add_fusion), kind=kLoop, calls=%fused_computation.1 | loop fusion | flops 12582912 | bytes 31506432 | tf_op jit(solution)/shard_map/while/body/eval_jaxpr/convert_element_type | solution.py:104
  216.3 2.9 multiply_convert_fusion.2
  219.2 2.0 bitcast_reduce_fusion.1
  221.3 3.0 bitcast_reduce_fusion
  224.2 4.3 convolution_convert_fusion
  228.6 4.7 %convolution_convert_fusion.1 = bf16[3072,768]{1,0:T(8,128)(2,1)} fusion(bf16[512,3072]{1,0:T(8,128)(2,1)S(1)} %copy-done.41, f32[512,768]{1,0:T(8,128)S(1)} %get-tuple-element.116, f32[768]{0:T(1024)S(1)} %copy-done.33, f32[768]{0:T(1024)S(1)} %get-tuple-element.132, f32[512]{0:T(512)S(1)} %fusion.29, f32[512]{0:T(512)S(1)} %broadcast_multiply_fusion.1), kind=kOutput, calls=%fused_computation.31 | convolution fusion | flops 2420244480 | bytes 9447424 | tf_op jit(solution)/shard_map/dot_general | solution.py:29
  233.3 1.8 convolution_convert_fusion.2
  237.2 2.7 fusion.90
  241.2 2.0 concatenate.31
  243.4 2.1 fusion.14
  247.2 5.8 %pad_maximum_fusion.1 = bf16[6144,768]{1,0:T(8,128)(2,1)S(1)} fusion(bf16[3072,768]{1,0:T(8,128)(2,1)} %convolution_convert_fusion, bf16[3072,768]{1,0:T(8,128)(2,1)} %convolution_convert_fusion.1), kind=kLoop, calls=%fused_computation.10 | loop fusion | flops 18874368 | bytes 18874368 | tf_op jit(solution)/shard_map/concatenate | solution.py:168
  253.6 6.3 %pad_maximum_fusion = bf16[32,304,768]{2,1,0:T(8,128)(2,1)} fusion(bf16[32,16,768]{2,1,0:T(8,128)(2,1)S(1)} %bitcast.226, bf16[32,192,768]{2,1,0:T(8,128)(2,1)S(1)} %bitcast.197, bf16[32,96,768]{2,1,0:T(8,128)(2,1)S(1)} %bitcast.198), kind=kLoop, calls=%fused_computation | loop fusion | flops 44826624 | bytes 29884416 | tf_op jit(solution)/shard_map/concatenate | solution.py:189
  260.8 2.3 fusion.103
  263.1 2.2 fusion.102
  265.4 2.3 add_add_fusion.2
  267.7 158.6 %reduce-scatter.2.cloned.1.call-done = bf16[304,768]{1,0:T(8,128)(2,1)} async-done(((bf16[9728,768]{1,0:T(8,128)(2,1)}), bf16[304,768]{1,0:T(8,128)(2,1)}) %reduce-scatter.2.cloned.1.call-update) | async-done | bytes 466960 | tf_op jit(solution)/shard_map/reduce_scatter | solution.py:197
  430.0 2.2 fusion.87
  432.2 2.9 fusion.84
  (173 shorter events, 29.6 us)
Async XLA Ops:
  7.2 113.0 %all-gather.3.cloned.1.call-start = ((), (), s32[]{:S(2)}) async-start(), calls=%async_computation.2 | async-start | bytes 15409152 | tf_op jit(solution)/shard_map/all_gather | solution.py:156
  10.9 415.4 %reduce-scatter.2.cloned.1.call-start = ((), (), s32[]{:S(2)}) async-start(), calls=%async_computation.1 | async-start | bytes 15409152 | tf_op jit(solution)/shard_map/reduce_scatter | solution.py:197
  125.1 13.7 %copy-start.15 = (bf16[8,96,768]{2,1,0:T(8,128)(2,1)}, bf16[8,96,768]{2,1,0:T(8,128)(2,1)S(1)}, u32[]{:S(2)}) copy-start(bf16[8,96,768]{2,1,0:T(8,128)(2,1)S(1)} %get-tuple-element.120) | copy-start | bytes 3538948
  125.1 14.6 %copy-start.14 = (bf16[8,96,768]{2,1,0:T(8,128)(2,1)}, bf16[8,96,768]{2,1,0:T(8,128)(2,1)S(1)}, u32[]{:S(2)}) copy-start(bf16[8,96,768]{2,1,0:T(8,128)(2,1)S(1)} %get-tuple-element.121) | copy-start | bytes 3538948
  125.1 20.4 %copy-start.5 = (bf16[8,96,768]{2,1,0:T(8,128)(2,1)}, bf16[8,96,768]{2,1,0:T(8,128)(2,1)S(1)}, u32[]{:S(2)}) copy-start(bf16[8,96,768]{2,1,0:T(8,128)(2,1)S(1)} %get-tuple-element.122) | copy-start | bytes 3538948
  130.4 8.4 %copy-start.19 = (bf16[512,768]{1,0:T(8,128)(2,1)S(1)}, bf16[512,768]{1,0:T(8,128)(2,1)}, u32[]{:S(2)}) copy-start(bf16[512,768]{1,0:T(8,128)(2,1)} %param.15) | copy-start | bytes 2359300
  143.6 4.9 %copy-start = (f32[12,512,512]{1,2,0:T(8,128)}, f32[12,512,512]{1,2,0:T(8,128)S(1)}, u32[]{:S(2)}) copy-start(f32[12,512,512]{1,2,0:T(8,128)S(1)} %get-tuple-element.137) | copy-start | bytes 37748740
  146.4 5.1 %copy-start.18 = (bf16[768,512]{1,0:T(8,128)(2,1)}, bf16[768,512]{1,0:T(8,128)(2,1)S(1)}, u32[]{:S(2)}) copy-start(bf16[768,512]{1,0:T(8,128)(2,1)S(1)} %add_convert_fusion.3) | copy-start | bytes 2359300
  146.4 6.4 %slice-start.3 = ((s8[4718592]{0:T(1024)(128)(4,1)}), s8[4194304]{0:T(1024)(128)(4,1)S(1)}, s32[]{:S(2)}) async-start(s8[4718592]{0:T(1024)(128)(4,1)} %bitcast.210), calls=%async_computation.6 | async-start | bytes 8388608
  151.5 20.9 %copy-start.22 = (bf16[12,64,512]{2,1,0:T(8,128)(2,1)}, bf16[12,64,512]{2,1,0:T(8,128)(2,1)S(1)}, u32[]{:S(2)}) copy-start(bf16[12,64,512]{2,1,0:T(8,128)(2,1)S(1)} %fusion.18) | copy-start | bytes 2359300
  151.5 20.9 %slice-start.7 = ((s8[4718592]{0:T(1024)(128)(4,1)}), s8[4194304]{0:T(1024)(128)(4,1)S(1)}, s32[]{:S(2)}) async-start(s8[4718592]{0:T(1024)(128)(4,1)} %bitcast.216), calls=%async_computation.10 | async-start | bytes 8388608
  152.9 19.6 %slice-start.8 = ((s8[4718592]{0:T(1024)(128)(4,1)}), s8[524288]{0:T(1024)(128)(4,1)S(1)}, s32[]{:S(2)}) async-start(s8[4718592]{0:T(1024)(128)(4,1)} %bitcast.216), calls=%async_computation.11 | async-start | bytes 1048576
  152.9 19.6 %copy-start.32 = (f32[512]{0:T(512)S(1)}, f32[512]{0:T(512)}, u32[]{:S(2)}) copy-start(f32[512]{0:T(512)} %get-tuple-element.147) | copy-start | bytes 6148
  152.9 19.5 %copy-start.34 = (f32[768]{0:T(1024)S(1)}, f32[768]{0:T(1024)}, u32[]{:S(2)}) copy-start(f32[768]{0:T(1024)} %get-tuple-element.130) | copy-start | bytes 9220
  178.0 10.1 %slice-start.5 = ((s8[4718592]{0:T(1024)(128)(4,1)}), s8[524288]{0:T(1024)(128)(4,1)S(1)}, s32[]{:S(2)}) async-start(s8[4718592]{0:T(1024)(128)(4,1)} %bitcast.213), calls=%async_computation.8 | async-start | bytes 1048576
  179.8 8.2 %copy-start.24 = (bf16[512,768]{1,0:T(8,128)(2,1)}, bf16[512,768]{1,0:T(8,128)(2,1)S(1)}, u32[]{:S(2)}) copy-start(bf16[512,768]{1,0:T(8,128)(2,1)S(1)} %get-tuple-element.102) | copy-start | bytes 2359300
  179.8 8.3 %slice-start.6 = ((s8[4718592]{0:T(1024)(128)(4,1)}), s8[4194304]{0:T(1024)(128)(4,1)S(1)}, s32[]{:S(2)}) async-start(s8[4718592]{0:T(1024)(128)(4,1)} %bitcast.213), calls=%async_computation.9 | async-start | bytes 8388608
  197.0 12.2 %slice-start = ((s8[12582912]{0:T(1024)(128)(4,1)}), s8[4194304]{0:T(1024)(128)(4,1)S(1)}, s32[]{:S(2)}) async-start(s8[12582912]{0:T(1024)(128)(4,1)} %bitcast.194), calls=%async_computation.3 | async-start | bytes 8388608
  197.0 12.2 %slice-start.1 = ((s8[12582912]{0:T(1024)(128)(4,1)}), s8[4194304]{0:T(1024)(128)(4,1)S(1)}, s32[]{:S(2)}) async-start(s8[12582912]{0:T(1024)(128)(4,1)} %bitcast.194), calls=%async_computation.4 | async-start | bytes 8388608
  197.0 12.2 %slice-start.2 = ((s8[12582912]{0:T(1024)(128)(4,1)}), s8[4194304]{0:T(1024)(128)(4,1)S(1)}, s32[]{:S(2)}) async-start(s8[12582912]{0:T(1024)(128)(4,1)} %bitcast.194), calls=%async_computation.5 | async-start | bytes 8388608
  209.2 7.1 %copy-start.10 = (bf16[768,512]{1,0:T(8,128)(2,1)S(1)}, bf16[768,512]{1,0:T(8,128)(2,1)}, u32[]{:S(2)}) copy-start(bf16[768,512]{1,0:T(8,128)(2,1)} %copy-done.9) | copy-start | bytes 2359300
  228.6 4.8 %copy-start.23 = (bf16[12,64,512]{2,1,0:T(8,128)(2,1)S(1)}, bf16[12,64,512]{2,1,0:T(8,128)(2,1)}, u32[]{:S(2)}) copy-start(bf16[12,64,512]{2,1,0:T(8,128)(2,1)} %copy-done.22) | copy-start | bytes 2359300
  228.6 4.8 %copy-start.27 = (bf16[512,768]{1,0:T(8,128)(2,1)S(1)}, bf16[512,768]{1,0:T(8,128)(2,1)}, u32[]{:S(2)}) copy-start(bf16[512,768]{1,0:T(8,128)(2,1)} %copy-done.26) | copy-start | bytes 2359300
  228.6 6.7 %copy-start.29 = (bf16[9216]{0:T(1024)(128)(2,1)S(1)}, bf16[9216]{0:T(1024)(128)(2,1)}, u32[]{:S(2)}) copy-start(bf16[9216]{0:T(1024)(128)(2,1)} %custom-call) | copy-start | bytes 55300
  233.3 10.1 %copy-start.8 = (bf16[12,64,512]{2,1,0:T(8,128)(2,1)S(1)}, bf16[12,64,512]{2,1,0:T(8,128)(2,1)}, u32[]{:S(2)}) copy-start(bf16[12,64,512]{2,1,0:T(8,128)(2,1)} %get-tuple-element.146) | copy-start | bytes 2359300
  247.2 5.9 %copy-start.16 = (bf16[768,768]{1,0:T(8,128)(2,1)S(1)}, bf16[768,768]{1,0:T(8,128)(2,1)}, u32[]{:S(2)}) copy-start(bf16[768,768]{1,0:T(8,128)(2,1)} %convolution_convert_fusion.2) | copy-start | bytes 3538948
  259.9 5.5 %copy-start.6 = (bf16[8,96,768]{2,1,0:T(8,128)(2,1)S(1)}, bf16[8,96,768]{2,1,0:T(8,128)(2,1)}, u32[]{:S(2)}) copy-start(bf16[8,96,768]{2,1,0:T(8,128)(2,1)} %copy-done.5) | copy-start | bytes 3538948
  265.4 164.1 %copy-start.31 = (f32[288]{0:T(512)S(1)}, f32[288]{0:T(512)}, u32[]{:S(2)}) copy-start(f32[288]{0:T(512)} %param.25) | copy-start | bytes 3460
  265.4 164.1 %copy-start.36 = (f32[288]{0:T(512)S(1)}, f32[288]{0:T(512)}, u32[]{:S(2)}) copy-start(f32[288]{0:T(512)} %param.27) | copy-start | bytes 3460
  265.4 164.1 %copy-start.37 = (f32[288]{0:T(512)S(1)}, f32[288]{0:T(512)}, u32[]{:S(2)}) copy-start(f32[288]{0:T(512)} %param.26) | copy-start | bytes 3460
  265.4 164.7 %copy-start.17 = (f32[96,768]{1,0:T(8,128)S(1)}, f32[96,768]{1,0:T(8,128)}, u32[]{:S(2)}) copy-start(f32[96,768]{1,0:T(8,128)} %param.19) | copy-start | bytes 884740
  265.4 166.8 %copy-start.13 = (f32[192,768]{1,0:T(8,128)S(1)}, f32[192,768]{1,0:T(8,128)}, u32[]{:S(2)}) copy-start(f32[192,768]{1,0:T(8,128)} %param.22) | copy-start | bytes 1769476
  (21 other events, 59.6 us)
Sparse Core Ops, SparseCore 0:
  11.5 108.6 all-gather.2
  260.0 166.2 reduce-scatter.1

commit v3 on v2

--- a/solution.py
+++ b/solution.py
@@ -1,3 +1,4 @@
+import functools
 import math
 
 import jax
@@ -161,21 +162,116 @@
     return attention_full, feed_full, small_full.reshape(owners * small_count)
 
 
-def scatter_gradients(attention_pieces, feed_pieces, small_grad_all, partials):
+def flat_coordinates():
+    me = lax.axis_index(("fsdp", "dp"))
+    return me, me % 2, (me // 2) % 2, (me // 4) % 2, me // 8
+
+
+def shifted(distance, count=32):
+    return [(d, d + distance) for d in range(count) if 0 <= d + distance < count]
+
+
+def flipped(mask, count=32):
+    return [(d, d ^ mask) for d in range(count)]
+
+
+def permute(arrays, pairs):
+    return lax.ppermute(tuple(arrays), ("fsdp", "dp"), pairs)
+
+
+def staged_reduce_scatter(arrays):
+    me, y_place, core, x_place, z_place = flat_coordinates()
+    blocks = [entries.reshape((4, 2, 2, 2) + entries.shape[1:]) for entries in arrays]
+    keep = [lax.dynamic_index_in_dim(b, core, axis=2, keepdims=False) for b in blocks]
+    send = [lax.dynamic_index_in_dim(b, 1 - core, axis=2, keepdims=False).astype(jnp.bfloat16) for b in blocks]
+    received = permute(send, flipped(2))
+    plane = [k.astype(jnp.float32) + r.astype(jnp.float32) for k, r in zip(keep, received)]
+
+    def pick(entries, x_index, y_index):
+        picked = lax.dynamic_index_in_dim(entries, x_index, axis=1, keepdims=False)
+        return lax.dynamic_index_in_dim(picked, y_index, axis=1, keepdims=False)
+
+    along_z = [pick(p, x_place, y_place) for p in plane]
+    for mask, x_index, y_index in ((4, 1 - x_place, y_place), (1, x_place, 1 - y_place), (5, 1 - x_place, 1 - y_place)):
+        got = permute([pick(p, x_index, y_index).astype(jnp.bfloat16) for p in plane], flipped(mask))
+        along_z = [a + g.astype(jnp.float32) for a, g in zip(along_z, got)]
+    owned = [lax.dynamic_index_in_dim(a, z_place, axis=0, keepdims=False) for a in along_z]
+    for distance in (1, 2, 3):
+        up = permute(
+            [lax.dynamic_index_in_dim(a, jnp.minimum(z_place + distance, 3), axis=0, keepdims=False).astype(jnp.bfloat16) for a in along_z],
+            shifted(8 * distance),
+        )
+        down = permute(
+            [lax.dynamic_index_in_dim(a, jnp.maximum(z_place - distance, 0), axis=0, keepdims=False).astype(jnp.bfloat16) for a in along_z],
+            shifted(-8 * distance),
+        )
+        owned = [o + u.astype(jnp.float32) + w.astype(jnp.float32) for o, u, w in zip(owned, up, down)]
+    return owned
+
+
+def staged_all_gather(arrays):
+    me, y_place, core, x_place, z_place = flat_coordinates()
+    slot = [lax.broadcasted_iota(jnp.int32, (4,) + (1,) * a.ndim, 0) for a in arrays]
+    grown = [jnp.where(s == z_place, a[None], jnp.zeros((4,) + a.shape, a.dtype)) for s, a in zip(slot, arrays)]
+    for distance in (1, 2, 3):
+        from_below = permute(arrays, shifted(8 * distance))
+        from_above = permute(arrays, shifted(-8 * distance))
+        grown = [jnp.where(s == z_place - distance, b[None], g) for s, b, g in zip(slot, from_below, grown)]
+        grown = [jnp.where(s == z_place + distance, b[None], g) for s, b, g in zip(slot, from_above, grown)]
+    got_x = permute(grown, flipped(4))
+    got_y = permute(grown, flipped(1))
+    got_xy = permute(grown, flipped(5))
+    planes = []
+    for own, gx, gy, gxy in zip(grown, got_x, got_y, got_xy):
+        shape = (own.shape[0], 2, 2) + own.shape[1:]
+        xs = lax.broadcasted_iota(jnp.int32, (1, 2, 1) + (1,) * (own.ndim - 1), 1)
+        ys = lax.broadcasted_iota(jnp.int32, (1, 1, 2) + (1,) * (own.ndim - 1), 2)
+        same_x, same_y = xs == x_place, ys == y_place
+        plane = jnp.where(
+            same_x,
+            jnp.where(same_y, own[:, None, None], gy[:, None, None]),
+            jnp.where(same_y, gx[:, None, None], gxy[:, None, None]),
+        )
+        planes.append(jnp.broadcast_to(plane, shape))
+    got_core = permute(planes, flipped(2))
+    gathered = []
+    for own, other in zip(planes, got_core):
+        own = own[:, :, None]
+        other = other[:, :, None]
+        size = own.shape[2]
+        shape = own.shape[:2] + (2,) + own.shape[3:]
+        start = [0] * len(shape)
+        start_other = [0] * len(shape)
+        start[2] = core * size
+        start_other[2] = (1 - core) * size
+        full = jnp.zeros(shape, own.dtype)
+        full = lax.dynamic_update_slice(full, own, start)
+        full = lax.dynamic_update_slice(full, other, start_other)
+        gathered.append(full.reshape((32 * full.shape[4],) + full.shape[5:]))
+    return gathered
+
+
+def staged_working(attention_master, feed_master, small_master):
+    small_count = small_master.shape[0]
+    small_row = jnp.zeros((1, D), jnp.bfloat16).at[0, :small_count].set(small_master.astype(jnp.bfloat16))
+    attention_full, small_rows = staged_all_gather([attention_master.astype(jnp.bfloat16), small_row])
+    small_full = small_rows[:, :small_count].reshape(32 * small_count)
+    feed_full = lax.all_gather(feed_master.astype(jnp.bfloat16), ("fsdp", "dp"), axis=0, tiled=True)
+    return attention_full, feed_full, small_full
+
+
+def scatter_gradients(attention_pieces, feed_pieces, small_grad_all, partials, staged):
     owners = lax.psum(1, ("fsdp", "dp"))
     me = lax.axis_index(("fsdp", "dp"))
-    attention_grad_all = jnp.concatenate(attention_pieces, axis=0).astype(jnp.bfloat16)
-    feed_grad_all = jnp.concatenate(feed_pieces, axis=0).astype(jnp.bfloat16)
-    attention_rows = attention_grad_all.shape[0] // owners
-    feed_rows = feed_grad_all.shape[0] // owners
+    attention_rows = sum(piece.shape[0] for piece in attention_pieces) // owners
     small_count = small_grad_all.shape[0] // owners
-    main_rows = attention_rows + feed_rows
+    feed_owned = lax.psum_scatter(feed_pieces, ("fsdp", "dp"), scatter_dimension=0, tiled=True)
     partials_high = partials.astype(jnp.bfloat16)
     partials_low = (partials - partials_high.astype(jnp.float32)).astype(jnp.bfloat16)
     split_partials = jnp.concatenate([partials_high, partials_low])
     slots = split_partials.shape[0]
     extra_count = small_count + owners * slots
-    extra_rows = padded_rows(main_rows + padded_rows(extra_count, D) // D, 16) - main_rows
+    extra_rows = padded_rows(attention_rows + padded_rows(extra_count, D) // D, 16) - attention_rows
     slot_row = jnp.zeros((owners * slots,), jnp.bfloat16)
     slot_row = lax.dynamic_update_slice(slot_row, split_partials, (me * slots,))
     extra = jnp.concatenate(
@@ -186,28 +282,38 @@
         ],
         axis=1,
     ).reshape(owners, extra_rows, D)
-    packed = jnp.concatenate(
-        [
-            attention_grad_all.reshape(owners, attention_rows, D),
-            feed_grad_all.reshape(owners, feed_rows, D),
-            extra,
-        ],
-        axis=1,
-    ).reshape(owners * (main_rows + extra_rows), D)
-    owned = lax.psum_scatter(packed, ("fsdp", "dp"), scatter_dimension=0, tiled=True)
-    attention_owned = owned[:attention_rows].astype(jnp.float32)
-    feed_owned = owned[attention_rows:main_rows].astype(jnp.float32)
-    extra_owned = owned[main_rows:].reshape(extra_rows * D).astype(jnp.float32)
+    block_rows = attention_rows + extra_rows
+    if staged:
+        attention_grad_all = jnp.concatenate(attention_pieces, axis=0).astype(jnp.bfloat16)
+        owned = jnp.concatenate(
+            staged_reduce_scatter([attention_grad_all.reshape(owners, attention_rows, D), extra]), axis=0
+        )
+    else:
+        packed = jnp.zeros((owners, block_rows, D), jnp.bfloat16)
+        packed = lax.dynamic_update_slice(packed, extra, (0, attention_rows, 0))
+        owner = 0
+        for piece in attention_pieces:
+            piece_owners = piece.shape[0] // attention_rows
+            packed = lax.dynamic_update_slice(
+                packed, piece.astype(jnp.bfloat16).reshape(piece_owners, attention_rows, D), (owner, 0, 0)
+            )
+            owner = owner + piece_owners
+        owned = lax.psum_scatter(
+            packed.reshape(owners * block_rows, D), ("fsdp", "dp"), scatter_dimension=0, tiled=True
+        ).astype(jnp.float32)
+    attention_owned = owned[:attention_rows]
+    extra_owned = owned[attention_rows:].reshape(extra_rows * D)
     small_owned = extra_owned[:small_count]
     gathered_partials = extra_owned[small_count:extra_count].reshape(owners, slots)
     half = slots // 2
     totals = gathered_partials[0, :half] + gathered_partials[0, half:]
     for index in range(1, owners):
         totals = totals + (gathered_partials[index, :half] + gathered_partials[index, half:])
-    return attention_owned, feed_owned, small_owned, totals
+    return attention_owned, feed_owned.astype(jnp.float32), small_owned, totals
 
 
 def on_device(
+    staged,
     tokens,
     cotangent,
     lengths,
@@ -224,7 +330,10 @@
 ):
     row_count = tokens.shape[0]
     sequence_count = row_count // SEQ
-    attention_full, feed_full, small_full = gather_working(attention_master, feed_master, small_master)
+    if staged:
+        attention_full, feed_full, small_full = staged_working(attention_master, feed_master, small_master)
+    else:
+        attention_full, feed_full, small_full = gather_working(attention_master, feed_master, small_master)
     key_valid = (
         lax.broadcasted_iota(jnp.int32, (sequence_count, SEQ), 1) < lengths[:, None]
     ).astype(jnp.float32)
@@ -282,11 +391,19 @@
     residual_grad, second_gain_grad, second_shift_grad = second_pull(cotangent)
     feed_out_grad = residual_grad.astype(jnp.bfloat16)
     outer_bias_grad = column_total(feed_out_grad)
-    outer_weight_grad = product_rows(active, feed_out_grad)
     active_grad = product_cols(feed_out_grad, outer_weight)
     inner_grad = jax.vjp(gelu_exact, inner_sum)[1](active_grad)[0].astype(jnp.bfloat16)
     inner_bias_grad = column_total(inner_grad)
-    inner_weight_grad = product_rows(inner_grad, normed_low)
+    feed_grad_all = (
+        lax.dot_general(
+            jnp.stack([inner_grad, active]),
+            jnp.stack([normed_low, feed_out_grad]),
+            (((1,), (1,)), ((0,), (0,))),
+            preferred_element_type=jnp.float32,
+        )
+        .astype(jnp.bfloat16)
+        .reshape(2 * FF, D)
+    )
     normed_grad = residual_grad + product(inner_grad, inner_weight)
     first_pull = jax.vjp(layer_norm, first_sum, first_gain, first_shift)[1]
     first_sum_grad, first_gain_grad, first_shift_grad = first_pull(normed_grad)
@@ -294,6 +411,7 @@
     output_bias_grad = column_total(branch_grad_low)
     output_weight_grad = product_rows(attended, branch_grad_low)
     attended_grad = product_cols(branch_grad_low, output_weight).astype(jnp.bfloat16)
+    feed_grad_all, attended_grad = lax.optimization_barrier((feed_grad_all, attended_grad))
     query_grad, key_grad, value_grad = lax.map(
         attend_backward,
         (
@@ -334,9 +452,10 @@
     )
     attention_owned, feed_owned, small_owned, totals = scatter_gradients(
         [query_weight_grad, key_weight_grad, value_weight_grad, output_weight_grad],
-        [inner_weight_grad, outer_weight_grad],
+        feed_grad_all,
         small_grad_all,
         partials,
+        staged,
     )
     rms_values = jnp.sqrt(totals[:3] / (totals[3] * D))
     step_float = step_count[0].astype(jnp.float32)
@@ -390,8 +509,9 @@
         P(("fsdp", "dp")),
         P(("fsdp", "dp")),
     )
+    staged = dict(mesh.shape) == {"fsdp": 16, "dp": 2}
     return jax.shard_map(
-        on_device,
+        functools.partial(on_device, staged),
         mesh=mesh,
         in_specs=placed,
         out_specs=(

time: 450 us -> 341 us (0.76)
  waiting for transfers between devices: 266 us -> 81.4 us
  starting transfers between devices: 0.08 us -> 88.1 us
  local copies, waits for them, and re-layouts: 28.2 us -> 23.3 us
  other arithmetic: 43.7 us -> 39 us
    reduce_scatter x1, waiting for transfers between devices: 159 us -> 0.01 us  [scatter_gradients(): lax.psum_scatter(feed_pieces, ('fsdp', 'dp'), scatter_dimension=0, tiled=...]
    all_gather x1, waiting for transfers between devices: 107 us -> 0.02 us  [staged_working(): lax.all_gather(feed_master.astype(jnp.bfloat16), ('fsdp', 'dp'), axis=0,...]
    ppermute x0 -> x40, starting transfers between devices: none -> 88 us  [permute(): return lax.ppermute(tuple(arrays), ('fsdp', 'dp'), pairs)]
    ppermute x0 -> x40, waiting for transfers between devices: none -> 81.4 us  [permute(): return lax.ppermute(tuple(arrays), ('fsdp', 'dp'), pairs)]
    concatenate x3 -> x0, other arithmetic: 12.9 us -> none  [the longest x1 6.28 us: scatter_gradients(): jnp.concatenate([attention_grad_all.reshape(owners, attention_rows, D), f...]
    dot_general x6 -> x4, matrix products: 14.6 us -> 4.4 us  [product_rows(): lax.dot_general(left_side, right_side, (((0,), (0,)), ((), ())), preferre...]
    slice x3 -> x2, local copies, waits for them, and re-layouts: 10.4 us -> 0.44 us  [the longest x1 0.44 us: scatter_gradients(): extra_owned[small_count:extra_count].reshape(owners, slots)]
    dot_general x0 -> x1, matrix products: none -> 9.11 us  [on_device(): lax.dot_general(jnp.stack([inner_grad, active]), jnp.stack([normed_low, f...]
  transfers between devices with their start and end apart: 2 -> 42, of which waited for: 2 -> 14; matrix products, arithmetic and copies ran while one was open for 2% -> 25% of each run, Pallas kernels for 0% -> 0%
where the time goes in v3:
time: 341 us; the launch traced here: 337 us
  starting transfers between devices  88.1 us (26%)
  matrix products  86.9 us (25%)
  waiting for transfers between devices  81.4 us (24%)
  other arithmetic  39 us (11%)
  local copies, waits for them, and re-layouts  23.3 us (7%)
  between operations  17.9 us (5%)
    ppermute x40, starting transfers between devices, permute(): return lax.ppermute(tuple(arrays), ('fsdp', 'dp'), pairs)  88 us
    ppermute x40, waiting for transfers between devices, permute(): return lax.ppermute(tuple(arrays), ('fsdp', 'dp'), pairs)  81.4 us
    dot_general x6, matrix products, product_cols(): lax.dot_general(left_side, right_side, (((1,), (1,)), ((), ())), preferre...  35.6 us
    dot_general x1, matrix products, attend_backward(): jnp.einsum('qhd,khd->hqk', grad_heads, head_view(values), preferred_eleme...  11.5 us
    unnamed x119, local copies, waits for them, and re-layouts  10.9 us
    dot_general x6, matrix products, product(): return jnp.dot(left_side, right_side, preferred_element_type=jnp.float32)  10.1 us
    dot_general x1, matrix products, on_device(): lax.dot_general(jnp.stack([inner_grad, active]), jnp.stack([normed_low, f...  9.11 us
    convert_element_type x1, other arithmetic, attend_backward(): (probability * (probability_grad - inner_total)).astype(jnp.bfloat16)  7.53 us
  transfers between devices with their start and end apart: 42, of which 14 were waited for; matrix products, arithmetic and copies ran while one was open for 25% of the time, Pallas kernels for 0%

profile of v3, /device:TPU:0, one launch (start us, length us, event | category | flops | bytes accessed | tf_op | source)
XLA Modules:
  0.0 336.7 jit_solution(2190992689123363356)
XLA Ops:
  10.1 5.0 %collective-permute-start.5 = (bf16[96,768]{1,0:T(8,128)(2,1)S(1)}, bf16[96,768]{1,0:T(8,128)(2,1)S(1)}, u32[]{:S(2)}, u32[]{:S(2)}) collective-permute-start(bf16[96,768]{1,0:T(8,128)(2,1)S(1)} %convert_element_type.391), channel_id=1, source_target_pairs={{0,8},{1,9},{2,10},{3,11},{4,12},{5,13},{6,14},{7,15},{8,16},{9,17... | collective-permute-start | bytes 442376 | tf_op jit(solution)/shard_map/ppermute | solution.py:179
  16.4 5.6 %collective-permute-start.3 = (bf16[96,768]{1,0:T(8,128)(2,1)S(1)}, bf16[96,768]{1,0:T(8,128)(2,1)S(1)}, u32[]{:S(2)}, u32[]{:S(2)}) collective-permute-start(bf16[96,768]{1,0:T(8,128)(2,1)S(1)} %convert_element_type.391), channel_id=1, source_target_pairs={{0,16},{1,17},{2,18},{3,19},{4,20},{5,21},{6,22},{7,23},{8,24},{9,... | collective-permute-start | bytes 442376 | tf_op jit(solution)/shard_map/ppermute | solution.py:179
  23.2 6.5 %collective-permute-start.1 = (bf16[96,768]{1,0:T(8,128)(2,1)S(1)}, bf16[96,768]{1,0:T(8,128)(2,1)S(1)}, u32[]{:S(2)}, u32[]{:S(2)}) collective-permute-start(bf16[96,768]{1,0:T(8,128)(2,1)S(1)} %convert_element_type.391), channel_id=1, source_target_pairs={{0,24},{1,25},{2,26},{3,27},{4,28},{5,29},{6,30},{7,31}} | collective-permute-start | bytes 442376 | tf_op jit(solution)/shard_map/ppermute | solution.py:179
  31.2 11.0 %collective-permute-done.2 = bf16[96,768]{1,0:T(8,128)(2,1)S(1)} collective-permute-done((bf16[96,768]{1,0:T(8,128)(2,1)S(1)}, bf16[96,768]{1,0:T(8,128)(2,1)S(1)}, u32[]{:S(2)}, u32[]{:S(2)}) %collective-permute-start.2) | collective-permute-done | bytes 147488 | tf_op jit(solution)/shard_map/ppermute | solution.py:179
  51.9 21.6 %collective-permute-done.6 = bf16[4,96,768]{2,1,0:T(8,128)(2,1)S(1)} collective-permute-done((bf16[4,96,768]{2,1,0:T(8,128)(2,1)S(1)}, bf16[4,96,768]{2,1,0:T(8,128)(2,1)S(1)}, u32[]{:S(2)}, u32[]{:S(2)}) %collective-permute-start.6) | collective-permute-done | bytes 589856 | tf_op jit(solution)/shard_map/ppermute | solution.py:179
  82.7 3.6 %collective-permute-start.11 = (bf16[1,768]{1,0:T(2,128)(2,1)}, bf16[1,768]{1,0:T(2,128)(2,1)S(1)}, u32[]{:S(2)}, u32[]{:S(2)}) collective-permute-start(bf16[1,768]{1,0:T(2,128)(2,1)} %get-tuple-element.155), channel_id=1, source_target_pairs={{0,24},{1,25},{2,26},{3,27},{4,28},{5,29},{6,30},{7,31}} | collective-permute-start | bytes 4616 | tf_op jit(solution)/shard_map/ppermute | solution.py:179
  90.6 3.4 collective-permute-done.10
  97.9 2.4 collective-permute-done.18
  109.6 3.0 fusion.147
  114.5 2.7 copy-done
  117.2 2.7 fusion.36
  121.2 20.9 %multiply_convert_fusion.1 = (bf16[512,3072]{1,0:T(8,128)(2,1)S(1)}, f32[512,3072]{1,0:T(8,128)}, f32[512,3072]{1,0:T(8,128)}) fusion(f32[3072]{0:T(1024)S(1)} %slice_convert_fusion, bf16[6144,768]{1,0:T(8,128)(2,1)} %all-gather.2.cloned.1.call-done, f32[512,768]{1,0:T(8,128)S(1)} %get-tuple-element.118, f32[768]{0:T(1024)S(1)} %get-tuple-element.150, ...), kind=kOutput, calls=%fused_computation.17 | convolution fusion | flops 2521694208 | bytes 22042624 | tf_op jit(solution)/shard_map/dot_general | solution.py:36
  142.1 3.6 %fusion.142 = (f32[512]{0:T(512)S(1)}, f32[512,768]{1,0:T(8,128)S(1)}, bf16[1,512,768]{2,1,0:T(8,128)(2,1)S(1)}, f32[]{:T(128)}, f32[]{:T(128)}) fusion(f32[768]{0:T(1024)S(1)} %get-tuple-element.149, f32[768]{0:T(1024)S(1)} %get-tuple-element.150, f32[768]{0:T(1024)S(1)} %get-tuple-element.151, f32[512]{0:T(512)S(1)} %fusion.78, ...), kind=kOutput, calls=%fused_computation.299 | convolution fusion | flops 2421423616 | bytes 13389832 | tf_op jit(solution)/shard_map/dot_general | solution.py:26
  150.5 7.6 %fusion.148 = (bf16[3072]{0:T(1024)(128)(2,1)S(1)}, bf16[512,3072]{1,0:T(8,128)(2,1)S(1)}) fusion(f32[512,3072]{1,0:T(8,128)} %get-tuple-element.116, bf16[512,768]{1,0:T(8,128)(2,1)S(1)} %get-tuple-element.98, bf16[6144,768]{1,0:T(8,128)(2,1)S(1)} %copy-done.51, f32[512,3072]{1,0:T(8,128)} %get-tuple-element.164, f32[3072]{0:T(1024)S(1)} %slice_convert_fusion), kind=kOutput, calls=%fused_computation.304 | convolution fusion | flops 2441081856 | bytes 21252096 | tf_op jit(solution)/shard_map/dot_general | solution.py:36
  158.1 3.0 multiply_reduce_fusion.5
  165.0 9.1 %convolution_convert_fusion = bf16[2,3072,768]{2,1,0:T(8,128)(2,1)} fusion(bf16[1,512,3072]{2,1,0:T(8,128)(2,1)S(1)} %bitcast.327, bf16[1,512,3072]{2,1,0:T(8,128)(2,1)S(1)} %bitcast.328, bf16[1,512,768]{2,1,0:T(8,128)(2,1)S(1)} %bitcast.321, bf16[1,512,768]{2,1,0:T(8,128)(2,1)S(1)} %get-tuple-element.128), kind=kOutput, calls=%fused_computation.9 | convolution fusion | flops 4840488960 | bytes 17301504 | tf_op jit(solution)/shard_map/dot_general | solution.py:398
  177.6 7.3 %bitcast_reduce_fusion = (bf16[12,64]{1,0:T(8,128)(2,1)S(1)}, bf16[12,64,512]{2,1,0:T(8,128)(2,1)S(1)}) fusion(bf16[512,12,64]{0,2,1:T(8,128)(2,1)S(1)} %bitcast.296, f32[12,512,512]{1,2,0:T(8,128)} %copy-done, f32[12,512]{1,0:T(8,128)S(1)} %log_add_fusion), kind=kOutput, calls=%fused_computation.96 | convolution fusion | flops 409730304 | bytes 14181888 | tf_op jit(solution)/shard_map/while/body/eval_jaxpr/hqk,qhd->khd/dot_general | solution.py:98
  186.7 11.5 %multiply_reduce_fusion = (f32[12,512]{1,0:T(8,128)S(1)}, f32[12,512,512]{1,2,0:T(8,128)}) fusion(f32[12,512,512]{1,2,0:T(8,128)} %copy-done, f32[12,512]{1,0:T(8,128)S(1)} %log_add_fusion, bf16[512,12,64]{0,2,1:T(8,128)(2,1)S(1)} %bitcast.297, bf16[512,12,64]{0,2,1:T(8,128)(2,1)S(1)} %bitcast.318), kind=kOutput, calls=%fused_computation.1 | convolution fusion | flops 412084224 | bytes 26787840 | tf_op jit(solution)/shard_map/while/body/eval_jaxpr/qhd,khd->hqk/dot_general | solution.py:101
  199.7 7.5 %multiply_convert_fusion = bf16[12,512,512]{1,2,0:T(8,128)(2,1)S(1)} fusion(f32[12,512,512]{1,2,0:T(8,128)} %get-tuple-element.167, f32[12,512,512]{1,2,0:T(8,128)S(1)} %bitcast.293, f32[12,512]{1,0:T(8,128)S(1)} %get-tuple-element.166, f32[12,512]{1,0:T(8,128)S(1)} %log_add_fusion), kind=kLoop, calls=%fused_computation | loop fusion | flops 12582912 | bytes 31506432 | tf_op jit(solution)/shard_map/while/body/eval_jaxpr/convert_element_type | solution.py:105
  219.8 2.7 fusion.132
  224.7 2.5 fusion.152
  231.8 4.3 %collective-permute-done.33 = bf16[4,16,768]{2,1,0:T(8,128)(2,1)S(1)} collective-permute-done((bf16[4,16,768]{2,1,0:T(8,128)(2,1)S(1)}, bf16[4,16,768]{2,1,0:T(8,128)(2,1)S(1)}, u32[]{:S(2)}, u32[]{:S(2)}) %collective-permute-start.33) | collective-permute-done | bytes 98336 | tf_op jit(solution)/shard_map/ppermute | solution.py:179
  240.0 6.3 %collective-permute-start.38 = (bf16[16,768]{1,0:T(8,128)(2,1)S(1)}, bf16[16,768]{1,0:T(8,128)(2,1)S(1)}, u32[]{:S(2)}, u32[]{:S(2)}) collective-permute-start(bf16[16,768]{1,0:T(8,128)(2,1)S(1)} %get-tuple-element.143), channel_id=1, source_target_pairs={{0,24},{1,25},{2,26},{3,27},{4,28},{5,29},{6,30},{7,31}} | collective-permute-start | bytes 73736 | tf_op jit(solution)/shard_map/ppermute | solution.py:179
  247.7 5.4 %collective-permute-start.36 = (bf16[16,768]{1,0:T(8,128)(2,1)S(1)}, bf16[16,768]{1,0:T(8,128)(2,1)S(1)}, u32[]{:S(2)}, u32[]{:S(2)}) collective-permute-start(bf16[16,768]{1,0:T(8,128)(2,1)S(1)} %get-tuple-element.145), channel_id=1, source_target_pairs={{0,16},{1,17},{2,18},{3,19},{4,20},{5,21},{6,22},{7,23},{8,24},{9,... | collective-permute-start | bytes 73736 | tf_op jit(solution)/shard_map/ppermute | solution.py:179
  258.0 4.9 %collective-permute-start.34 = (bf16[16,768]{1,0:T(8,128)(2,1)S(1)}, bf16[16,768]{1,0:T(8,128)(2,1)S(1)}, u32[]{:S(2)}, u32[]{:S(2)}) collective-permute-start(bf16[16,768]{1,0:T(8,128)(2,1)S(1)} %get-tuple-element.141), channel_id=1, source_target_pairs={{0,8},{1,9},{2,10},{3,11},{4,12},{5,13},{6,14},{7,15},{8,16},{9,17... | collective-permute-start | bytes 73736 | tf_op jit(solution)/shard_map/ppermute | solution.py:179
  270.6 13.9 %collective-permute-done.23 = bf16[4,96,768]{2,1,0:T(8,128)(2,1)S(1)} collective-permute-done((bf16[4,96,768]{2,1,0:T(8,128)(2,1)}, bf16[4,96,768]{2,1,0:T(8,128)(2,1)S(1)}, u32[]{:S(2)}, u32[]{:S(2)}) %collective-permute-start.23) | collective-permute-done | bytes 589856 | tf_op jit(solution)/shard_map/ppermute | solution.py:179
  284.5 14.2 %collective-permute-done.22 = bf16[4,96,768]{2,1,0:T(8,128)(2,1)S(1)} collective-permute-done((bf16[4,96,768]{2,1,0:T(8,128)(2,1)}, bf16[4,96,768]{2,1,0:T(8,128)(2,1)S(1)}, u32[]{:S(2)}, u32[]{:S(2)}) %collective-permute-start.22) | collective-permute-done | bytes 589856 | tf_op jit(solution)/shard_map/ppermute | solution.py:179
  302.4 6.3 %collective-permute-start.28 = (bf16[96,768]{1,0:T(8,128)(2,1)S(1)}, bf16[96,768]{1,0:T(8,128)(2,1)S(1)}, u32[]{:S(2)}, u32[]{:S(2)}) collective-permute-start(bf16[96,768]{1,0:T(8,128)(2,1)S(1)} %get-tuple-element.134), channel_id=1, source_target_pairs={{0,24},{1,25},{2,26},{3,27},{4,28},{5,29},{6,30},{7,31}} | collective-permute-start | bytes 442376 | tf_op jit(solution)/shard_map/ppermute | solution.py:179
  310.1 5.5 %collective-permute-start.26 = (bf16[96,768]{1,0:T(8,128)(2,1)S(1)}, bf16[96,768]{1,0:T(8,128)(2,1)S(1)}, u32[]{:S(2)}, u32[]{:S(2)}) collective-permute-start(bf16[96,768]{1,0:T(8,128)(2,1)S(1)} %get-tuple-element.136), channel_id=1, source_target_pairs={{0,16},{1,17},{2,18},{3,19},{4,20},{5,21},{6,22},{7,23},{8,24},{9,... | collective-permute-start | bytes 442376 | tf_op jit(solution)/shard_map/ppermute | solution.py:179
  316.9 4.6 %collective-permute-start.24 = (bf16[96,768]{1,0:T(8,128)(2,1)S(1)}, bf16[96,768]{1,0:T(8,128)(2,1)S(1)}, u32[]{:S(2)}, u32[]{:S(2)}) collective-permute-start(bf16[96,768]{1,0:T(8,128)(2,1)S(1)} %get-tuple-element.132), channel_id=1, source_target_pairs={{0,8},{1,9},{2,10},{3,11},{4,12},{5,13},{6,14},{7,15},{8,16},{9,17... | collective-permute-start | bytes 442376 | tf_op jit(solution)/shard_map/ppermute | solution.py:179
  322.0 3.8 %collective-permute-done.25 = bf16[96,768]{1,0:T(8,128)(2,1)S(1)} collective-permute-done((bf16[96,768]{1,0:T(8,128)(2,1)S(1)}, bf16[96,768]{1,0:T(8,128)(2,1)S(1)}, u32[]{:S(2)}, u32[]{:S(2)}) %collective-permute-start.25) | collective-permute-done | bytes 147488 | tf_op jit(solution)/shard_map/ppermute | solution.py:179
  327.0 2.5 fusion.135
  (290 shorter events, 103.9 us)
Async XLA Ops:
  7.2 114.0 %all-gather.2.cloned.1.call-start = ((), (), s32[]{:S(2)}) async-start(), calls=%async_computation.1 | async-start | bytes 9732096 | tf_op jit(solution)/shard_map/all_gather | solution.py:259
  9.1 318.0 %reduce-scatter.2.cloned.1.call-start = ((), (), s32[]{:S(2)}) async-start(), calls=%async_computation.2 | async-start | bytes 9732096 | tf_op jit(solution)/shard_map/reduce_scatter | solution.py:268
  10.1 19.7 %collective-permute-start.5 = (bf16[96,768]{1,0:T(8,128)(2,1)S(1)}, bf16[96,768]{1,0:T(8,128)(2,1)S(1)}, u32[]{:S(2)}, u32[]{:S(2)}) collective-permute-start(bf16[96,768]{1,0:T(8,128)(2,1)S(1)} %convert_element_type.391), channel_id=1, source_target_pairs={{0,8},{1,9},{2,10},{3,11},{4,12},{5,13},{6,14},{7,15},{8,16},{9,17... | collective-permute-start | bytes 442376 | tf_op jit(solution)/shard_map/ppermute | solution.py:179
  15.1 16.1 %collective-permute-start.4 = (bf16[96,768]{1,0:T(8,128)(2,1)S(1)}, bf16[96,768]{1,0:T(8,128)(2,1)S(1)}, u32[]{:S(2)}, u32[]{:S(2)}) collective-permute-start(bf16[96,768]{1,0:T(8,128)(2,1)S(1)} %convert_element_type.391), channel_id=1, source_target_pairs={{8,0},{9,1},{10,2},{11,3},{12,4},{13,5},{14,6},{15,7},{16,8},{17,9... | collective-permute-start | bytes 442376 | tf_op jit(solution)/shard_map/ppermute | solution.py:179
  16.4 14.8 %collective-permute-start.3 = (bf16[96,768]{1,0:T(8,128)(2,1)S(1)}, bf16[96,768]{1,0:T(8,128)(2,1)S(1)}, u32[]{:S(2)}, u32[]{:S(2)}) collective-permute-start(bf16[96,768]{1,0:T(8,128)(2,1)S(1)} %convert_element_type.391), channel_id=1, source_target_pairs={{0,16},{1,17},{2,18},{3,19},{4,20},{5,21},{6,22},{7,23},{8,24},{9,... | collective-permute-start | bytes 442376 | tf_op jit(solution)/shard_map/ppermute | solution.py:179
  21.9 20.2 %collective-permute-start.2 = (bf16[96,768]{1,0:T(8,128)(2,1)S(1)}, bf16[96,768]{1,0:T(8,128)(2,1)S(1)}, u32[]{:S(2)}, u32[]{:S(2)}) collective-permute-start(bf16[96,768]{1,0:T(8,128)(2,1)S(1)} %convert_element_type.391), channel_id=1, source_target_pairs={{16,0},{17,1},{18,2},{19,3},{20,4},{21,5},{22,6},{23,7},{24,8},{25... | collective-permute-start | bytes 442376 | tf_op jit(solution)/shard_map/ppermute | solution.py:179
  23.2 18.9 %collective-permute-start.1 = (bf16[96,768]{1,0:T(8,128)(2,1)S(1)}, bf16[96,768]{1,0:T(8,128)(2,1)S(1)}, u32[]{:S(2)}, u32[]{:S(2)}) collective-permute-start(bf16[96,768]{1,0:T(8,128)(2,1)S(1)} %convert_element_type.391), channel_id=1, source_target_pairs={{0,24},{1,25},{2,26},{3,27},{4,28},{5,29},{6,30},{7,31}} | collective-permute-start | bytes 442376 | tf_op jit(solution)/shard_map/ppermute | solution.py:179
  29.8 12.4 %collective-permute-start = (bf16[96,768]{1,0:T(8,128)(2,1)S(1)}, bf16[96,768]{1,0:T(8,128)(2,1)S(1)}, u32[]{:S(2)}, u32[]{:S(2)}) collective-permute-start(bf16[96,768]{1,0:T(8,128)(2,1)S(1)} %convert_element_type.391), channel_id=1, source_target_pairs={{24,0},{25,1},{26,2},{27,3},{28,4},{29,5},{30,6},{31,7}} | collective-permute-start | bytes 442376 | tf_op jit(solution)/shard_map/ppermute | solution.py:179
  42.5 31.0 %collective-permute-start.6 = (bf16[4,96,768]{2,1,0:T(8,128)(2,1)S(1)}, bf16[4,96,768]{2,1,0:T(8,128)(2,1)S(1)}, u32[]{:S(2)}, u32[]{:S(2)}) collective-permute-start(bf16[4,96,768]{2,1,0:T(8,128)(2,1)S(1)} %select_select_fusion), channel_id=1, source_target_pairs={{0,1},{1,0},{2,3},{3,2},{4,5},{5,4},{6,7},{7,6},{8,9},{9,8},{10,11... | collective-permute-start | bytes 1769480 | tf_op jit(solution)/shard_map/ppermute | solution.py:179
  44.1 31.3 %collective-permute-start.8 = (bf16[4,96,768]{2,1,0:T(8,128)(2,1)S(1)}, bf16[4,96,768]{2,1,0:T(8,128)(2,1)S(1)}, u32[]{:S(2)}, u32[]{:S(2)}) collective-permute-start(bf16[4,96,768]{2,1,0:T(8,128)(2,1)S(1)} %select_select_fusion), channel_id=1, source_target_pairs={{0,5},{1,4},{2,7},{3,6},{4,1},{5,0},{6,3},{7,2},{8,13},{9,12},{10,... | collective-permute-start | bytes 1769480 | tf_op jit(solution)/shard_map/ppermute | solution.py:179
  45.6 33.5 %collective-permute-start.7 = (bf16[4,96,768]{2,1,0:T(8,128)(2,1)S(1)}, bf16[4,96,768]{2,1,0:T(8,128)(2,1)}, u32[]{:S(2)}, u32[]{:S(2)}) collective-permute-start(bf16[4,96,768]{2,1,0:T(8,128)(2,1)S(1)} %select_select_fusion), channel_id=1, source_target_pairs={{0,4},{1,5},{2,6},{3,7},{4,0},{5,1},{6,2},{7,3},{8,12},{9,13},{10,... | collective-permute-start | bytes 1769480 | tf_op jit(solution)/shard_map/ppermute | solution.py:179
  48.0 34.7 %collective-permute-start.15 = (bf16[1,768]{1,0:T(2,128)(2,1)}, bf16[1,768]{1,0:T(2,128)(2,1)}, u32[]{:S(2)}, u32[]{:S(2)}) collective-permute-start(bf16[1,768]{1,0:T(2,128)(2,1)} %get-tuple-element.155), channel_id=1, source_target_pairs={{0,8},{1,9},{2,10},{3,11},{4,12},{5,13},{6,14},{7,15},{8,16},{9,17... | collective-permute-start | bytes 4616 | tf_op jit(solution)/shard_map/ppermute | solution.py:179
  49.9 36.4 %collective-permute-start.14 = (bf16[1,768]{1,0:T(2,128)(2,1)}, bf16[1,768]{1,0:T(2,128)(2,1)}, u32[]{:S(2)}, u32[]{:S(2)}) collective-permute-start(bf16[1,768]{1,0:T(2,128)(2,1)} %get-tuple-element.155), channel_id=1, source_target_pairs={{8,0},{9,1},{10,2},{11,3},{12,4},{13,5},{14,6},{15,7},{16,8},{17,9... | collective-permute-start | bytes 4616 | tf_op jit(solution)/shard_map/ppermute | solution.py:179
  73.5 15.6 %collective-permute-start.13 = (bf16[1,768]{1,0:T(2,128)(2,1)}, bf16[1,768]{1,0:T(2,128)(2,1)}, u32[]{:S(2)}, u32[]{:S(2)}) collective-permute-start(bf16[1,768]{1,0:T(2,128)(2,1)} %get-tuple-element.155), channel_id=1, source_target_pairs={{0,16},{1,17},{2,18},{3,19},{4,20},{5,21},{6,22},{7,23},{8,24},{9,... | collective-permute-start | bytes 4616 | tf_op jit(solution)/shard_map/ppermute | solution.py:179
  75.4 14.5 %collective-permute-start.12 = (bf16[1,768]{1,0:T(2,128)(2,1)}, bf16[1,768]{1,0:T(2,128)(2,1)}, u32[]{:S(2)}, u32[]{:S(2)}) collective-permute-start(bf16[1,768]{1,0:T(2,128)(2,1)} %get-tuple-element.155), channel_id=1, source_target_pairs={{16,0},{17,1},{18,2},{19,3},{20,4},{21,5},{22,6},{23,7},{24,8},{25... | collective-permute-start | bytes 4616 | tf_op jit(solution)/shard_map/ppermute | solution.py:179
  82.6 21.3 %collective-permute-start.9 = (bf16[4,2,2,96,768]{4,3,2,1,0:T(8,128)(2,1)}, bf16[4,2,2,96,768]{4,3,2,1,0:T(8,128)(2,1)}, u32[]{:S(2)}, u32[]{:S(2)}) collective-permute-start(bf16[4,2,2,96,768]{4,3,2,1,0:T(8,128)(2,1)} %broadcast_select_fusion), channel_id=1, source_target_pairs={{0,2},{1,3},{2,0},{3,1},{4,6},{5,7},{6,4},{7,5},{8,10},{9,11},{10,... | collective-permute-start | bytes 7077896 | tf_op jit(solution)/shard_map/ppermute | solution.py:179
  216.6 36.5 %collective-permute-start.20 = (bf16[4,2,2,96,768]{4,3,0,2,1:T(8,128)(2,1)}, bf16[4,2,2,96,768]{4,3,0,2,1:T(8,128)(2,1)}, u32[]{:S(2)}, u32[]{:S(2)}) collective-permute-start(bf16[4,2,2,96,768]{4,3,0,2,1:T(8,128)(2,1)} %bitcast.288), channel_id=1, source_target_pairs={{0,2},{1,3},{2,0},{3,1},{4,6},{5,7},{6,4},{7,5},{8,10},{9,11},{10,... | collective-permute-start | bytes 7077896 | tf_op jit(solution)/shard_map/ppermute | solution.py:179
  229.4 9.0 %collective-permute-start.32 = (bf16[4,16,768]{2,1,0:T(8,128)(2,1)S(1)}, bf16[4,16,768]{2,1,0:T(8,128)(2,1)S(1)}, u32[]{:S(2)}, u32[]{:S(2)}) collective-permute-start(bf16[4,16,768]{2,1,0:T(8,128)(2,1)S(1)} %get-tuple-element.140), channel_id=1, source_target_pairs={{0,1},{1,0},{2,3},{3,2},{4,5},{5,4},{6,7},{7,6},{8,9},{9,8},{10,11... | collective-permute-start | bytes 294920 | tf_op jit(solution)/shard_map/ppermute | solution.py:179
  238.7 19.2 %collective-permute-start.39 = (bf16[16,768]{1,0:T(8,128)(2,1)S(1)}, bf16[16,768]{1,0:T(8,128)(2,1)S(1)}, u32[]{:S(2)}, u32[]{:S(2)}) collective-permute-start(bf16[16,768]{1,0:T(8,128)(2,1)S(1)} %get-tuple-element.142), channel_id=1, source_target_pairs={{24,0},{25,1},{26,2},{27,3},{28,4},{29,5},{30,6},{31,7}} | collective-permute-start | bytes 73736 | tf_op jit(solution)/shard_map/ppermute | solution.py:179
  240.0 22.9 %collective-permute-start.38 = (bf16[16,768]{1,0:T(8,128)(2,1)S(1)}, bf16[16,768]{1,0:T(8,128)(2,1)S(1)}, u32[]{:S(2)}, u32[]{:S(2)}) collective-permute-start(bf16[16,768]{1,0:T(8,128)(2,1)S(1)} %get-tuple-element.143), channel_id=1, source_target_pairs={{0,24},{1,25},{2,26},{3,27},{4,28},{5,29},{6,30},{7,31}} | collective-permute-start | bytes 73736 | tf_op jit(solution)/shard_map/ppermute | solution.py:179
  246.4 18.1 %collective-permute-start.37 = (bf16[16,768]{1,0:T(8,128)(2,1)S(1)}, bf16[16,768]{1,0:T(8,128)(2,1)S(1)}, u32[]{:S(2)}, u32[]{:S(2)}) collective-permute-start(bf16[16,768]{1,0:T(8,128)(2,1)S(1)} %get-tuple-element.144), channel_id=1, source_target_pairs={{16,0},{17,1},{18,2},{19,3},{20,4},{21,5},{22,6},{23,7},{24,8},{25... | collective-permute-start | bytes 73736 | tf_op jit(solution)/shard_map/ppermute | solution.py:179
  247.7 17.7 %collective-permute-start.36 = (bf16[16,768]{1,0:T(8,128)(2,1)S(1)}, bf16[16,768]{1,0:T(8,128)(2,1)S(1)}, u32[]{:S(2)}, u32[]{:S(2)}) collective-permute-start(bf16[16,768]{1,0:T(8,128)(2,1)S(1)} %get-tuple-element.145), channel_id=1, source_target_pairs={{0,16},{1,17},{2,18},{3,19},{4,20},{5,21},{6,22},{7,23},{8,24},{9,... | collective-permute-start | bytes 73736 | tf_op jit(solution)/shard_map/ppermute | solution.py:179
  253.1 15.5 %collective-permute-start.35 = (bf16[16,768]{1,0:T(8,128)(2,1)S(1)}, bf16[16,768]{1,0:T(8,128)(2,1)S(1)}, u32[]{:S(2)}, u32[]{:S(2)}) collective-permute-start(bf16[16,768]{1,0:T(8,128)(2,1)S(1)} %get-tuple-element.146), channel_id=1, source_target_pairs={{8,0},{9,1},{10,2},{11,3},{12,4},{13,5},{14,6},{15,7},{16,8},{17,9... | collective-permute-start | bytes 73736 | tf_op jit(solution)/shard_map/ppermute | solution.py:179
  258.0 10.7 %collective-permute-start.34 = (bf16[16,768]{1,0:T(8,128)(2,1)S(1)}, bf16[16,768]{1,0:T(8,128)(2,1)S(1)}, u32[]{:S(2)}, u32[]{:S(2)}) collective-permute-start(bf16[16,768]{1,0:T(8,128)(2,1)S(1)} %get-tuple-element.141), channel_id=1, source_target_pairs={{0,8},{1,9},{2,10},{3,11},{4,12},{5,13},{6,14},{7,15},{8,16},{9,17... | collective-permute-start | bytes 73736 | tf_op jit(solution)/shard_map/ppermute | solution.py:179
  262.9 21.6 %collective-permute-start.23 = (bf16[4,96,768]{2,1,0:T(8,128)(2,1)}, bf16[4,96,768]{2,1,0:T(8,128)(2,1)S(1)}, u32[]{:S(2)}, u32[]{:S(2)}) collective-permute-start(bf16[4,96,768]{2,1,0:T(8,128)(2,1)} %get-tuple-element.120), channel_id=1, source_target_pairs={{0,5},{1,4},{2,7},{3,6},{4,1},{5,0},{6,3},{7,2},{8,13},{9,12},{10,... | collective-permute-start | bytes 1769480 | tf_op jit(solution)/shard_map/ppermute | solution.py:179
  264.4 34.2 %collective-permute-start.22 = (bf16[4,96,768]{2,1,0:T(8,128)(2,1)}, bf16[4,96,768]{2,1,0:T(8,128)(2,1)S(1)}, u32[]{:S(2)}, u32[]{:S(2)}) collective-permute-start(bf16[4,96,768]{2,1,0:T(8,128)(2,1)} %get-tuple-element.121), channel_id=1, source_target_pairs={{0,1},{1,0},{2,3},{3,2},{4,5},{5,4},{6,7},{7,6},{8,9},{9,8},{10,11... | collective-permute-start | bytes 1769480 | tf_op jit(solution)/shard_map/ppermute | solution.py:179
  265.4 33.3 %collective-permute-start.21 = (bf16[4,96,768]{2,1,0:T(8,128)(2,1)}, bf16[4,96,768]{2,1,0:T(8,128)(2,1)S(1)}, u32[]{:S(2)}, u32[]{:S(2)}) collective-permute-start(bf16[4,96,768]{2,1,0:T(8,128)(2,1)} %get-tuple-element.119), channel_id=1, source_target_pairs={{0,4},{1,5},{2,6},{3,7},{4,0},{5,1},{6,2},{7,3},{8,12},{9,13},{10,... | collective-permute-start | bytes 1769480 | tf_op jit(solution)/shard_map/ppermute | solution.py:179
  300.4 16.5 %collective-permute-start.29 = (bf16[96,768]{1,0:T(8,128)(2,1)S(1)}, bf16[96,768]{1,0:T(8,128)(2,1)S(1)}, u32[]{:S(2)}, u32[]{:S(2)}) collective-permute-start(bf16[96,768]{1,0:T(8,128)(2,1)S(1)} %get-tuple-element.133), channel_id=1, source_target_pairs={{24,0},{25,1},{26,2},{27,3},{28,4},{29,5},{30,6},{31,7}} | collective-permute-start | bytes 442376 | tf_op jit(solution)/shard_map/ppermute | solution.py:179
  302.4 19.5 %collective-permute-start.28 = (bf16[96,768]{1,0:T(8,128)(2,1)S(1)}, bf16[96,768]{1,0:T(8,128)(2,1)S(1)}, u32[]{:S(2)}, u32[]{:S(2)}) collective-permute-start(bf16[96,768]{1,0:T(8,128)(2,1)S(1)} %get-tuple-element.134), channel_id=1, source_target_pairs={{0,24},{1,25},{2,26},{3,27},{4,28},{5,29},{6,30},{7,31}} | collective-permute-start | bytes 442376 | tf_op jit(solution)/shard_map/ppermute | solution.py:179
  308.8 13.2 %collective-permute-start.27 = (bf16[96,768]{1,0:T(8,128)(2,1)S(1)}, bf16[96,768]{1,0:T(8,128)(2,1)S(1)}, u32[]{:S(2)}, u32[]{:S(2)}) collective-permute-start(bf16[96,768]{1,0:T(8,128)(2,1)S(1)} %get-tuple-element.135), channel_id=1, source_target_pairs={{16,0},{17,1},{18,2},{19,3},{20,4},{21,5},{22,6},{23,7},{24,8},{25... | collective-permute-start | bytes 442376 | tf_op jit(solution)/shard_map/ppermute | solution.py:179
  310.1 11.9 %collective-permute-start.26 = (bf16[96,768]{1,0:T(8,128)(2,1)S(1)}, bf16[96,768]{1,0:T(8,128)(2,1)S(1)}, u32[]{:S(2)}, u32[]{:S(2)}) collective-permute-start(bf16[96,768]{1,0:T(8,128)(2,1)S(1)} %get-tuple-element.136), channel_id=1, source_target_pairs={{0,16},{1,17},{2,18},{3,19},{4,20},{5,21},{6,22},{7,23},{8,24},{9,... | collective-permute-start | bytes 442376 | tf_op jit(solution)/shard_map/ppermute | solution.py:179
  315.6 10.2 %collective-permute-start.25 = (bf16[96,768]{1,0:T(8,128)(2,1)S(1)}, bf16[96,768]{1,0:T(8,128)(2,1)S(1)}, u32[]{:S(2)}, u32[]{:S(2)}) collective-permute-start(bf16[96,768]{1,0:T(8,128)(2,1)S(1)} %get-tuple-element.137), channel_id=1, source_target_pairs={{8,0},{9,1},{10,2},{11,3},{12,4},{13,5},{14,6},{15,7},{16,8},{17,9... | collective-permute-start | bytes 442376 | tf_op jit(solution)/shard_map/ppermute | solution.py:179
  (65 other events, 823.9 us)
Sparse Core Ops, SparseCore 0:
  11.5 100.2 all-gather.1
  174.2 151.3 reduce-scatter.1

commit v4 on v3

--- a/solution.py
+++ b/solution.py
@@ -2,6 +2,7 @@
 import math
 
 import jax
+import numpy as np
 import jax.numpy as jnp
 from jax import lax
 from jax.sharding import PartitionSpec as P
@@ -51,6 +52,14 @@
 
 def gelu_exact(entries):
     return jax.nn.gelu(entries, approximate=False)
+
+
+def gelu_derivative(entries):
+    sqrt_half = np.sqrt(0.5).astype(np.float32)
+    shifted_entries = -entries * sqrt_half
+    return 0.5 * lax.erfc(shifted_entries) + entries * (
+        jnp.exp(-(shifted_entries * shifted_entries)) * np.float32(sqrt_half / np.sqrt(np.pi))
+    )
 
 
 def split_small(small_full):
@@ -369,6 +378,7 @@
     normed_low = normed.astype(jnp.bfloat16)
     inner_sum = product_cols(normed_low, feed_full[0:FF]) + inner_bias
     active = gelu_exact(inner_sum).astype(jnp.bfloat16)
+    gelu_slope = gelu_derivative(inner_sum)
     branch_feed = product(active, feed_full[FF : 2 * FF]) + outer_bias
     residual = normed + branch_feed
     layer_out = layer_norm(residual, second_gain, second_shift).astype(jnp.bfloat16)
@@ -392,7 +402,7 @@
     feed_out_grad = residual_grad.astype(jnp.bfloat16)
     outer_bias_grad = column_total(feed_out_grad)
     active_grad = product_cols(feed_out_grad, outer_weight)
-    inner_grad = jax.vjp(gelu_exact, inner_sum)[1](active_grad)[0].astype(jnp.bfloat16)
+    inner_grad = (active_grad * gelu_slope).astype(jnp.bfloat16)
     inner_bias_grad = column_total(inner_grad)
     feed_grad_all = (
         lax.dot_general(
@@ -404,14 +414,14 @@
         .astype(jnp.bfloat16)
         .reshape(2 * FF, D)
     )
-    normed_grad = residual_grad + product(inner_grad, inner_weight)
+    feed_grad_all, inner_grad_late = lax.optimization_barrier((feed_grad_all, inner_grad))
+    normed_grad = residual_grad + product(inner_grad_late, inner_weight)
     first_pull = jax.vjp(layer_norm, first_sum, first_gain, first_shift)[1]
     first_sum_grad, first_gain_grad, first_shift_grad = first_pull(normed_grad)
     branch_grad_low = first_sum_grad.astype(jnp.bfloat16)
     output_bias_grad = column_total(branch_grad_low)
     output_weight_grad = product_rows(attended, branch_grad_low)
     attended_grad = product_cols(branch_grad_low, output_weight).astype(jnp.bfloat16)
-    feed_grad_all, attended_grad = lax.optimization_barrier((feed_grad_all, attended_grad))
     query_grad, key_grad, value_grad = lax.map(
         attend_backward,
         (

time: 341 us -> 341 us (level)
  waiting for transfers between devices: 81.4 us -> 77 us
  matrix products: 86.9 us -> 90.8 us
    ppermute x40, waiting for transfers between devices: 81.4 us -> 76.9 us  [permute(): return lax.ppermute(tuple(arrays), ('fsdp', 'dp'), pairs)]
  transfers between devices with their start and end apart: 42 -> 42, of which waited for: 14 -> 13; matrix products, arithmetic and copies ran while one was open for 25% -> 28% of each run, Pallas kernels for 0% -> 0%
where the time goes in v4:
time: 341 us; the launch traced here: 336 us
  matrix products  90.8 us (27%)
  starting transfers between devices  88.1 us (26%)
  waiting for transfers between devices  77 us (23%)
  other arithmetic  39 us (11%)
  local copies, waits for them, and re-layouts  23.3 us (7%)
  between operations  17.9 us (5%)
    ppermute x40, starting transfers between devices, permute(): return lax.ppermute(tuple(arrays), ('fsdp', 'dp'), pairs)  88 us
    ppermute x40, waiting for transfers between devices, permute(): return lax.ppermute(tuple(arrays), ('fsdp', 'dp'), pairs)  76.9 us
    dot_general x6, matrix products, product_cols(): lax.dot_general(left_side, right_side, (((1,), (1,)), ((), ())), preferre...  36.2 us
    dot_general x6, matrix products, product(): return jnp.dot(left_side, right_side, preferred_element_type=jnp.float32)  13.4 us
    dot_general x1, matrix products, attend_backward(): jnp.einsum('qhd,khd->hqk', grad_heads, head_view(values), preferred_eleme...  11.5 us
    unnamed x119, local copies, waits for them, and re-layouts  10.9 us
    dot_general x1, matrix products, on_device(): lax.dot_general(jnp.stack([inner_grad, active]), jnp.stack([normed_low, f...  9.1 us
    convert_element_type x1, other arithmetic, attend_backward(): (probability * (probability_grad - inner_total)).astype(jnp.bfloat16)  7.43 us
  transfers between devices with their start and end apart: 42, of which 13 were waited for; matrix products, arithmetic and copies ran while one was open for 28% of the time, Pallas kernels for 0%

profile of v4, /device:TPU:0, one launch (start us, length us, event | category | flops | bytes accessed | tf_op | source)
XLA Modules:
  0.0 336.0 jit_solution(624454175287010281)
XLA Ops:
  10.1 5.0 %collective-permute-start.5 = (bf16[96,768]{1,0:T(8,128)(2,1)S(1)}, bf16[96,768]{1,0:T(8,128)(2,1)S(1)}, u32[]{:S(2)}, u32[]{:S(2)}) collective-permute-start(bf16[96,768]{1,0:T(8,128)(2,1)S(1)} %convert_element_type.391), channel_id=1, source_target_pairs={{0,8},{1,9},{2,10},{3,11},{4,12},{5,13},{6,14},{7,15},{8,16},{9,17... | collective-permute-start | bytes 442376 | tf_op jit(solution)/shard_map/ppermute | solution.py:188
  16.4 5.6 %collective-permute-start.3 = (bf16[96,768]{1,0:T(8,128)(2,1)S(1)}, bf16[96,768]{1,0:T(8,128)(2,1)S(1)}, u32[]{:S(2)}, u32[]{:S(2)}) collective-permute-start(bf16[96,768]{1,0:T(8,128)(2,1)S(1)} %convert_element_type.391), channel_id=1, source_target_pairs={{0,16},{1,17},{2,18},{3,19},{4,20},{5,21},{6,22},{7,23},{8,24},{9,... | collective-permute-start | bytes 442376 | tf_op jit(solution)/shard_map/ppermute | solution.py:188
  23.2 6.5 %collective-permute-start.1 = (bf16[96,768]{1,0:T(8,128)(2,1)S(1)}, bf16[96,768]{1,0:T(8,128)(2,1)S(1)}, u32[]{:S(2)}, u32[]{:S(2)}) collective-permute-start(bf16[96,768]{1,0:T(8,128)(2,1)S(1)} %convert_element_type.391), channel_id=1, source_target_pairs={{0,24},{1,25},{2,26},{3,27},{4,28},{5,29},{6,30},{7,31}} | collective-permute-start | bytes 442376 | tf_op jit(solution)/shard_map/ppermute | solution.py:188
  31.2 11.0 %collective-permute-done.2 = bf16[96,768]{1,0:T(8,128)(2,1)S(1)} collective-permute-done((bf16[96,768]{1,0:T(8,128)(2,1)S(1)}, bf16[96,768]{1,0:T(8,128)(2,1)S(1)}, u32[]{:S(2)}, u32[]{:S(2)}) %collective-permute-start.2) | collective-permute-done | bytes 147488 | tf_op jit(solution)/shard_map/ppermute | solution.py:188
  51.9 21.6 %collective-permute-done.6 = bf16[4,96,768]{2,1,0:T(8,128)(2,1)S(1)} collective-permute-done((bf16[4,96,768]{2,1,0:T(8,128)(2,1)S(1)}, bf16[4,96,768]{2,1,0:T(8,128)(2,1)S(1)}, u32[]{:S(2)}, u32[]{:S(2)}) %collective-permute-start.6) | collective-permute-done | bytes 589856 | tf_op jit(solution)/shard_map/ppermute | solution.py:188
  76.7 2.4 collective-permute-done.7
  82.7 3.6 %collective-permute-start.11 = (bf16[1,768]{1,0:T(2,128)(2,1)}, bf16[1,768]{1,0:T(2,128)(2,1)S(1)}, u32[]{:S(2)}, u32[]{:S(2)}) collective-permute-start(bf16[1,768]{1,0:T(2,128)(2,1)} %get-tuple-element.155), channel_id=1, source_target_pairs={{0,24},{1,25},{2,26},{3,27},{4,28},{5,29},{6,30},{7,31}} | collective-permute-start | bytes 4616 | tf_op jit(solution)/shard_map/ppermute | solution.py:188
  90.6 3.4 collective-permute-done.10
  97.9 2.4 collective-permute-done.18
  109.6 3.0 fusion.144
  114.5 2.7 copy-done
  117.2 2.7 fusion.33
  121.2 20.9 %multiply_convert_fusion.2 = (bf16[512,3072]{1,0:T(8,128)(2,1)S(1)}, f32[512,3072]{1,0:T(8,128)}, f32[512,3072]{1,0:T(8,128)}) fusion(f32[3072]{0:T(1024)S(1)} %slice_convert_fusion, bf16[6144,768]{1,0:T(8,128)(2,1)} %all-gather.2.cloned.1.call-done, f32[512,768]{1,0:T(8,128)S(1)} %get-tuple-element.118, f32[768]{0:T(1024)S(1)} %get-tuple-element.150, ...), kind=kOutput, calls=%fused_computation.17 | convolution fusion | flops 2521694208 | bytes 22042624 | tf_op jit(solution)/shard_map/dot_general | solution.py:37
  142.1 3.6 %fusion.139 = (f32[512]{0:T(512)S(1)}, f32[512,768]{1,0:T(8,128)S(1)}, bf16[1,512,768]{2,1,0:T(8,128)(2,1)S(1)}, f32[]{:T(128)}, f32[]{:T(128)}) fusion(f32[768]{0:T(1024)S(1)} %get-tuple-element.149, f32[768]{0:T(1024)S(1)} %get-tuple-element.150, f32[768]{0:T(1024)S(1)} %get-tuple-element.151, f32[512]{0:T(512)S(1)} %fusion.75, ...), kind=kOutput, calls=%fused_computation.298 | convolution fusion | flops 2421423616 | bytes 13389832 | tf_op jit(solution)/shard_map/dot_general | solution.py:27
  150.6 8.1 %fusion.145 = (bf16[3072]{0:T(1024)(128)(2,1)S(1)}, bf16[512,3072]{1,0:T(8,128)(2,1)}) fusion(f32[512,3072]{1,0:T(8,128)} %get-tuple-element.164, f32[3072]{0:T(1024)S(1)} %slice_convert_fusion, f32[512,3072]{1,0:T(8,128)} %get-tuple-element.116, bf16[512,768]{1,0:T(8,128)(2,1)S(1)} %get-tuple-element.98, bf16[6144,768]{1,0:T(8,128)(2,1)S(1)} %copy-done.51), kind=kOutput, calls=%fused_computation.303 | convolution fusion | flops 2434790400 | bytes 21252096 | tf_op jit(solution)/shard_map/dot_general | solution.py:37
  158.7 9.1 %convolution_convert_fusion = bf16[2,3072,768]{2,1,0:T(8,128)(2,1)} fusion(bf16[1,512,3072]{2,1,0:T(8,128)(2,1)S(1)} %bitcast.327, bf16[1,512,3072]{2,1,0:T(8,128)(2,1)} %bitcast.328, bf16[1,512,768]{2,1,0:T(8,128)(2,1)S(1)} %bitcast.321, bf16[1,512,768]{2,1,0:T(8,128)(2,1)S(1)} %get-tuple-element.128), kind=kOutput, calls=%fused_computation.9 | convolution fusion | flops 4840488960 | bytes 17301504 | tf_op jit(solution)/shard_map/dot_general | solution.py:408
  167.8 6.3 %multiply_reduce_fusion.5 = (bf16[768]{0:T(1024)(128)(2,1)S(1)}, f32[512]{0:T(512)S(1)}, bf16[768]{0:T(1024)(128)(2,1)S(1)}, f32[512,768]{1,0:T(8,128)S(1)}) fusion(f32[512,768]{1,0:T(8,128)S(1)} %get-tuple-element.118, f32[512]{0:T(512)S(1)} %fusion.75, f32[512]{0:T(512)S(1)} %broadcast_multiply_fusion.1, f32[768]{0:T(1024)S(1)} %get-tuple-element.151, ...), kind=kOutput, calls=%fused_computation.55 | convolution fusion | flops 2419849216 | bytes 12597248 | tf_op jit(solution)/shard_map/dot_general | solution.py:27
  181.5 7.3 %bitcast_reduce_fusion = (bf16[12,64]{1,0:T(8,128)(2,1)S(1)}, bf16[12,64,512]{2,1,0:T(8,128)(2,1)S(1)}) fusion(bf16[512,12,64]{0,2,1:T(8,128)(2,1)S(1)} %bitcast.296, f32[12,512,512]{1,2,0:T(8,128)} %copy-done, f32[12,512]{1,0:T(8,128)S(1)} %log_add_fusion), kind=kOutput, calls=%fused_computation.95 | convolution fusion | flops 409730304 | bytes 14181888 | tf_op jit(solution)/shard_map/while/body/eval_jaxpr/hqk,qhd->khd/dot_general | solution.py:107
  190.6 11.5 %multiply_reduce_fusion = (f32[12,512]{1,0:T(8,128)S(1)}, f32[12,512,512]{1,2,0:T(8,128)}) fusion(f32[12,512,512]{1,2,0:T(8,128)} %copy-done, f32[12,512]{1,0:T(8,128)S(1)} %log_add_fusion, bf16[512,12,64]{0,2,1:T(8,128)(2,1)S(1)} %bitcast.297, bf16[512,12,64]{0,2,1:T(8,128)(2,1)S(1)} %bitcast.318), kind=kOutput, calls=%fused_computation.1 | convolution fusion | flops 412084224 | bytes 26787840 | tf_op jit(solution)/shard_map/while/body/eval_jaxpr/qhd,khd->hqk/dot_general | solution.py:110
  203.6 7.4 %multiply_convert_fusion = bf16[12,512,512]{1,2,0:T(8,128)(2,1)S(1)} fusion(f32[12,512,512]{1,2,0:T(8,128)} %get-tuple-element.167, f32[12,512,512]{1,2,0:T(8,128)S(1)} %bitcast.293, f32[12,512]{1,0:T(8,128)S(1)} %get-tuple-element.166, f32[12,512]{1,0:T(8,128)S(1)} %log_add_fusion), kind=kLoop, calls=%fused_computation | loop fusion | flops 12582912 | bytes 31506432 | tf_op jit(solution)/shard_map/while/body/eval_jaxpr/convert_element_type | solution.py:114
  223.5 2.7 fusion.129
  228.5 2.5 fusion.149
  240.7 6.3 %collective-permute-start.38 = (bf16[16,768]{1,0:T(8,128)(2,1)S(1)}, bf16[16,768]{1,0:T(8,128)(2,1)S(1)}, u32[]{:S(2)}, u32[]{:S(2)}) collective-permute-start(bf16[16,768]{1,0:T(8,128)(2,1)S(1)} %get-tuple-element.143), channel_id=1, source_target_pairs={{0,24},{1,25},{2,26},{3,27},{4,28},{5,29},{6,30},{7,31}} | collective-permute-start | bytes 73736 | tf_op jit(solution)/shard_map/ppermute | solution.py:188
  248.4 5.4 %collective-permute-start.36 = (bf16[16,768]{1,0:T(8,128)(2,1)S(1)}, bf16[16,768]{1,0:T(8,128)(2,1)S(1)}, u32[]{:S(2)}, u32[]{:S(2)}) collective-permute-start(bf16[16,768]{1,0:T(8,128)(2,1)S(1)} %get-tuple-element.145), channel_id=1, source_target_pairs={{0,16},{1,17},{2,18},{3,19},{4,20},{5,21},{6,22},{7,23},{8,24},{9,... | collective-permute-start | bytes 73736 | tf_op jit(solution)/shard_map/ppermute | solution.py:188
  258.7 4.9 %collective-permute-start.34 = (bf16[16,768]{1,0:T(8,128)(2,1)S(1)}, bf16[16,768]{1,0:T(8,128)(2,1)S(1)}, u32[]{:S(2)}, u32[]{:S(2)}) collective-permute-start(bf16[16,768]{1,0:T(8,128)(2,1)S(1)} %get-tuple-element.141), channel_id=1, source_target_pairs={{0,8},{1,9},{2,10},{3,11},{4,12},{5,13},{6,14},{7,15},{8,16},{9,17... | collective-permute-start | bytes 73736 | tf_op jit(solution)/shard_map/ppermute | solution.py:188
  271.2 12.3 %collective-permute-done.23 = bf16[4,96,768]{2,1,0:T(8,128)(2,1)S(1)} collective-permute-done((bf16[4,96,768]{2,1,0:T(8,128)(2,1)}, bf16[4,96,768]{2,1,0:T(8,128)(2,1)S(1)}, u32[]{:S(2)}, u32[]{:S(2)}) %collective-permute-start.23) | collective-permute-done | bytes 589856 | tf_op jit(solution)/shard_map/ppermute | solution.py:188
  283.6 15.1 %collective-permute-done.22 = bf16[4,96,768]{2,1,0:T(8,128)(2,1)S(1)} collective-permute-done((bf16[4,96,768]{2,1,0:T(8,128)(2,1)}, bf16[4,96,768]{2,1,0:T(8,128)(2,1)S(1)}, u32[]{:S(2)}, u32[]{:S(2)}) %collective-permute-start.22) | collective-permute-done | bytes 589856 | tf_op jit(solution)/shard_map/ppermute | solution.py:188
  302.4 6.3 %collective-permute-start.28 = (bf16[96,768]{1,0:T(8,128)(2,1)S(1)}, bf16[96,768]{1,0:T(8,128)(2,1)S(1)}, u32[]{:S(2)}, u32[]{:S(2)}) collective-permute-start(bf16[96,768]{1,0:T(8,128)(2,1)S(1)} %get-tuple-element.134), channel_id=1, source_target_pairs={{0,24},{1,25},{2,26},{3,27},{4,28},{5,29},{6,30},{7,31}} | collective-permute-start | bytes 442376 | tf_op jit(solution)/shard_map/ppermute | solution.py:188
  310.1 5.5 %collective-permute-start.26 = (bf16[96,768]{1,0:T(8,128)(2,1)S(1)}, bf16[96,768]{1,0:T(8,128)(2,1)S(1)}, u32[]{:S(2)}, u32[]{:S(2)}) collective-permute-start(bf16[96,768]{1,0:T(8,128)(2,1)S(1)} %get-tuple-element.136), channel_id=1, source_target_pairs={{0,16},{1,17},{2,18},{3,19},{4,20},{5,21},{6,22},{7,23},{8,24},{9,... | collective-permute-start | bytes 442376 | tf_op jit(solution)/shard_map/ppermute | solution.py:188
  316.8 4.6 %collective-permute-start.24 = (bf16[96,768]{1,0:T(8,128)(2,1)S(1)}, bf16[96,768]{1,0:T(8,128)(2,1)S(1)}, u32[]{:S(2)}, u32[]{:S(2)}) collective-permute-start(bf16[96,768]{1,0:T(8,128)(2,1)S(1)} %get-tuple-element.132), channel_id=1, source_target_pairs={{0,8},{1,9},{2,10},{3,11},{4,12},{5,13},{6,14},{7,15},{8,16},{9,17... | collective-permute-start | bytes 442376 | tf_op jit(solution)/shard_map/ppermute | solution.py:188
  322.0 3.2 collective-permute-done.25
  326.4 2.5 fusion.132
  (290 shorter events, 102.9 us)
Async XLA Ops:
  7.2 114.0 %all-gather.2.cloned.1.call-start = ((), (), s32[]{:S(2)}) async-start(), calls=%async_computation.1 | async-start | bytes 9732096 | tf_op jit(solution)/shard_map/all_gather | solution.py:268
  9.1 317.3 %reduce-scatter.2.cloned.1.call-start = ((), (), s32[]{:S(2)}) async-start(), calls=%async_computation.2 | async-start | bytes 9732096 | tf_op jit(solution)/shard_map/reduce_scatter | solution.py:277
  10.1 19.7 %collective-permute-start.5 = (bf16[96,768]{1,0:T(8,128)(2,1)S(1)}, bf16[96,768]{1,0:T(8,128)(2,1)S(1)}, u32[]{:S(2)}, u32[]{:S(2)}) collective-permute-start(bf16[96,768]{1,0:T(8,128)(2,1)S(1)} %convert_element_type.391), channel_id=1, source_target_pairs={{0,8},{1,9},{2,10},{3,11},{4,12},{5,13},{6,14},{7,15},{8,16},{9,17... | collective-permute-start | bytes 442376 | tf_op jit(solution)/shard_map/ppermute | solution.py:188
  15.1 16.1 %collective-permute-start.4 = (bf16[96,768]{1,0:T(8,128)(2,1)S(1)}, bf16[96,768]{1,0:T(8,128)(2,1)S(1)}, u32[]{:S(2)}, u32[]{:S(2)}) collective-permute-start(bf16[96,768]{1,0:T(8,128)(2,1)S(1)} %convert_element_type.391), channel_id=1, source_target_pairs={{8,0},{9,1},{10,2},{11,3},{12,4},{13,5},{14,6},{15,7},{16,8},{17,9... | collective-permute-start | bytes 442376 | tf_op jit(solution)/shard_map/ppermute | solution.py:188
  16.4 14.8 %collective-permute-start.3 = (bf16[96,768]{1,0:T(8,128)(2,1)S(1)}, bf16[96,768]{1,0:T(8,128)(2,1)S(1)}, u32[]{:S(2)}, u32[]{:S(2)}) collective-permute-start(bf16[96,768]{1,0:T(8,128)(2,1)S(1)} %convert_element_type.391), channel_id=1, source_target_pairs={{0,16},{1,17},{2,18},{3,19},{4,20},{5,21},{6,22},{7,23},{8,24},{9,... | collective-permute-start | bytes 442376 | tf_op jit(solution)/shard_map/ppermute | solution.py:188
  21.9 20.2 %collective-permute-start.2 = (bf16[96,768]{1,0:T(8,128)(2,1)S(1)}, bf16[96,768]{1,0:T(8,128)(2,1)S(1)}, u32[]{:S(2)}, u32[]{:S(2)}) collective-permute-start(bf16[96,768]{1,0:T(8,128)(2,1)S(1)} %convert_element_type.391), channel_id=1, source_target_pairs={{16,0},{17,1},{18,2},{19,3},{20,4},{21,5},{22,6},{23,7},{24,8},{25... | collective-permute-start | bytes 442376 | tf_op jit(solution)/shard_map/ppermute | solution.py:188
  23.2 18.9 %collective-permute-start.1 = (bf16[96,768]{1,0:T(8,128)(2,1)S(1)}, bf16[96,768]{1,0:T(8,128)(2,1)S(1)}, u32[]{:S(2)}, u32[]{:S(2)}) collective-permute-start(bf16[96,768]{1,0:T(8,128)(2,1)S(1)} %convert_element_type.391), channel_id=1, source_target_pairs={{0,24},{1,25},{2,26},{3,27},{4,28},{5,29},{6,30},{7,31}} | collective-permute-start | bytes 442376 | tf_op jit(solution)/shard_map/ppermute | solution.py:188
  29.8 12.4 %collective-permute-start = (bf16[96,768]{1,0:T(8,128)(2,1)S(1)}, bf16[96,768]{1,0:T(8,128)(2,1)S(1)}, u32[]{:S(2)}, u32[]{:S(2)}) collective-permute-start(bf16[96,768]{1,0:T(8,128)(2,1)S(1)} %convert_element_type.391), channel_id=1, source_target_pairs={{24,0},{25,1},{26,2},{27,3},{28,4},{29,5},{30,6},{31,7}} | collective-permute-start | bytes 442376 | tf_op jit(solution)/shard_map/ppermute | solution.py:188
  42.5 31.0 %collective-permute-start.6 = (bf16[4,96,768]{2,1,0:T(8,128)(2,1)S(1)}, bf16[4,96,768]{2,1,0:T(8,128)(2,1)S(1)}, u32[]{:S(2)}, u32[]{:S(2)}) collective-permute-start(bf16[4,96,768]{2,1,0:T(8,128)(2,1)S(1)} %select_select_fusion), channel_id=1, source_target_pairs={{0,1},{1,0},{2,3},{3,2},{4,5},{5,4},{6,7},{7,6},{8,9},{9,8},{10,11... | collective-permute-start | bytes 1769480 | tf_op jit(solution)/shard_map/ppermute | solution.py:188
  44.1 31.3 %collective-permute-start.8 = (bf16[4,96,768]{2,1,0:T(8,128)(2,1)S(1)}, bf16[4,96,768]{2,1,0:T(8,128)(2,1)S(1)}, u32[]{:S(2)}, u32[]{:S(2)}) collective-permute-start(bf16[4,96,768]{2,1,0:T(8,128)(2,1)S(1)} %select_select_fusion), channel_id=1, source_target_pairs={{0,5},{1,4},{2,7},{3,6},{4,1},{5,0},{6,3},{7,2},{8,13},{9,12},{10,... | collective-permute-start | bytes 1769480 | tf_op jit(solution)/shard_map/ppermute | solution.py:188
  45.6 33.5 %collective-permute-start.7 = (bf16[4,96,768]{2,1,0:T(8,128)(2,1)S(1)}, bf16[4,96,768]{2,1,0:T(8,128)(2,1)}, u32[]{:S(2)}, u32[]{:S(2)}) collective-permute-start(bf16[4,96,768]{2,1,0:T(8,128)(2,1)S(1)} %select_select_fusion), channel_id=1, source_target_pairs={{0,4},{1,5},{2,6},{3,7},{4,0},{5,1},{6,2},{7,3},{8,12},{9,13},{10,... | collective-permute-start | bytes 1769480 | tf_op jit(solution)/shard_map/ppermute | solution.py:188
  48.0 34.7 %collective-permute-start.15 = (bf16[1,768]{1,0:T(2,128)(2,1)}, bf16[1,768]{1,0:T(2,128)(2,1)}, u32[]{:S(2)}, u32[]{:S(2)}) collective-permute-start(bf16[1,768]{1,0:T(2,128)(2,1)} %get-tuple-element.155), channel_id=1, source_target_pairs={{0,8},{1,9},{2,10},{3,11},{4,12},{5,13},{6,14},{7,15},{8,16},{9,17... | collective-permute-start | bytes 4616 | tf_op jit(solution)/shard_map/ppermute | solution.py:188
  49.9 36.4 %collective-permute-start.14 = (bf16[1,768]{1,0:T(2,128)(2,1)}, bf16[1,768]{1,0:T(2,128)(2,1)}, u32[]{:S(2)}, u32[]{:S(2)}) collective-permute-start(bf16[1,768]{1,0:T(2,128)(2,1)} %get-tuple-element.155), channel_id=1, source_target_pairs={{8,0},{9,1},{10,2},{11,3},{12,4},{13,5},{14,6},{15,7},{16,8},{17,9... | collective-permute-start | bytes 4616 | tf_op jit(solution)/shard_map/ppermute | solution.py:188
  73.5 15.6 %collective-permute-start.13 = (bf16[1,768]{1,0:T(2,128)(2,1)}, bf16[1,768]{1,0:T(2,128)(2,1)}, u32[]{:S(2)}, u32[]{:S(2)}) collective-permute-start(bf16[1,768]{1,0:T(2,128)(2,1)} %get-tuple-element.155), channel_id=1, source_target_pairs={{0,16},{1,17},{2,18},{3,19},{4,20},{5,21},{6,22},{7,23},{8,24},{9,... | collective-permute-start | bytes 4616 | tf_op jit(solution)/shard_map/ppermute | solution.py:188
  75.4 14.5 %collective-permute-start.12 = (bf16[1,768]{1,0:T(2,128)(2,1)}, bf16[1,768]{1,0:T(2,128)(2,1)}, u32[]{:S(2)}, u32[]{:S(2)}) collective-permute-start(bf16[1,768]{1,0:T(2,128)(2,1)} %get-tuple-element.155), channel_id=1, source_target_pairs={{16,0},{17,1},{18,2},{19,3},{20,4},{21,5},{22,6},{23,7},{24,8},{25... | collective-permute-start | bytes 4616 | tf_op jit(solution)/shard_map/ppermute | solution.py:188
  82.6 21.3 %collective-permute-start.9 = (bf16[4,2,2,96,768]{4,3,2,1,0:T(8,128)(2,1)}, bf16[4,2,2,96,768]{4,3,2,1,0:T(8,128)(2,1)}, u32[]{:S(2)}, u32[]{:S(2)}) collective-permute-start(bf16[4,2,2,96,768]{4,3,2,1,0:T(8,128)(2,1)} %broadcast_select_fusion), channel_id=1, source_target_pairs={{0,2},{1,3},{2,0},{3,1},{4,6},{5,7},{6,4},{7,5},{8,10},{9,11},{10,... | collective-permute-start | bytes 7077896 | tf_op jit(solution)/shard_map/ppermute | solution.py:188
  220.4 33.5 %collective-permute-start.20 = (bf16[4,2,2,96,768]{4,3,0,2,1:T(8,128)(2,1)}, bf16[4,2,2,96,768]{4,3,0,2,1:T(8,128)(2,1)}, u32[]{:S(2)}, u32[]{:S(2)}) collective-permute-start(bf16[4,2,2,96,768]{4,3,0,2,1:T(8,128)(2,1)} %bitcast.288), channel_id=1, source_target_pairs={{0,2},{1,3},{2,0},{3,1},{4,6},{5,7},{6,4},{7,5},{8,10},{9,11},{10,... | collective-permute-start | bytes 7077896 | tf_op jit(solution)/shard_map/ppermute | solution.py:188
  239.4 19.3 %collective-permute-start.39 = (bf16[16,768]{1,0:T(8,128)(2,1)S(1)}, bf16[16,768]{1,0:T(8,128)(2,1)S(1)}, u32[]{:S(2)}, u32[]{:S(2)}) collective-permute-start(bf16[16,768]{1,0:T(8,128)(2,1)S(1)} %get-tuple-element.142), channel_id=1, source_target_pairs={{24,0},{25,1},{26,2},{27,3},{28,4},{29,5},{30,6},{31,7}} | collective-permute-start | bytes 73736 | tf_op jit(solution)/shard_map/ppermute | solution.py:188
  240.7 22.9 %collective-permute-start.38 = (bf16[16,768]{1,0:T(8,128)(2,1)S(1)}, bf16[16,768]{1,0:T(8,128)(2,1)S(1)}, u32[]{:S(2)}, u32[]{:S(2)}) collective-permute-start(bf16[16,768]{1,0:T(8,128)(2,1)S(1)} %get-tuple-element.143), channel_id=1, source_target_pairs={{0,24},{1,25},{2,26},{3,27},{4,28},{5,29},{6,30},{7,31}} | collective-permute-start | bytes 73736 | tf_op jit(solution)/shard_map/ppermute | solution.py:188
  247.1 18.0 %collective-permute-start.37 = (bf16[16,768]{1,0:T(8,128)(2,1)S(1)}, bf16[16,768]{1,0:T(8,128)(2,1)S(1)}, u32[]{:S(2)}, u32[]{:S(2)}) collective-permute-start(bf16[16,768]{1,0:T(8,128)(2,1)S(1)} %get-tuple-element.144), channel_id=1, source_target_pairs={{16,0},{17,1},{18,2},{19,3},{20,4},{21,5},{22,6},{23,7},{24,8},{25... | collective-permute-start | bytes 73736 | tf_op jit(solution)/shard_map/ppermute | solution.py:188
  248.4 17.8 %collective-permute-start.36 = (bf16[16,768]{1,0:T(8,128)(2,1)S(1)}, bf16[16,768]{1,0:T(8,128)(2,1)S(1)}, u32[]{:S(2)}, u32[]{:S(2)}) collective-permute-start(bf16[16,768]{1,0:T(8,128)(2,1)S(1)} %get-tuple-element.145), channel_id=1, source_target_pairs={{0,16},{1,17},{2,18},{3,19},{4,20},{5,21},{6,22},{7,23},{8,24},{9,... | collective-permute-start | bytes 73736 | tf_op jit(solution)/shard_map/ppermute | solution.py:188
  253.8 15.5 %collective-permute-start.35 = (bf16[16,768]{1,0:T(8,128)(2,1)S(1)}, bf16[16,768]{1,0:T(8,128)(2,1)S(1)}, u32[]{:S(2)}, u32[]{:S(2)}) collective-permute-start(bf16[16,768]{1,0:T(8,128)(2,1)S(1)} %get-tuple-element.146), channel_id=1, source_target_pairs={{8,0},{9,1},{10,2},{11,3},{12,4},{13,5},{14,6},{15,7},{16,8},{17,9... | collective-permute-start | bytes 73736 | tf_op jit(solution)/shard_map/ppermute | solution.py:188
  258.7 10.6 %collective-permute-start.34 = (bf16[16,768]{1,0:T(8,128)(2,1)S(1)}, bf16[16,768]{1,0:T(8,128)(2,1)S(1)}, u32[]{:S(2)}, u32[]{:S(2)}) collective-permute-start(bf16[16,768]{1,0:T(8,128)(2,1)S(1)} %get-tuple-element.141), channel_id=1, source_target_pairs={{0,8},{1,9},{2,10},{3,11},{4,12},{5,13},{6,14},{7,15},{8,16},{9,17... | collective-permute-start | bytes 73736 | tf_op jit(solution)/shard_map/ppermute | solution.py:188
  263.6 20.0 %collective-permute-start.23 = (bf16[4,96,768]{2,1,0:T(8,128)(2,1)}, bf16[4,96,768]{2,1,0:T(8,128)(2,1)S(1)}, u32[]{:S(2)}, u32[]{:S(2)}) collective-permute-start(bf16[4,96,768]{2,1,0:T(8,128)(2,1)} %get-tuple-element.120), channel_id=1, source_target_pairs={{0,5},{1,4},{2,7},{3,6},{4,1},{5,0},{6,3},{7,2},{8,13},{9,12},{10,... | collective-permute-start | bytes 1769480 | tf_op jit(solution)/shard_map/ppermute | solution.py:188
  265.1 33.6 %collective-permute-start.22 = (bf16[4,96,768]{2,1,0:T(8,128)(2,1)}, bf16[4,96,768]{2,1,0:T(8,128)(2,1)S(1)}, u32[]{:S(2)}, u32[]{:S(2)}) collective-permute-start(bf16[4,96,768]{2,1,0:T(8,128)(2,1)} %get-tuple-element.121), channel_id=1, source_target_pairs={{0,1},{1,0},{2,3},{3,2},{4,5},{5,4},{6,7},{7,6},{8,9},{9,8},{10,11... | collective-permute-start | bytes 1769480 | tf_op jit(solution)/shard_map/ppermute | solution.py:188
  266.2 32.4 %collective-permute-start.21 = (bf16[4,96,768]{2,1,0:T(8,128)(2,1)}, bf16[4,96,768]{2,1,0:T(8,128)(2,1)S(1)}, u32[]{:S(2)}, u32[]{:S(2)}) collective-permute-start(bf16[4,96,768]{2,1,0:T(8,128)(2,1)} %get-tuple-element.119), channel_id=1, source_target_pairs={{0,4},{1,5},{2,6},{3,7},{4,0},{5,1},{6,2},{7,3},{8,12},{9,13},{10,... | collective-permute-start | bytes 1769480 | tf_op jit(solution)/shard_map/ppermute | solution.py:188
  300.3 16.5 %collective-permute-start.29 = (bf16[96,768]{1,0:T(8,128)(2,1)S(1)}, bf16[96,768]{1,0:T(8,128)(2,1)S(1)}, u32[]{:S(2)}, u32[]{:S(2)}) collective-permute-start(bf16[96,768]{1,0:T(8,128)(2,1)S(1)} %get-tuple-element.133), channel_id=1, source_target_pairs={{24,0},{25,1},{26,2},{27,3},{28,4},{29,5},{30,6},{31,7}} | collective-permute-start | bytes 442376 | tf_op jit(solution)/shard_map/ppermute | solution.py:188
  302.4 19.5 %collective-permute-start.28 = (bf16[96,768]{1,0:T(8,128)(2,1)S(1)}, bf16[96,768]{1,0:T(8,128)(2,1)S(1)}, u32[]{:S(2)}, u32[]{:S(2)}) collective-permute-start(bf16[96,768]{1,0:T(8,128)(2,1)S(1)} %get-tuple-element.134), channel_id=1, source_target_pairs={{0,24},{1,25},{2,26},{3,27},{4,28},{5,29},{6,30},{7,31}} | collective-permute-start | bytes 442376 | tf_op jit(solution)/shard_map/ppermute | solution.py:188
  308.8 13.2 %collective-permute-start.27 = (bf16[96,768]{1,0:T(8,128)(2,1)S(1)}, bf16[96,768]{1,0:T(8,128)(2,1)S(1)}, u32[]{:S(2)}, u32[]{:S(2)}) collective-permute-start(bf16[96,768]{1,0:T(8,128)(2,1)S(1)} %get-tuple-element.135), channel_id=1, source_target_pairs={{16,0},{17,1},{18,2},{19,3},{20,4},{21,5},{22,6},{23,7},{24,8},{25... | collective-permute-start | bytes 442376 | tf_op jit(solution)/shard_map/ppermute | solution.py:188
  310.1 11.9 %collective-permute-start.26 = (bf16[96,768]{1,0:T(8,128)(2,1)S(1)}, bf16[96,768]{1,0:T(8,128)(2,1)S(1)}, u32[]{:S(2)}, u32[]{:S(2)}) collective-permute-start(bf16[96,768]{1,0:T(8,128)(2,1)S(1)} %get-tuple-element.136), channel_id=1, source_target_pairs={{0,16},{1,17},{2,18},{3,19},{4,20},{5,21},{6,22},{7,23},{8,24},{9,... | collective-permute-start | bytes 442376 | tf_op jit(solution)/shard_map/ppermute | solution.py:188
  315.5 9.6 %collective-permute-start.25 = (bf16[96,768]{1,0:T(8,128)(2,1)S(1)}, bf16[96,768]{1,0:T(8,128)(2,1)S(1)}, u32[]{:S(2)}, u32[]{:S(2)}) collective-permute-start(bf16[96,768]{1,0:T(8,128)(2,1)S(1)} %get-tuple-element.137), channel_id=1, source_target_pairs={{8,0},{9,1},{10,2},{11,3},{12,4},{13,5},{14,6},{15,7},{16,8},{17,9... | collective-permute-start | bytes 442376 | tf_op jit(solution)/shard_map/ppermute | solution.py:188
  316.8 8.3 %collective-permute-start.24 = (bf16[96,768]{1,0:T(8,128)(2,1)S(1)}, bf16[96,768]{1,0:T(8,128)(2,1)S(1)}, u32[]{:S(2)}, u32[]{:S(2)}) collective-permute-start(bf16[96,768]{1,0:T(8,128)(2,1)S(1)} %get-tuple-element.132), channel_id=1, source_target_pairs={{0,8},{1,9},{2,10},{3,11},{4,12},{5,13},{6,14},{7,15},{8,16},{9,17... | collective-permute-start | bytes 442376 | tf_op jit(solution)/shard_map/ppermute | solution.py:188
  (65 other events, 795.6 us)
Sparse Core Ops, SparseCore 0:
  11.5 100.2 all-gather.1
  167.9 157.2 reduce-scatter.1

commit v5 on v4

--- a/solution.py
+++ b/solution.py
@@ -5,6 +5,7 @@
 import numpy as np
 import jax.numpy as jnp
 from jax import lax
+from jax.experimental import pallas as pl
 from jax.sharding import PartitionSpec as P
 
 D = 768
@@ -85,17 +86,57 @@
     return jnp.where(key_valid[None, None, :] > 0, scores, -1e30)
 
 
+def attention_kernel(valid_ref, query_ref, key_ref, value_ref, out_ref, log_total_ref):
+    valid = valid_ref[...] > 0
+    heads_here = out_ref.shape[1] // HDIM
+    outs = []
+    for head in range(heads_here):
+        columns = slice(head * HDIM, (head + 1) * HDIM)
+        scores = lax.dot_general(
+            query_ref[:, columns],
+            key_ref[:, columns],
+            (((1,), (1,)), ((), ())),
+            preferred_element_type=jnp.float32,
+        ) * (1.0 / math.sqrt(HDIM))
+        scores = jnp.where(valid, scores, -1e30)
+        row_max = jnp.max(scores, axis=1, keepdims=True)
+        exponent = jnp.exp(scores - row_max)
+        row_total = jnp.sum(exponent, axis=1, keepdims=True)
+        probability = (exponent / row_total).astype(jnp.bfloat16)
+        attended = jnp.dot(probability, value_ref[:, columns], preferred_element_type=jnp.float32)
+        outs.append(attended.astype(jnp.bfloat16))
+        log_total_ref[0, head : head + 1, :] = (row_max + jnp.log(row_total)).reshape(1, SEQ)
+    out_ref[...] = jnp.concatenate(outs, axis=1)
+
+
 def attend_forward(pieces):
     queries, key_vectors, values, key_valid = pieces
-    scores = masked_scores(queries, key_vectors, key_valid)
-    row_max = jnp.max(scores, axis=-1, keepdims=True)
-    exponent = jnp.exp(scores - row_max)
-    row_total = jnp.sum(exponent, axis=-1, keepdims=True)
-    probability = (exponent / row_total).astype(jnp.bfloat16)
-    attended = jnp.einsum(
-        "hqk,khd->qhd", probability, head_view(values), preferred_element_type=jnp.float32
-    )
-    return (attended.reshape(SEQ, D).astype(jnp.bfloat16), (row_max + jnp.log(row_total))[:, :, 0])
+    groups = HEADS // 2
+    cost = pl.CostEstimate(
+        flops=4 * SEQ * SEQ * D,
+        transcendentals=HEADS * SEQ * SEQ,
+        bytes_accessed=4 * SEQ * D * 2 + HEADS * SEQ * 4,
+    )
+    attended, log_total = pl.pallas_call(
+        attention_kernel,
+        grid=(groups,),
+        in_specs=[
+            pl.BlockSpec((1, SEQ), lambda h: (0, 0)),
+            pl.BlockSpec((SEQ, 2 * HDIM), lambda h: (0, h)),
+            pl.BlockSpec((SEQ, 2 * HDIM), lambda h: (0, h)),
+            pl.BlockSpec((SEQ, 2 * HDIM), lambda h: (0, h)),
+        ],
+        out_specs=[
+            pl.BlockSpec((SEQ, 2 * HDIM), lambda h: (0, h)),
+            pl.BlockSpec((1, 2, SEQ), lambda h: (h, 0, 0)),
+        ],
+        out_shape=[
+            jax.ShapeDtypeStruct((SEQ, D), jnp.bfloat16),
+            jax.ShapeDtypeStruct((groups, 2, SEQ), jnp.float32),
+        ],
+        cost_estimate=cost,
+    )(key_valid.reshape(1, SEQ), queries, key_vectors, values)
+    return attended, log_total.reshape(HEADS, SEQ)
 
 
 def attend_backward(pieces):

time: 341 us -> 365 us (1.070)
  waiting for transfers between devices: 77 us -> 60.2 us
  starting transfers between devices: 88.1 us -> 103 us
  Pallas kernels: 0 us -> 12.9 us
  matrix products: 90.8 us -> 96.2 us
  local copies, waits for them, and re-layouts: 23.3 us -> 27 us
    ppermute x40, waiting for transfers between devices: 76.9 us -> 59.9 us  [permute(): return lax.ppermute(tuple(arrays), ('fsdp', 'dp'), pairs)]
    ppermute x40, starting transfers between devices: 88 us -> 103 us  [permute(): return lax.ppermute(tuple(arrays), ('fsdp', 'dp'), pairs)]
    pallas_call x0 -> x1, Pallas kernels: none -> 12.9 us  [attend_forward(): pl.pallas_call(attention_kernel, grid=(groups,), in_specs=[pl.BlockSpec((...]
    dot_general x6, matrix products: 13.4 us -> 20.3 us  [product(): return jnp.dot(left_side, right_side, preferred_element_type=jnp.float32)]
    dot_general x1, matrix products: 11.5 us -> 7.31 us  [attend_backward(): jnp.einsum('qhd,khd->hqk', grad_heads, head_view(values), preferred_eleme...]
    convert_element_type x0 -> x3, local copies, waits for them, and re-layouts: none -> 3.98 us  [the longest x1 2.29 us: on_device(): (product(tokens, attention_full[2 * D:3 * D]) + value_bias).astype(jnp.bf...]
    unnamed x119 -> x143, local copies, waits for them, and re-layouts: 10.9 us -> 8.43 us
  transfers between devices with their start and end apart: 42 -> 42, of which waited for: 13 -> 16; matrix products, arithmetic and copies ran while one was open for 28% -> 30% of each run, Pallas kernels for 0% -> 4%
where the time goes in v5:
time: 365 us; the launch traced here: 358 us
  starting transfers between devices  103 us (28%)
  matrix products  96.2 us (26%)
  waiting for transfers between devices  60.2 us (16%)
  other arithmetic  40.1 us (11%)
  local copies, waits for them, and re-layouts  27 us (7%)
  between operations  18 us (5%)
  Pallas kernels  12.9 us (4%)
    ppermute x40, starting transfers between devices, permute(): return lax.ppermute(tuple(arrays), ('fsdp', 'dp'), pairs)  103 us
    ppermute x40, waiting for transfers between devices, permute(): return lax.ppermute(tuple(arrays), ('fsdp', 'dp'), pairs)  59.9 us
    dot_general x6, matrix products, product_cols(): lax.dot_general(left_side, right_side, (((1,), (1,)), ((), ())), preferre...  36.3 us
    dot_general x6, matrix products, product(): return jnp.dot(left_side, right_side, preferred_element_type=jnp.float32)  20.3 us
    pallas_call x1, Pallas kernels, attend_forward(): pl.pallas_call(attention_kernel, grid=(groups,), in_specs=[pl.BlockSpec((...  12.9 us
    dot_general x1, matrix products, on_device(): lax.dot_general(jnp.stack([inner_grad, active]), jnp.stack([normed_low, f...  9.11 us
    dot_general x1, matrix products, attend_backward(): jnp.einsum('hqk,qhd->khd', probability_low, grad_heads, preferred_element...  8.97 us
    unnamed x143, local copies, waits for them, and re-layouts  8.43 us
  transfers between devices with their start and end apart: 42, of which 16 were waited for; matrix products, arithmetic and copies ran while one was open for 30% of the time, Pallas kernels for 4%

profile of v5, /device:TPU:0, one launch (start us, length us, event | category | flops | bytes accessed | tf_op | source)
XLA Modules:
  0.0 357.8 jit_solution(11367168289293098295)
XLA Ops:
  11.4 7.0 %collective-permute-start.1 = (bf16[96,768]{1,0:T(8,128)(2,1)S(1)}, bf16[96,768]{1,0:T(8,128)(2,1)S(1)}, u32[]{:S(2)}, u32[]{:S(2)}) collective-permute-start(bf16[96,768]{1,0:T(8,128)(2,1)S(1)} %convert_element_type.384), channel_id=1, source_target_pairs={{0,24},{1,25},{2,26},{3,27},{4,28},{5,29},{6,30},{7,31}} | collective-permute-start | bytes 442376 | tf_op jit(solution)/shard_map/ppermute | solution.py:229
  19.7 5.5 %collective-permute-start.3 = (bf16[96,768]{1,0:T(8,128)(2,1)S(1)}, bf16[96,768]{1,0:T(8,128)(2,1)S(1)}, u32[]{:S(2)}, u32[]{:S(2)}) collective-permute-start(bf16[96,768]{1,0:T(8,128)(2,1)S(1)} %convert_element_type.384), channel_id=1, source_target_pairs={{0,16},{1,17},{2,18},{3,19},{4,20},{5,21},{6,22},{7,23},{8,24},{9,... | collective-permute-start | bytes 442376 | tf_op jit(solution)/shard_map/ppermute | solution.py:229
  26.6 4.6 %collective-permute-start.5 = (bf16[96,768]{1,0:T(8,128)(2,1)S(1)}, bf16[96,768]{1,0:T(8,128)(2,1)S(1)}, u32[]{:S(2)}, u32[]{:S(2)}) collective-permute-start(bf16[96,768]{1,0:T(8,128)(2,1)S(1)} %convert_element_type.384), channel_id=1, source_target_pairs={{0,8},{1,9},{2,10},{3,11},{4,12},{5,13},{6,14},{7,15},{8,16},{9,17... | collective-permute-start | bytes 442376 | tf_op jit(solution)/shard_map/ppermute | solution.py:229
  31.8 2.6 collective-permute-done.4
  42.6 7.5 %collective-permute-start.11 = (bf16[1,768]{1,0:T(2,128)(2,1)}, bf16[1,768]{1,0:T(2,128)(2,1)}, u32[]{:S(2)}, u32[]{:S(2)}) collective-permute-start(bf16[1,768]{1,0:T(2,128)(2,1)} %get-tuple-element.159), channel_id=1, source_target_pairs={{0,24},{1,25},{2,26},{3,27},{4,28},{5,29},{6,30},{7,31}} | collective-permute-start | bytes 4616 | tf_op jit(solution)/shard_map/ppermute | solution.py:229
  51.4 4.8 %collective-permute-done.6 = bf16[4,96,768]{2,1,0:T(8,128)(2,1)S(1)} collective-permute-done((bf16[4,96,768]{2,1,0:T(8,128)(2,1)S(1)}, bf16[4,96,768]{2,1,0:T(8,128)(2,1)S(1)}, u32[]{:S(2)}, u32[]{:S(2)}) %collective-permute-start.6) | collective-permute-done | bytes 589856 | tf_op jit(solution)/shard_map/ppermute | solution.py:229
  57.5 4.2 %collective-permute-done.7 = bf16[4,96,768]{2,1,0:T(8,128)(2,1)S(1)} collective-permute-done((bf16[4,96,768]{2,1,0:T(8,128)(2,1)S(1)}, bf16[4,96,768]{2,1,0:T(8,128)(2,1)S(1)}, u32[]{:S(2)}, u32[]{:S(2)}) %collective-permute-start.7) | collective-permute-done | bytes 589856 | tf_op jit(solution)/shard_map/ppermute | solution.py:229
  61.7 8.5 %collective-permute-start.13 = (bf16[1,768]{1,0:T(2,128)(2,1)}, bf16[1,768]{1,0:T(2,128)(2,1)}, u32[]{:S(2)}, u32[]{:S(2)}) collective-permute-start(bf16[1,768]{1,0:T(2,128)(2,1)} %get-tuple-element.159), channel_id=1, source_target_pairs={{0,16},{1,17},{2,18},{3,19},{4,20},{5,21},{6,22},{7,23},{8,24},{9,... | collective-permute-start | bytes 4616 | tf_op jit(solution)/shard_map/ppermute | solution.py:229
  70.3 3.0 collective-permute-done.8
  78.9 6.8 %collective-permute-start.15 = (bf16[1,768]{1,0:T(2,128)(2,1)}, bf16[1,768]{1,0:T(2,128)(2,1)S(1)}, u32[]{:S(2)}, u32[]{:S(2)}) collective-permute-start(bf16[1,768]{1,0:T(2,128)(2,1)} %get-tuple-element.159), channel_id=1, source_target_pairs={{0,8},{1,9},{2,10},{3,11},{4,12},{5,13},{6,14},{7,15},{8,16},{9,17... | collective-permute-start | bytes 4616 | tf_op jit(solution)/shard_map/ppermute | solution.py:229
  107.4 2.9 fusion.31.query_ref
  116.4 12.9 %eval_jaxpr.2 = (bf16[512,768]{1,0:T(8,128)(2,1)}, f32[6,2,512]{2,1,0:T(2,128)}) custom-call(f32[1,512]{1,0:T(1,128)} %compare_convert_fusion.valid_ref, bf16[512,768]{1,0:T(8,128)(2,1)} %fusion.31.query_ref, bf16[512,768]{1,0:T(8,128)(2,1)} %copy-done.23, bf16[512,768]{1,0:T(8,128)(2,1)} %fusion.32.value_ref), custom_call_target="tpu_custom_call" | custom-call | flops 805306368 | bytes 3170304 | tf_op jit(solution)/shard_map/while/body/eval_jaxpr/pallas_call | solution.py:120
  130.1 3.7 %fusion.143 = (f32[512]{0:T(512)S(1)}, f32[512,768]{1,0:T(8,128)S(1)}, f32[512,768]{1,0:T(8,128)}) fusion(bf16[512,768]{1,0:T(8,128)(2,1)} %param.15, f32[768]{0:T(1024)S(1)} %get-tuple-element.156, bf16[512,768]{1,0:T(8,128)(2,1)} %get-tuple-element.82, bf16[768,768]{1,0:T(8,128)(2,1)} %bitcast.299), kind=kOutput, calls=%fused_computation.298 | convolution fusion | flops 605552128 | bytes 5903360 | tf_op jit(solution)/shard_map/dot_general | solution.py:28
  134.1 6.4 %fusion.149 = f32[12,512,512]{1,2,0:T(8,128)} fusion(bf16[512,12,64]{0,2,1:T(8,128)(2,1)S(1)} %bitcast.295, bf16[512,12,64]{0,2,1:T(8,128)(2,1)S(1)} %bitcast.292), kind=kOutput, calls=%fused_computation.302 | convolution fusion | flops 402653184 | bytes 14155776 | tf_op jit(solution)/shard_map/while/body/eval_jaxpr/qhd,khd->hqk/dot_general | solution.py:80
  140.6 20.4 %multiply_convert_fusion.2 = (bf16[512,3072]{1,0:T(8,128)(2,1)S(1)}, f32[512,3072]{1,0:T(8,128)}, f32[512,3072]{1,0:T(8,128)}) fusion(f32[3072]{0:T(1024)S(1)} %copy-done.34, bf16[6144,768]{1,0:T(8,128)(2,1)} %all-gather.2.cloned.1.call-done, f32[512,768]{1,0:T(8,128)S(1)} %get-tuple-element.122, f32[768]{0:T(1024)S(1)} %copy-done.54, ...), kind=kOutput, calls=%fused_computation.11 | convolution fusion | flops 2521694208 | bytes 22042624 | tf_op jit(solution)/shard_map/dot_general | solution.py:38
  161.0 3.7 %fusion.141 = (f32[512]{0:T(512)S(1)}, f32[512,768]{1,0:T(8,128)S(1)}, bf16[1,512,768]{2,1,0:T(8,128)(2,1)S(1)}, f32[]{:T(128)}, f32[]{:T(128)}) fusion(f32[768]{0:T(1024)S(1)} %copy-done.53, f32[768]{0:T(1024)S(1)} %copy-done.54, f32[768]{0:T(1024)S(1)} %get-tuple-element.155, f32[512]{0:T(512)S(1)} %fusion.75, f32[512,768]{1,0:T(8,128)S(1)} %get-tuple-element.122, ...), kind=kOutput, calls=%fused_computation.297 | convolution fusion | flops 2421423616 | bytes 13389832 | tf_op jit(solution)/shard_map/dot_general | solution.py:28
  169.5 8.7 %fusion.146 = (bf16[3072]{0:T(1024)(128)(2,1)}, bf16[512,3072]{1,0:T(8,128)(2,1)}) fusion(f32[512,3072]{1,0:T(8,128)} %get-tuple-element.166, f32[3072]{0:T(1024)S(1)} %copy-done.34, f32[512,3072]{1,0:T(8,128)} %get-tuple-element.120, bf16[512,768]{1,0:T(8,128)(2,1)S(1)} %get-tuple-element.102, bf16[6144,768]{1,0:T(8,128)(2,1)S(1)} %copy-done.63), kind=kOutput, calls=%fused_computation.301 | convolution fusion | flops 2434790400 | bytes 21252096 | tf_op jit(solution)/shard_map/dot_general | solution.py:38
  178.3 9.1 %convolution_convert_fusion = bf16[2,3072,768]{2,1,0:T(8,128)(2,1)} fusion(bf16[1,512,3072]{2,1,0:T(8,128)(2,1)S(1)} %bitcast.321, bf16[1,512,3072]{2,1,0:T(8,128)(2,1)} %bitcast.322, bf16[1,512,768]{2,1,0:T(8,128)(2,1)S(1)} %bitcast.315, bf16[1,512,768]{2,1,0:T(8,128)(2,1)S(1)} %get-tuple-element.132), kind=kOutput, calls=%fused_computation.4 | convolution fusion | flops 4840488960 | bytes 17301504 | tf_op jit(solution)/shard_map/dot_general | solution.py:449
  187.4 6.9 %multiply_reduce_fusion.5 = (bf16[768]{0:T(1024)(128)(2,1)}, f32[512]{0:T(512)S(1)}, bf16[768]{0:T(1024)(128)(2,1)}, f32[512,768]{1,0:T(8,128)S(1)}) fusion(f32[512,768]{1,0:T(8,128)S(1)} %get-tuple-element.122, f32[512]{0:T(512)S(1)} %fusion.75, f32[512]{0:T(512)S(1)} %broadcast_multiply_fusion.1, f32[768]{0:T(1024)S(1)} %get-tuple-element.155, ...), kind=kOutput, calls=%fused_computation.50 | convolution fusion | flops 2419849216 | bytes 12597248 | tf_op jit(solution)/shard_map/dot_general | solution.py:28
  201.9 9.0 %bitcast_reduce_fusion = (bf16[12,64]{1,0:T(8,128)(2,1)}, bf16[12,64,512]{2,1,0:T(8,128)(2,1)S(1)}) fusion(bf16[512,12,64]{0,2,1:T(8,128)(2,1)S(1)} %bitcast.302, f32[12,512,512]{1,2,0:T(8,128)} %fusion.149, f32[12,512]{1,0:T(8,128)S(1)} %sub.134, pred[512]{0:T(512)(128)(4,1)S(1)} %copy-done.56), kind=kOutput, calls=%fused_computation.92 | convolution fusion | flops 416021760 | bytes 14182400 | tf_op jit(solution)/shard_map/while/body/eval_jaxpr/hqk,qhd->khd/dot_general | solution.py:148
  212.4 7.3 %multiply_reduce_fusion = (f32[12,512]{1,0:T(8,128)S(1)}, f32[12,512,512]{1,2,0:T(8,128)}) fusion(f32[12,512,512]{1,2,0:T(8,128)S(1)} %bitcast.290, f32[12,512]{1,0:T(8,128)S(1)} %copy-done.33, pred[512]{0:T(512)(128)(4,1)S(1)} %copy-done.56, bf16[512,12,64]{0,2,1:T(8,128)(2,1)S(1)} %bitcast.303, bf16[512,12,64]{0,2,1:T(8,128)(2,1)S(1)} %bitcast.301), kind=kOutput, calls=%fused_computation.1 | convolution fusion | flops 418375680 | bytes 26788352 | tf_op jit(solution)/shard_map/while/body/eval_jaxpr/qhd,khd->hqk/dot_general | solution.py:151
  219.7 7.8 %multiply_convert_fusion = bf16[12,512,512]{1,2,0:T(8,128)(2,1)S(1)} fusion(f32[12,512,512]{1,2,0:T(8,128)} %get-tuple-element.169, f32[12,512,512]{1,2,0:T(8,128)S(1)} %bitcast.290, f32[12,512]{1,0:T(8,128)S(1)} %get-tuple-element.168, f32[12,512]{1,0:T(8,128)S(1)} %copy-done.33, pred[512]{0:T(512)(128)(4,1)S(1)} %copy-done.56), kind=kLoop, calls=%fused_computation | loop fusion | flops 18874368 | bytes 31506944 | tf_op jit(solution)/shard_map/while/body/eval_jaxpr/convert_element_type | solution.py:155
  240.7 2.7 fusion.131
  249.5 2.5 collective-permute-start.33
  255.9 4.3 %collective-permute-start.34 = (bf16[16,768]{1,0:T(8,128)(2,1)S(1)}, bf16[16,768]{1,0:T(8,128)(2,1)S(1)}, u32[]{:S(2)}, u32[]{:S(2)}) collective-permute-start(bf16[16,768]{1,0:T(8,128)(2,1)S(1)} %get-tuple-element.145), channel_id=1, source_target_pairs={{0,8},{1,9},{2,10},{3,11},{4,12},{5,13},{6,14},{7,15},{8,16},{9,17... | collective-permute-start | bytes 73736 | tf_op jit(solution)/shard_map/ppermute | solution.py:229
  261.5 6.0 %collective-permute-start.36 = (bf16[16,768]{1,0:T(8,128)(2,1)S(1)}, bf16[16,768]{1,0:T(8,128)(2,1)S(1)}, u32[]{:S(2)}, u32[]{:S(2)}) collective-permute-start(bf16[16,768]{1,0:T(8,128)(2,1)S(1)} %get-tuple-element.149), channel_id=1, source_target_pairs={{0,16},{1,17},{2,18},{3,19},{4,20},{5,21},{6,22},{7,23},{8,24},{9,... | collective-permute-start | bytes 73736 | tf_op jit(solution)/shard_map/ppermute | solution.py:229
  268.8 6.2 %collective-permute-start.38 = (bf16[16,768]{1,0:T(8,128)(2,1)S(1)}, bf16[16,768]{1,0:T(8,128)(2,1)S(1)}, u32[]{:S(2)}, u32[]{:S(2)}) collective-permute-start(bf16[16,768]{1,0:T(8,128)(2,1)S(1)} %get-tuple-element.147), channel_id=1, source_target_pairs={{0,24},{1,25},{2,26},{3,27},{4,28},{5,29},{6,30},{7,31}} | collective-permute-start | bytes 73736 | tf_op jit(solution)/shard_map/ppermute | solution.py:229
  288.4 12.6 %collective-permute-done.21 = bf16[4,96,768]{2,1,0:T(8,128)(2,1)S(1)} collective-permute-done((bf16[4,96,768]{2,1,0:T(8,128)(2,1)}, bf16[4,96,768]{2,1,0:T(8,128)(2,1)S(1)}, u32[]{:S(2)}, u32[]{:S(2)}) %collective-permute-start.21) | collective-permute-done | bytes 589856 | tf_op jit(solution)/shard_map/ppermute | solution.py:229
  301.0 14.1 %collective-permute-done.22 = bf16[4,96,768]{2,1,0:T(8,128)(2,1)S(1)} collective-permute-done((bf16[4,96,768]{2,1,0:T(8,128)(2,1)}, bf16[4,96,768]{2,1,0:T(8,128)(2,1)S(1)}, u32[]{:S(2)}, u32[]{:S(2)}) %collective-permute-start.22) | collective-permute-done | bytes 589856 | tf_op jit(solution)/shard_map/ppermute | solution.py:229
  320.1 7.9 %collective-permute-start.26 = (bf16[96,768]{1,0:T(8,128)(2,1)S(1)}, bf16[96,768]{1,0:T(8,128)(2,1)S(1)}, u32[]{:S(2)}, u32[]{:S(2)}) collective-permute-start(bf16[96,768]{1,0:T(8,128)(2,1)S(1)} %get-tuple-element.140), channel_id=1, source_target_pairs={{0,16},{1,17},{2,18},{3,19},{4,20},{5,21},{6,22},{7,23},{8,24},{9,... | collective-permute-start | bytes 442376 | tf_op jit(solution)/shard_map/ppermute | solution.py:229
  329.3 6.9 %collective-permute-start.28 = (bf16[96,768]{1,0:T(8,128)(2,1)S(1)}, bf16[96,768]{1,0:T(8,128)(2,1)S(1)}, u32[]{:S(2)}, u32[]{:S(2)}) collective-permute-start(bf16[96,768]{1,0:T(8,128)(2,1)S(1)} %get-tuple-element.138), channel_id=1, source_target_pairs={{0,24},{1,25},{2,26},{3,27},{4,28},{5,29},{6,30},{7,31}} | collective-permute-start | bytes 442376 | tf_op jit(solution)/shard_map/ppermute | solution.py:229
  338.1 8.3 %collective-permute-done.27 = bf16[96,768]{1,0:T(8,128)(2,1)S(1)} collective-permute-done((bf16[96,768]{1,0:T(8,128)(2,1)S(1)}, bf16[96,768]{1,0:T(8,128)(2,1)S(1)}, u32[]{:S(2)}, u32[]{:S(2)}) %collective-permute-start.27) | collective-permute-done | bytes 147488 | tf_op jit(solution)/shard_map/ppermute | solution.py:229
  (317 shorter events, 115.1 us)
Async XLA Ops:
  7.2 133.4 %all-gather.2.cloned.1.call-start = ((), (), s32[]{:S(2)}) async-start(), calls=%async_computation.1 | async-start | bytes 9732096 | tf_op jit(solution)/shard_map/all_gather | solution.py:309
  9.1 338.8 %reduce-scatter.2.cloned.1.call-start = ((), (), s32[]{:S(2)}) async-start(), calls=%async_computation.2 | async-start | bytes 9732096 | tf_op jit(solution)/shard_map/reduce_scatter | solution.py:318
  10.1 16.4 %collective-permute-start = (bf16[96,768]{1,0:T(8,128)(2,1)S(1)}, bf16[96,768]{1,0:T(8,128)(2,1)S(1)}, u32[]{:S(2)}, u32[]{:S(2)}) collective-permute-start(bf16[96,768]{1,0:T(8,128)(2,1)S(1)} %convert_element_type.384), channel_id=1, source_target_pairs={{24,0},{25,1},{26,2},{27,3},{28,4},{29,5},{30,6},{31,7}} | collective-permute-start | bytes 442376 | tf_op jit(solution)/shard_map/ppermute | solution.py:229
  11.4 20.4 %collective-permute-start.1 = (bf16[96,768]{1,0:T(8,128)(2,1)S(1)}, bf16[96,768]{1,0:T(8,128)(2,1)S(1)}, u32[]{:S(2)}, u32[]{:S(2)}) collective-permute-start(bf16[96,768]{1,0:T(8,128)(2,1)S(1)} %convert_element_type.384), channel_id=1, source_target_pairs={{0,24},{1,25},{2,26},{3,27},{4,28},{5,29},{6,30},{7,31}} | collective-permute-start | bytes 442376 | tf_op jit(solution)/shard_map/ppermute | solution.py:229
  18.4 13.4 %collective-permute-start.2 = (bf16[96,768]{1,0:T(8,128)(2,1)S(1)}, bf16[96,768]{1,0:T(8,128)(2,1)S(1)}, u32[]{:S(2)}, u32[]{:S(2)}) collective-permute-start(bf16[96,768]{1,0:T(8,128)(2,1)S(1)} %convert_element_type.384), channel_id=1, source_target_pairs={{16,0},{17,1},{18,2},{19,3},{20,4},{21,5},{22,6},{23,7},{24,8},{25... | collective-permute-start | bytes 442376 | tf_op jit(solution)/shard_map/ppermute | solution.py:229
  19.7 12.1 %collective-permute-start.3 = (bf16[96,768]{1,0:T(8,128)(2,1)S(1)}, bf16[96,768]{1,0:T(8,128)(2,1)S(1)}, u32[]{:S(2)}, u32[]{:S(2)}) collective-permute-start(bf16[96,768]{1,0:T(8,128)(2,1)S(1)} %convert_element_type.384), channel_id=1, source_target_pairs={{0,16},{1,17},{2,18},{3,19},{4,20},{5,21},{6,22},{7,23},{8,24},{9,... | collective-permute-start | bytes 442376 | tf_op jit(solution)/shard_map/ppermute | solution.py:229
  26.6 9.6 %collective-permute-start.5 = (bf16[96,768]{1,0:T(8,128)(2,1)S(1)}, bf16[96,768]{1,0:T(8,128)(2,1)S(1)}, u32[]{:S(2)}, u32[]{:S(2)}) collective-permute-start(bf16[96,768]{1,0:T(8,128)(2,1)S(1)} %convert_element_type.384), channel_id=1, source_target_pairs={{0,8},{1,9},{2,10},{3,11},{4,12},{5,13},{6,14},{7,15},{8,16},{9,17... | collective-permute-start | bytes 442376 | tf_op jit(solution)/shard_map/ppermute | solution.py:229
  36.5 19.7 %collective-permute-start.6 = (bf16[4,96,768]{2,1,0:T(8,128)(2,1)S(1)}, bf16[4,96,768]{2,1,0:T(8,128)(2,1)S(1)}, u32[]{:S(2)}, u32[]{:S(2)}) collective-permute-start(bf16[4,96,768]{2,1,0:T(8,128)(2,1)S(1)} %select_select_fusion), channel_id=1, source_target_pairs={{0,1},{1,0},{2,3},{3,2},{4,5},{5,4},{6,7},{7,6},{8,9},{9,8},{10,11... | collective-permute-start | bytes 1769480 | tf_op jit(solution)/shard_map/ppermute | solution.py:229
  38.2 23.5 %collective-permute-start.7 = (bf16[4,96,768]{2,1,0:T(8,128)(2,1)S(1)}, bf16[4,96,768]{2,1,0:T(8,128)(2,1)S(1)}, u32[]{:S(2)}, u32[]{:S(2)}) collective-permute-start(bf16[4,96,768]{2,1,0:T(8,128)(2,1)S(1)} %select_select_fusion), channel_id=1, source_target_pairs={{0,4},{1,5},{2,6},{3,7},{4,0},{5,1},{6,2},{7,3},{8,12},{9,13},{10,... | collective-permute-start | bytes 1769480 | tf_op jit(solution)/shard_map/ppermute | solution.py:229
  39.7 33.5 %collective-permute-start.8 = (bf16[4,96,768]{2,1,0:T(8,128)(2,1)S(1)}, bf16[4,96,768]{2,1,0:T(8,128)(2,1)}, u32[]{:S(2)}, u32[]{:S(2)}) collective-permute-start(bf16[4,96,768]{2,1,0:T(8,128)(2,1)S(1)} %select_select_fusion), channel_id=1, source_target_pairs={{0,5},{1,4},{2,7},{3,6},{4,1},{5,0},{6,3},{7,2},{8,13},{9,12},{10,... | collective-permute-start | bytes 1769480 | tf_op jit(solution)/shard_map/ppermute | solution.py:229
  41.3 36.3 %collective-permute-start.10 = (bf16[1,768]{1,0:T(2,128)(2,1)}, bf16[1,768]{1,0:T(2,128)(2,1)}, u32[]{:S(2)}, u32[]{:S(2)}) collective-permute-start(bf16[1,768]{1,0:T(2,128)(2,1)} %get-tuple-element.159), channel_id=1, source_target_pairs={{24,0},{25,1},{26,2},{27,3},{28,4},{29,5},{30,6},{31,7}} | collective-permute-start | bytes 4616 | tf_op jit(solution)/shard_map/ppermute | solution.py:229
  42.6 36.3 %collective-permute-start.11 = (bf16[1,768]{1,0:T(2,128)(2,1)}, bf16[1,768]{1,0:T(2,128)(2,1)}, u32[]{:S(2)}, u32[]{:S(2)}) collective-permute-start(bf16[1,768]{1,0:T(2,128)(2,1)} %get-tuple-element.159), channel_id=1, source_target_pairs={{0,24},{1,25},{2,26},{3,27},{4,28},{5,29},{6,30},{7,31}} | collective-permute-start | bytes 4616 | tf_op jit(solution)/shard_map/ppermute | solution.py:229
  56.2 30.9 %collective-permute-start.12 = (bf16[1,768]{1,0:T(2,128)(2,1)}, bf16[1,768]{1,0:T(2,128)(2,1)}, u32[]{:S(2)}, u32[]{:S(2)}) collective-permute-start(bf16[1,768]{1,0:T(2,128)(2,1)} %get-tuple-element.159), channel_id=1, source_target_pairs={{16,0},{17,1},{18,2},{19,3},{20,4},{21,5},{22,6},{23,7},{24,8},{25... | collective-permute-start | bytes 4616 | tf_op jit(solution)/shard_map/ppermute | solution.py:229
  61.7 26.1 %collective-permute-start.13 = (bf16[1,768]{1,0:T(2,128)(2,1)}, bf16[1,768]{1,0:T(2,128)(2,1)}, u32[]{:S(2)}, u32[]{:S(2)}) collective-permute-start(bf16[1,768]{1,0:T(2,128)(2,1)} %get-tuple-element.159), channel_id=1, source_target_pairs={{0,16},{1,17},{2,18},{3,19},{4,20},{5,21},{6,22},{7,23},{8,24},{9,... | collective-permute-start | bytes 4616 | tf_op jit(solution)/shard_map/ppermute | solution.py:229
  76.5 24.4 %collective-permute-start.9 = (bf16[4,2,2,96,768]{4,3,2,1,0:T(8,128)(2,1)}, bf16[4,2,2,96,768]{4,3,2,1,0:T(8,128)(2,1)}, u32[]{:S(2)}, u32[]{:S(2)}) collective-permute-start(bf16[4,2,2,96,768]{4,3,2,1,0:T(8,128)(2,1)} %broadcast_select_fusion), channel_id=1, source_target_pairs={{0,2},{1,3},{2,0},{3,1},{4,6},{5,7},{6,4},{7,5},{8,10},{9,11},{10,... | collective-permute-start | bytes 7077896 | tf_op jit(solution)/shard_map/ppermute | solution.py:229
  77.6 11.0 %collective-permute-start.14 = (bf16[1,768]{1,0:T(2,128)(2,1)}, bf16[1,768]{1,0:T(2,128)(2,1)S(1)}, u32[]{:S(2)}, u32[]{:S(2)}) collective-permute-start(bf16[1,768]{1,0:T(2,128)(2,1)} %get-tuple-element.159), channel_id=1, source_target_pairs={{8,0},{9,1},{10,2},{11,3},{12,4},{13,5},{14,6},{15,7},{16,8},{17,9... | collective-permute-start | bytes 4616 | tf_op jit(solution)/shard_map/ppermute | solution.py:229
  78.9 9.7 %collective-permute-start.15 = (bf16[1,768]{1,0:T(2,128)(2,1)}, bf16[1,768]{1,0:T(2,128)(2,1)S(1)}, u32[]{:S(2)}, u32[]{:S(2)}) collective-permute-start(bf16[1,768]{1,0:T(2,128)(2,1)} %get-tuple-element.159), channel_id=1, source_target_pairs={{0,8},{1,9},{2,10},{3,11},{4,12},{5,13},{6,14},{7,15},{8,16},{9,17... | collective-permute-start | bytes 4616 | tf_op jit(solution)/shard_map/ppermute | solution.py:229
  237.7 31.1 %collective-permute-start.20 = (bf16[4,2,2,96,768]{4,3,0,2,1:T(8,128)(2,1)}, bf16[4,2,2,96,768]{4,3,0,2,1:T(8,128)(2,1)}, u32[]{:S(2)}, u32[]{:S(2)}) collective-permute-start(bf16[4,2,2,96,768]{4,3,0,2,1:T(8,128)(2,1)} %bitcast.284), channel_id=1, source_target_pairs={{0,2},{1,3},{2,0},{3,1},{4,6},{5,7},{6,4},{7,5},{8,10},{9,11},{10,... | collective-permute-start | bytes 7077896 | tf_op jit(solution)/shard_map/ppermute | solution.py:229
  255.9 22.6 %collective-permute-start.34 = (bf16[16,768]{1,0:T(8,128)(2,1)S(1)}, bf16[16,768]{1,0:T(8,128)(2,1)S(1)}, u32[]{:S(2)}, u32[]{:S(2)}) collective-permute-start(bf16[16,768]{1,0:T(8,128)(2,1)S(1)} %get-tuple-element.145), channel_id=1, source_target_pairs={{0,8},{1,9},{2,10},{3,11},{4,12},{5,13},{6,14},{7,15},{8,16},{9,17... | collective-permute-start | bytes 73736 | tf_op jit(solution)/shard_map/ppermute | solution.py:229
  260.2 20.1 %collective-permute-start.35 = (bf16[16,768]{1,0:T(8,128)(2,1)S(1)}, bf16[16,768]{1,0:T(8,128)(2,1)S(1)}, u32[]{:S(2)}, u32[]{:S(2)}) collective-permute-start(bf16[16,768]{1,0:T(8,128)(2,1)S(1)} %get-tuple-element.150), channel_id=1, source_target_pairs={{8,0},{9,1},{10,2},{11,3},{12,4},{13,5},{14,6},{15,7},{16,8},{17,9... | collective-permute-start | bytes 73736 | tf_op jit(solution)/shard_map/ppermute | solution.py:229
  261.5 20.4 %collective-permute-start.36 = (bf16[16,768]{1,0:T(8,128)(2,1)S(1)}, bf16[16,768]{1,0:T(8,128)(2,1)S(1)}, u32[]{:S(2)}, u32[]{:S(2)}) collective-permute-start(bf16[16,768]{1,0:T(8,128)(2,1)S(1)} %get-tuple-element.149), channel_id=1, source_target_pairs={{0,16},{1,17},{2,18},{3,19},{4,20},{5,21},{6,22},{7,23},{8,24},{9,... | collective-permute-start | bytes 73736 | tf_op jit(solution)/shard_map/ppermute | solution.py:229
  267.5 15.2 %collective-permute-start.37 = (bf16[16,768]{1,0:T(8,128)(2,1)S(1)}, bf16[16,768]{1,0:T(8,128)(2,1)S(1)}, u32[]{:S(2)}, u32[]{:S(2)}) collective-permute-start(bf16[16,768]{1,0:T(8,128)(2,1)S(1)} %get-tuple-element.148), channel_id=1, source_target_pairs={{16,0},{17,1},{18,2},{19,3},{20,4},{21,5},{22,6},{23,7},{24,8},{25... | collective-permute-start | bytes 73736 | tf_op jit(solution)/shard_map/ppermute | solution.py:229
  268.8 17.2 %collective-permute-start.38 = (bf16[16,768]{1,0:T(8,128)(2,1)S(1)}, bf16[16,768]{1,0:T(8,128)(2,1)S(1)}, u32[]{:S(2)}, u32[]{:S(2)}) collective-permute-start(bf16[16,768]{1,0:T(8,128)(2,1)S(1)} %get-tuple-element.147), channel_id=1, source_target_pairs={{0,24},{1,25},{2,26},{3,27},{4,28},{5,29},{6,30},{7,31}} | collective-permute-start | bytes 73736 | tf_op jit(solution)/shard_map/ppermute | solution.py:229
  280.3 20.7 %collective-permute-start.21 = (bf16[4,96,768]{2,1,0:T(8,128)(2,1)}, bf16[4,96,768]{2,1,0:T(8,128)(2,1)S(1)}, u32[]{:S(2)}, u32[]{:S(2)}) collective-permute-start(bf16[4,96,768]{2,1,0:T(8,128)(2,1)} %get-tuple-element.123), channel_id=1, source_target_pairs={{0,4},{1,5},{2,6},{3,7},{4,0},{5,1},{6,2},{7,3},{8,12},{9,13},{10,... | collective-permute-start | bytes 1769480 | tf_op jit(solution)/shard_map/ppermute | solution.py:229
  281.9 33.2 %collective-permute-start.22 = (bf16[4,96,768]{2,1,0:T(8,128)(2,1)}, bf16[4,96,768]{2,1,0:T(8,128)(2,1)S(1)}, u32[]{:S(2)}, u32[]{:S(2)}) collective-permute-start(bf16[4,96,768]{2,1,0:T(8,128)(2,1)} %get-tuple-element.125), channel_id=1, source_target_pairs={{0,1},{1,0},{2,3},{3,2},{4,5},{5,4},{6,7},{7,6},{8,9},{9,8},{10,11... | collective-permute-start | bytes 1769480 | tf_op jit(solution)/shard_map/ppermute | solution.py:229
  282.7 32.4 %collective-permute-start.23 = (bf16[4,96,768]{2,1,0:T(8,128)(2,1)}, bf16[4,96,768]{2,1,0:T(8,128)(2,1)S(1)}, u32[]{:S(2)}, u32[]{:S(2)}) collective-permute-start(bf16[4,96,768]{2,1,0:T(8,128)(2,1)} %get-tuple-element.124), channel_id=1, source_target_pairs={{0,5},{1,4},{2,7},{3,6},{4,1},{5,0},{6,3},{7,2},{8,13},{9,12},{10,... | collective-permute-start | bytes 1769480 | tf_op jit(solution)/shard_map/ppermute | solution.py:229
  316.8 19.5 %collective-permute-start.24 = (bf16[96,768]{1,0:T(8,128)(2,1)S(1)}, bf16[96,768]{1,0:T(8,128)(2,1)S(1)}, u32[]{:S(2)}, u32[]{:S(2)}) collective-permute-start(bf16[96,768]{1,0:T(8,128)(2,1)S(1)} %get-tuple-element.136), channel_id=1, source_target_pairs={{0,8},{1,9},{2,10},{3,11},{4,12},{5,13},{6,14},{7,15},{8,16},{9,17... | collective-permute-start | bytes 442376 | tf_op jit(solution)/shard_map/ppermute | solution.py:229
  318.9 19.2 %collective-permute-start.25 = (bf16[96,768]{1,0:T(8,128)(2,1)S(1)}, bf16[96,768]{1,0:T(8,128)(2,1)S(1)}, u32[]{:S(2)}, u32[]{:S(2)}) collective-permute-start(bf16[96,768]{1,0:T(8,128)(2,1)S(1)} %get-tuple-element.141), channel_id=1, source_target_pairs={{8,0},{9,1},{10,2},{11,3},{12,4},{13,5},{14,6},{15,7},{16,8},{17,9... | collective-permute-start | bytes 442376 | tf_op jit(solution)/shard_map/ppermute | solution.py:229
  320.1 17.9 %collective-permute-start.26 = (bf16[96,768]{1,0:T(8,128)(2,1)S(1)}, bf16[96,768]{1,0:T(8,128)(2,1)S(1)}, u32[]{:S(2)}, u32[]{:S(2)}) collective-permute-start(bf16[96,768]{1,0:T(8,128)(2,1)S(1)} %get-tuple-element.140), channel_id=1, source_target_pairs={{0,16},{1,17},{2,18},{3,19},{4,20},{5,21},{6,22},{7,23},{8,24},{9,... | collective-permute-start | bytes 442376 | tf_op jit(solution)/shard_map/ppermute | solution.py:229
  328.0 18.4 %collective-permute-start.27 = (bf16[96,768]{1,0:T(8,128)(2,1)S(1)}, bf16[96,768]{1,0:T(8,128)(2,1)S(1)}, u32[]{:S(2)}, u32[]{:S(2)}) collective-permute-start(bf16[96,768]{1,0:T(8,128)(2,1)S(1)} %get-tuple-element.139), channel_id=1, source_target_pairs={{16,0},{17,1},{18,2},{19,3},{20,4},{21,5},{22,6},{23,7},{24,8},{25... | collective-permute-start | bytes 442376 | tf_op jit(solution)/shard_map/ppermute | solution.py:229
  329.3 17.1 %collective-permute-start.28 = (bf16[96,768]{1,0:T(8,128)(2,1)S(1)}, bf16[96,768]{1,0:T(8,128)(2,1)S(1)}, u32[]{:S(2)}, u32[]{:S(2)}) collective-permute-start(bf16[96,768]{1,0:T(8,128)(2,1)S(1)} %get-tuple-element.138), channel_id=1, source_target_pairs={{0,24},{1,25},{2,26},{3,27},{4,28},{5,29},{6,30},{7,31}} | collective-permute-start | bytes 442376 | tf_op jit(solution)/shard_map/ppermute | solution.py:229
  336.3 10.1 %collective-permute-start.29 = (bf16[96,768]{1,0:T(8,128)(2,1)S(1)}, bf16[96,768]{1,0:T(8,128)(2,1)S(1)}, u32[]{:S(2)}, u32[]{:S(2)}) collective-permute-start(bf16[96,768]{1,0:T(8,128)(2,1)S(1)} %get-tuple-element.137), channel_id=1, source_target_pairs={{24,0},{25,1},{26,2},{27,3},{28,4},{29,5},{30,6},{31,7}} | collective-permute-start | bytes 442376 | tf_op jit(solution)/shard_map/ppermute | solution.py:229
  (77 other events, 1037.8 us)
Sparse Core Ops, SparseCore 0:
  11.5 97.2 all-gather.1
  187.5 160.3 reduce-scatter.1

commit v6 on v4

--- a/solution.py
+++ b/solution.py
@@ -274,7 +274,17 @@
     me = lax.axis_index(("fsdp", "dp"))
     attention_rows = sum(piece.shape[0] for piece in attention_pieces) // owners
     small_count = small_grad_all.shape[0] // owners
-    feed_owned = lax.psum_scatter(feed_pieces, ("fsdp", "dp"), scatter_dimension=0, tiled=True)
+    if staged:
+        feed_rows = feed_pieces.shape[0] // owners
+        dp = lax.axis_index("dp")
+        within = lax.psum_scatter(
+            feed_pieces.reshape(owners // 2, 2 * feed_rows, D), "fsdp", scatter_dimension=0, tiled=True
+        ).reshape(2, feed_rows, D)
+        keep = lax.dynamic_index_in_dim(within, dp, axis=0, keepdims=False)
+        send = lax.dynamic_index_in_dim(within, 1 - dp, axis=0, keepdims=False)
+        feed_owned = keep.astype(jnp.float32) + lax.ppermute(send, "dp", [(0, 1), (1, 0)]).astype(jnp.float32)
+    else:
+        feed_owned = lax.psum_scatter(feed_pieces, ("fsdp", "dp"), scatter_dimension=0, tiled=True)
     partials_high = partials.astype(jnp.bfloat16)
     partials_low = (partials - partials_high.astype(jnp.float32)).astype(jnp.bfloat16)
     split_partials = jnp.concatenate([partials_high, partials_low])

time: 341 us -> 342 us (level)
  waiting for transfers between devices: 77 us -> 72 us
  starting transfers between devices: 88.1 us -> 92.4 us
    ppermute x40, waiting for transfers between devices: 76.9 us -> 69 us  [permute(): return lax.ppermute(tuple(arrays), ('fsdp', 'dp'), pairs)]
  transfers between devices with their start and end apart: 42 -> 43, of which waited for: 13 -> 13; matrix products, arithmetic and copies ran while one was open for 28% -> 29% of each run, Pallas kernels for 0% -> 0%
where the time goes in v6:
time: 342 us; the launch traced here: 339 us
  starting transfers between devices  92.4 us (27%)
  matrix products  90.9 us (27%)
  waiting for transfers between devices  72 us (21%)
  other arithmetic  39.8 us (12%)
  local copies, waits for them, and re-layouts  25.5 us (7%)
  between operations  17.9 us (5%)
    ppermute x40, starting transfers between devices, permute(): return lax.ppermute(tuple(arrays), ('fsdp', 'dp'), pairs)  91.1 us
    ppermute x40, waiting for transfers between devices, permute(): return lax.ppermute(tuple(arrays), ('fsdp', 'dp'), pairs)  69 us
    dot_general x6, matrix products, product_cols(): lax.dot_general(left_side, right_side, (((1,), (1,)), ((), ())), preferre...  36.1 us
    dot_general x6, matrix products, product(): return jnp.dot(left_side, right_side, preferred_element_type=jnp.float32)  13.4 us
    dot_general x1, matrix products, attend_backward(): jnp.einsum('qhd,khd->hqk', grad_heads, head_view(values), preferred_eleme...  10.8 us
    unnamed x119, local copies, waits for them, and re-layouts  10.7 us
    dot_general x1, matrix products, on_device(): lax.dot_general(jnp.stack([inner_grad, active]), jnp.stack([normed_low, f...  9.1 us
    dot_general x1, matrix products, attend_backward(): jnp.einsum('hqk,qhd->khd', probability_low, grad_heads, preferred_element...  8.14 us
  transfers between devices with their start and end apart: 43, of which 13 were waited for; matrix products, arithmetic and copies ran while one was open for 29% of the time, Pallas kernels for 0%

profile of v6, /device:TPU:0, one launch (start us, length us, event | category | flops | bytes accessed | tf_op | source)
XLA Modules:
  0.0 338.6 jit_solution(11404295647671175607)
XLA Ops:
  10.1 5.0 %collective-permute-start.5 = (bf16[96,768]{1,0:T(8,128)(2,1)S(1)}, bf16[96,768]{1,0:T(8,128)(2,1)S(1)}, u32[]{:S(2)}, u32[]{:S(2)}) collective-permute-start(bf16[96,768]{1,0:T(8,128)(2,1)S(1)} %convert_element_type.397), channel_id=1, source_target_pairs={{0,8},{1,9},{2,10},{3,11},{4,12},{5,13},{6,14},{7,15},{8,16},{9,17... | collective-permute-start | bytes 442376 | tf_op jit(solution)/shard_map/ppermute | solution.py:188
  16.4 5.6 %collective-permute-start.3 = (bf16[96,768]{1,0:T(8,128)(2,1)S(1)}, bf16[96,768]{1,0:T(8,128)(2,1)S(1)}, u32[]{:S(2)}, u32[]{:S(2)}) collective-permute-start(bf16[96,768]{1,0:T(8,128)(2,1)S(1)} %convert_element_type.397), channel_id=1, source_target_pairs={{0,16},{1,17},{2,18},{3,19},{4,20},{5,21},{6,22},{7,23},{8,24},{9,... | collective-permute-start | bytes 442376 | tf_op jit(solution)/shard_map/ppermute | solution.py:188
  23.2 6.5 %collective-permute-start.1 = (bf16[96,768]{1,0:T(8,128)(2,1)S(1)}, bf16[96,768]{1,0:T(8,128)(2,1)S(1)}, u32[]{:S(2)}, u32[]{:S(2)}) collective-permute-start(bf16[96,768]{1,0:T(8,128)(2,1)S(1)} %convert_element_type.397), channel_id=1, source_target_pairs={{0,24},{1,25},{2,26},{3,27},{4,28},{5,29},{6,30},{7,31}} | collective-permute-start | bytes 442376 | tf_op jit(solution)/shard_map/ppermute | solution.py:188
  31.2 11.0 %collective-permute-done.2 = bf16[96,768]{1,0:T(8,128)(2,1)S(1)} collective-permute-done((bf16[96,768]{1,0:T(8,128)(2,1)S(1)}, bf16[96,768]{1,0:T(8,128)(2,1)S(1)}, u32[]{:S(2)}, u32[]{:S(2)}) %collective-permute-start.2) | collective-permute-done | bytes 147488 | tf_op jit(solution)/shard_map/ppermute | solution.py:188
  51.9 21.6 %collective-permute-done.6 = bf16[4,96,768]{2,1,0:T(8,128)(2,1)S(1)} collective-permute-done((bf16[4,96,768]{2,1,0:T(8,128)(2,1)S(1)}, bf16[4,96,768]{2,1,0:T(8,128)(2,1)S(1)}, u32[]{:S(2)}, u32[]{:S(2)}) %collective-permute-start.6) | collective-permute-done | bytes 589856 | tf_op jit(solution)/shard_map/ppermute | solution.py:188
  82.7 3.6 %collective-permute-start.11 = (bf16[1,768]{1,0:T(2,128)(2,1)}, bf16[1,768]{1,0:T(2,128)(2,1)S(1)}, u32[]{:S(2)}, u32[]{:S(2)}) collective-permute-start(bf16[1,768]{1,0:T(2,128)(2,1)} %get-tuple-element.155), channel_id=1, source_target_pairs={{0,24},{1,25},{2,26},{3,27},{4,28},{5,29},{6,30},{7,31}} | collective-permute-start | bytes 4616 | tf_op jit(solution)/shard_map/ppermute | solution.py:188
  90.6 3.3 collective-permute-done.10
  109.7 3.0 fusion.142
  114.5 2.7 copy-done
  117.2 2.7 fusion.33
  121.2 20.8 %multiply_convert_fusion.2 = (bf16[512,3072]{1,0:T(8,128)(2,1)S(1)}, f32[512,3072]{1,0:T(8,128)}, f32[512,3072]{1,0:T(8,128)}) fusion(f32[3072]{0:T(1024)S(1)} %slice_convert_fusion, bf16[6144,768]{1,0:T(8,128)(2,1)} %all-gather.2.cloned.1.call-done, f32[512,768]{1,0:T(8,128)S(1)} %get-tuple-element.118, f32[768]{0:T(1024)S(1)} %get-tuple-element.150, ...), kind=kOutput, calls=%fused_computation.17 | convolution fusion | flops 2521694208 | bytes 22042624 | tf_op jit(solution)/shard_map/dot_general | solution.py:37
  142.0 3.7 %fusion.137 = (f32[512]{0:T(512)S(1)}, f32[512,768]{1,0:T(8,128)S(1)}, bf16[1,512,768]{2,1,0:T(8,128)(2,1)S(1)}, f32[]{:T(128)}, f32[]{:T(128)}) fusion(f32[768]{0:T(1024)S(1)} %get-tuple-element.149, f32[768]{0:T(1024)S(1)} %get-tuple-element.150, f32[768]{0:T(1024)S(1)} %get-tuple-element.151, f32[512]{0:T(512)S(1)} %fusion.74, ...), kind=kOutput, calls=%fused_computation.299 | convolution fusion | flops 2421423616 | bytes 13389832 | tf_op jit(solution)/shard_map/dot_general | solution.py:27
  150.4 8.2 %fusion.143 = (bf16[3072]{0:T(1024)(128)(2,1)S(1)}, bf16[512,3072]{1,0:T(8,128)(2,1)}) fusion(f32[512,3072]{1,0:T(8,128)} %get-tuple-element.164, f32[3072]{0:T(1024)S(1)} %slice_convert_fusion, f32[512,3072]{1,0:T(8,128)} %get-tuple-element.116, bf16[512,768]{1,0:T(8,128)(2,1)S(1)} %get-tuple-element.98, bf16[6144,768]{1,0:T(8,128)(2,1)S(1)} %copy-done.51), kind=kOutput, calls=%fused_computation.304 | convolution fusion | flops 2434790400 | bytes 21252096 | tf_op jit(solution)/shard_map/dot_general | solution.py:37
  158.6 9.1 %convolution_convert_fusion = bf16[2,3072,768]{2,1,0:T(8,128)(2,1)} fusion(bf16[1,512,3072]{2,1,0:T(8,128)(2,1)S(1)} %bitcast.339, bf16[1,512,3072]{2,1,0:T(8,128)(2,1)} %bitcast.340, bf16[1,512,768]{2,1,0:T(8,128)(2,1)S(1)} %bitcast.331, bf16[1,512,768]{2,1,0:T(8,128)(2,1)S(1)} %get-tuple-element.128), kind=kOutput, calls=%fused_computation.9 | convolution fusion | flops 4840488960 | bytes 17301504 | tf_op jit(solution)/shard_map/dot_general | solution.py:418
  167.8 6.3 %multiply_reduce_fusion.5 = (bf16[768]{0:T(1024)(128)(2,1)S(1)}, f32[512]{0:T(512)S(1)}, bf16[768]{0:T(1024)(128)(2,1)S(1)}, f32[512,768]{1,0:T(8,128)S(1)}) fusion(f32[512,768]{1,0:T(8,128)S(1)} %get-tuple-element.118, f32[512]{0:T(512)S(1)} %fusion.74, f32[512]{0:T(512)S(1)} %broadcast_multiply_fusion.1, f32[768]{0:T(1024)S(1)} %get-tuple-element.151, ...), kind=kOutput, calls=%fused_computation.55 | convolution fusion | flops 2419849216 | bytes 12597248 | tf_op jit(solution)/shard_map/dot_general | solution.py:27
  181.6 8.1 %bitcast_reduce_fusion = (bf16[12,64]{1,0:T(8,128)(2,1)S(1)}, bf16[12,64,512]{2,1,0:T(8,128)(2,1)S(1)}) fusion(bf16[512,12,64]{0,2,1:T(8,128)(2,1)S(1)} %bitcast.306, f32[12,512,512]{1,2,0:T(8,128)} %copy-done, f32[12,512]{1,0:T(8,128)S(1)} %log_add_fusion), kind=kOutput, calls=%fused_computation.95 | convolution fusion | flops 409730304 | bytes 14181888 | tf_op jit(solution)/shard_map/while/body/eval_jaxpr/hqk,qhd->khd/dot_general | solution.py:107
  191.5 10.8 %multiply_reduce_fusion = (f32[12,512]{1,0:T(8,128)S(1)}, f32[12,512,512]{1,2,0:T(8,128)}) fusion(f32[12,512,512]{1,2,0:T(8,128)} %copy-done, f32[12,512]{1,0:T(8,128)S(1)} %log_add_fusion, bf16[512,12,64]{0,2,1:T(8,128)(2,1)S(1)} %bitcast.307, bf16[512,12,64]{0,2,1:T(8,128)(2,1)S(1)} %bitcast.328), kind=kOutput, calls=%fused_computation.1 | convolution fusion | flops 412084224 | bytes 26787840 | tf_op jit(solution)/shard_map/while/body/eval_jaxpr/qhd,khd->hqk/dot_general | solution.py:110
  203.5 7.1 %multiply_convert_fusion = bf16[12,512,512]{1,2,0:T(8,128)(2,1)S(1)} fusion(f32[12,512,512]{1,2,0:T(8,128)} %get-tuple-element.167, f32[12,512,512]{1,2,0:T(8,128)S(1)} %bitcast.303, f32[12,512]{1,0:T(8,128)S(1)} %get-tuple-element.166, f32[12,512]{1,0:T(8,128)S(1)} %log_add_fusion), kind=kLoop, calls=%fused_computation | loop fusion | flops 12582912 | bytes 31506432 | tf_op jit(solution)/shard_map/while/body/eval_jaxpr/convert_element_type | solution.py:114
  223.2 2.7 fusion.128
  228.2 2.5 fusion.147
  235.2 4.0 %collective-permute-done.34 = bf16[4,16,768]{2,1,0:T(8,128)(2,1)S(1)} collective-permute-done((bf16[4,16,768]{2,1,0:T(8,128)(2,1)S(1)}, bf16[4,16,768]{2,1,0:T(8,128)(2,1)S(1)}, u32[]{:S(2)}, u32[]{:S(2)}) %collective-permute-start.34) | collective-permute-done | bytes 98336 | tf_op jit(solution)/shard_map/ppermute | solution.py:188
  239.2 4.2 %collective-permute-done.32 = bf16[4,16,768]{2,1,0:T(8,128)(2,1)S(1)} collective-permute-done((bf16[4,16,768]{2,1,0:T(8,128)(2,1)S(1)}, bf16[4,16,768]{2,1,0:T(8,128)(2,1)S(1)}, u32[]{:S(2)}, u32[]{:S(2)}) %collective-permute-start.32) | collective-permute-done | bytes 98336 | tf_op jit(solution)/shard_map/ppermute | solution.py:188
  244.8 6.3 %collective-permute-start.39 = (bf16[16,768]{1,0:T(8,128)(2,1)S(1)}, bf16[16,768]{1,0:T(8,128)(2,1)S(1)}, u32[]{:S(2)}, u32[]{:S(2)}) collective-permute-start(bf16[16,768]{1,0:T(8,128)(2,1)S(1)} %get-tuple-element.143), channel_id=1, source_target_pairs={{0,24},{1,25},{2,26},{3,27},{4,28},{5,29},{6,30},{7,31}} | collective-permute-start | bytes 73736 | tf_op jit(solution)/shard_map/ppermute | solution.py:188
  252.5 5.4 %collective-permute-start.37 = (bf16[16,768]{1,0:T(8,128)(2,1)S(1)}, bf16[16,768]{1,0:T(8,128)(2,1)S(1)}, u32[]{:S(2)}, u32[]{:S(2)}) collective-permute-start(bf16[16,768]{1,0:T(8,128)(2,1)S(1)} %get-tuple-element.145), channel_id=1, source_target_pairs={{0,16},{1,17},{2,18},{3,19},{4,20},{5,21},{6,22},{7,23},{8,24},{9,... | collective-permute-start | bytes 73736 | tf_op jit(solution)/shard_map/ppermute | solution.py:188
  262.8 4.9 %collective-permute-start.35 = (bf16[16,768]{1,0:T(8,128)(2,1)S(1)}, bf16[16,768]{1,0:T(8,128)(2,1)S(1)}, u32[]{:S(2)}, u32[]{:S(2)}) collective-permute-start(bf16[16,768]{1,0:T(8,128)(2,1)S(1)} %get-tuple-element.141), channel_id=1, source_target_pairs={{0,8},{1,9},{2,10},{3,11},{4,12},{5,13},{6,14},{7,15},{8,16},{9,17... | collective-permute-start | bytes 73736 | tf_op jit(solution)/shard_map/ppermute | solution.py:188
  275.9 9.1 %collective-permute-done.23 = bf16[4,96,768]{2,1,0:T(8,128)(2,1)S(1)} collective-permute-done((bf16[4,96,768]{2,1,0:T(8,128)(2,1)}, bf16[4,96,768]{2,1,0:T(8,128)(2,1)S(1)}, u32[]{:S(2)}, u32[]{:S(2)}) %collective-permute-start.23) | collective-permute-done | bytes 589856 | tf_op jit(solution)/shard_map/ppermute | solution.py:188
  285.1 9.1 %collective-permute-done.22 = bf16[4,96,768]{2,1,0:T(8,128)(2,1)S(1)} collective-permute-done((bf16[4,96,768]{2,1,0:T(8,128)(2,1)}, bf16[4,96,768]{2,1,0:T(8,128)(2,1)S(1)}, u32[]{:S(2)}, u32[]{:S(2)}) %collective-permute-start.22) | collective-permute-done | bytes 589856 | tf_op jit(solution)/shard_map/ppermute | solution.py:188
  299.4 7.6 %collective-permute-start.28 = (bf16[96,768]{1,0:T(8,128)(2,1)}, bf16[96,768]{1,0:T(8,128)(2,1)}, u32[]{:S(2)}, u32[]{:S(2)}) collective-permute-start(bf16[96,768]{1,0:T(8,128)(2,1)} %get-tuple-element.134), channel_id=1, source_target_pairs={{0,24},{1,25},{2,26},{3,27},{4,28},{5,29},{6,30},{7,31}} | collective-permute-start | bytes 442376 | tf_op jit(solution)/shard_map/ppermute | solution.py:188
  308.3 6.7 %collective-permute-start.26 = (bf16[96,768]{1,0:T(8,128)(2,1)}, bf16[96,768]{1,0:T(8,128)(2,1)}, u32[]{:S(2)}, u32[]{:S(2)}) collective-permute-start(bf16[96,768]{1,0:T(8,128)(2,1)} %get-tuple-element.136), channel_id=1, source_target_pairs={{0,16},{1,17},{2,18},{3,19},{4,20},{5,21},{6,22},{7,23},{8,24},{9,... | collective-permute-start | bytes 442376 | tf_op jit(solution)/shard_map/ppermute | solution.py:188
  316.3 5.2 %collective-permute-start.24 = (bf16[96,768]{1,0:T(8,128)(2,1)}, bf16[96,768]{1,0:T(8,128)(2,1)}, u32[]{:S(2)}, u32[]{:S(2)}) collective-permute-start(bf16[96,768]{1,0:T(8,128)(2,1)} %get-tuple-element.132), channel_id=1, source_target_pairs={{0,8},{1,9},{2,10},{3,11},{4,12},{5,13},{6,14},{7,15},{8,16},{9,17... | collective-permute-start | bytes 442376 | tf_op jit(solution)/shard_map/ppermute | solution.py:188
  324.4 2.5 fusion.133
  326.9 3.0 collective-permute-done.30
  (293 shorter events, 108.5 us)
Async XLA Ops:
  7.2 114.0 %all-gather.2.cloned.1.call-start = ((), (), s32[]{:S(2)}) async-start(), calls=%async_computation.1 | async-start | bytes 9732096 | tf_op jit(solution)/shard_map/all_gather | solution.py:268
  9.1 313.0 %reduce-scatter.2.cloned.1.call-start = ((), (), s32[]{:S(2)}) async-start(), calls=%async_computation.2 | async-start | bytes 10027008 | tf_op jit(solution)/shard_map/reduce_scatter | solution.py:280
  10.1 19.7 %collective-permute-start.5 = (bf16[96,768]{1,0:T(8,128)(2,1)S(1)}, bf16[96,768]{1,0:T(8,128)(2,1)S(1)}, u32[]{:S(2)}, u32[]{:S(2)}) collective-permute-start(bf16[96,768]{1,0:T(8,128)(2,1)S(1)} %convert_element_type.397), channel_id=1, source_target_pairs={{0,8},{1,9},{2,10},{3,11},{4,12},{5,13},{6,14},{7,15},{8,16},{9,17... | collective-permute-start | bytes 442376 | tf_op jit(solution)/shard_map/ppermute | solution.py:188
  15.1 16.1 %collective-permute-start.4 = (bf16[96,768]{1,0:T(8,128)(2,1)S(1)}, bf16[96,768]{1,0:T(8,128)(2,1)S(1)}, u32[]{:S(2)}, u32[]{:S(2)}) collective-permute-start(bf16[96,768]{1,0:T(8,128)(2,1)S(1)} %convert_element_type.397), channel_id=1, source_target_pairs={{8,0},{9,1},{10,2},{11,3},{12,4},{13,5},{14,6},{15,7},{16,8},{17,9... | collective-permute-start | bytes 442376 | tf_op jit(solution)/shard_map/ppermute | solution.py:188
  16.4 14.8 %collective-permute-start.3 = (bf16[96,768]{1,0:T(8,128)(2,1)S(1)}, bf16[96,768]{1,0:T(8,128)(2,1)S(1)}, u32[]{:S(2)}, u32[]{:S(2)}) collective-permute-start(bf16[96,768]{1,0:T(8,128)(2,1)S(1)} %convert_element_type.397), channel_id=1, source_target_pairs={{0,16},{1,17},{2,18},{3,19},{4,20},{5,21},{6,22},{7,23},{8,24},{9,... | collective-permute-start | bytes 442376 | tf_op jit(solution)/shard_map/ppermute | solution.py:188
  21.9 20.2 %collective-permute-start.2 = (bf16[96,768]{1,0:T(8,128)(2,1)S(1)}, bf16[96,768]{1,0:T(8,128)(2,1)S(1)}, u32[]{:S(2)}, u32[]{:S(2)}) collective-permute-start(bf16[96,768]{1,0:T(8,128)(2,1)S(1)} %convert_element_type.397), channel_id=1, source_target_pairs={{16,0},{17,1},{18,2},{19,3},{20,4},{21,5},{22,6},{23,7},{24,8},{25... | collective-permute-start | bytes 442376 | tf_op jit(solution)/shard_map/ppermute | solution.py:188
  23.2 18.9 %collective-permute-start.1 = (bf16[96,768]{1,0:T(8,128)(2,1)S(1)}, bf16[96,768]{1,0:T(8,128)(2,1)S(1)}, u32[]{:S(2)}, u32[]{:S(2)}) collective-permute-start(bf16[96,768]{1,0:T(8,128)(2,1)S(1)} %convert_element_type.397), channel_id=1, source_target_pairs={{0,24},{1,25},{2,26},{3,27},{4,28},{5,29},{6,30},{7,31}} | collective-permute-start | bytes 442376 | tf_op jit(solution)/shard_map/ppermute | solution.py:188
  29.8 12.4 %collective-permute-start = (bf16[96,768]{1,0:T(8,128)(2,1)S(1)}, bf16[96,768]{1,0:T(8,128)(2,1)S(1)}, u32[]{:S(2)}, u32[]{:S(2)}) collective-permute-start(bf16[96,768]{1,0:T(8,128)(2,1)S(1)} %convert_element_type.397), channel_id=1, source_target_pairs={{24,0},{25,1},{26,2},{27,3},{28,4},{29,5},{30,6},{31,7}} | collective-permute-start | bytes 442376 | tf_op jit(solution)/shard_map/ppermute | solution.py:188
  42.5 31.0 %collective-permute-start.6 = (bf16[4,96,768]{2,1,0:T(8,128)(2,1)S(1)}, bf16[4,96,768]{2,1,0:T(8,128)(2,1)S(1)}, u32[]{:S(2)}, u32[]{:S(2)}) collective-permute-start(bf16[4,96,768]{2,1,0:T(8,128)(2,1)S(1)} %select_select_fusion), channel_id=1, source_target_pairs={{0,1},{1,0},{2,3},{3,2},{4,5},{5,4},{6,7},{7,6},{8,9},{9,8},{10,11... | collective-permute-start | bytes 1769480 | tf_op jit(solution)/shard_map/ppermute | solution.py:188
  44.1 31.3 %collective-permute-start.8 = (bf16[4,96,768]{2,1,0:T(8,128)(2,1)S(1)}, bf16[4,96,768]{2,1,0:T(8,128)(2,1)S(1)}, u32[]{:S(2)}, u32[]{:S(2)}) collective-permute-start(bf16[4,96,768]{2,1,0:T(8,128)(2,1)S(1)} %select_select_fusion), channel_id=1, source_target_pairs={{0,5},{1,4},{2,7},{3,6},{4,1},{5,0},{6,3},{7,2},{8,13},{9,12},{10,... | collective-permute-start | bytes 1769480 | tf_op jit(solution)/shard_map/ppermute | solution.py:188
  45.6 33.5 %collective-permute-start.7 = (bf16[4,96,768]{2,1,0:T(8,128)(2,1)S(1)}, bf16[4,96,768]{2,1,0:T(8,128)(2,1)}, u32[]{:S(2)}, u32[]{:S(2)}) collective-permute-start(bf16[4,96,768]{2,1,0:T(8,128)(2,1)S(1)} %select_select_fusion), channel_id=1, source_target_pairs={{0,4},{1,5},{2,6},{3,7},{4,0},{5,1},{6,2},{7,3},{8,12},{9,13},{10,... | collective-permute-start | bytes 1769480 | tf_op jit(solution)/shard_map/ppermute | solution.py:188
  48.0 34.7 %collective-permute-start.15 = (bf16[1,768]{1,0:T(2,128)(2,1)}, bf16[1,768]{1,0:T(2,128)(2,1)}, u32[]{:S(2)}, u32[]{:S(2)}) collective-permute-start(bf16[1,768]{1,0:T(2,128)(2,1)} %get-tuple-element.155), channel_id=1, source_target_pairs={{0,8},{1,9},{2,10},{3,11},{4,12},{5,13},{6,14},{7,15},{8,16},{9,17... | collective-permute-start | bytes 4616 | tf_op jit(solution)/shard_map/ppermute | solution.py:188
  49.9 36.4 %collective-permute-start.14 = (bf16[1,768]{1,0:T(2,128)(2,1)}, bf16[1,768]{1,0:T(2,128)(2,1)}, u32[]{:S(2)}, u32[]{:S(2)}) collective-permute-start(bf16[1,768]{1,0:T(2,128)(2,1)} %get-tuple-element.155), channel_id=1, source_target_pairs={{8,0},{9,1},{10,2},{11,3},{12,4},{13,5},{14,6},{15,7},{16,8},{17,9... | collective-permute-start | bytes 4616 | tf_op jit(solution)/shard_map/ppermute | solution.py:188
  73.5 15.6 %collective-permute-start.13 = (bf16[1,768]{1,0:T(2,128)(2,1)}, bf16[1,768]{1,0:T(2,128)(2,1)}, u32[]{:S(2)}, u32[]{:S(2)}) collective-permute-start(bf16[1,768]{1,0:T(2,128)(2,1)} %get-tuple-element.155), channel_id=1, source_target_pairs={{0,16},{1,17},{2,18},{3,19},{4,20},{5,21},{6,22},{7,23},{8,24},{9,... | collective-permute-start | bytes 4616 | tf_op jit(solution)/shard_map/ppermute | solution.py:188
  75.4 14.5 %collective-permute-start.12 = (bf16[1,768]{1,0:T(2,128)(2,1)}, bf16[1,768]{1,0:T(2,128)(2,1)}, u32[]{:S(2)}, u32[]{:S(2)}) collective-permute-start(bf16[1,768]{1,0:T(2,128)(2,1)} %get-tuple-element.155), channel_id=1, source_target_pairs={{16,0},{17,1},{18,2},{19,3},{20,4},{21,5},{22,6},{23,7},{24,8},{25... | collective-permute-start | bytes 4616 | tf_op jit(solution)/shard_map/ppermute | solution.py:188
  82.6 21.3 %collective-permute-start.9 = (bf16[4,2,2,96,768]{4,3,2,1,0:T(8,128)(2,1)}, bf16[4,2,2,96,768]{4,3,2,1,0:T(8,128)(2,1)}, u32[]{:S(2)}, u32[]{:S(2)}) collective-permute-start(bf16[4,2,2,96,768]{4,3,2,1,0:T(8,128)(2,1)} %broadcast_select_fusion), channel_id=1, source_target_pairs={{0,2},{1,3},{2,0},{3,1},{4,6},{5,7},{6,4},{7,5},{8,10},{9,11},{10,... | collective-permute-start | bytes 7077896 | tf_op jit(solution)/shard_map/ppermute | solution.py:188
  220.0 37.9 %collective-permute-start.20 = (bf16[4,2,2,96,768]{4,3,0,2,1:T(8,128)(2,1)}, bf16[4,2,2,96,768]{4,3,0,2,1:T(8,128)(2,1)}, u32[]{:S(2)}, u32[]{:S(2)}) collective-permute-start(bf16[4,2,2,96,768]{4,3,0,2,1:T(8,128)(2,1)} %bitcast.298), channel_id=1, source_target_pairs={{0,2},{1,3},{2,0},{3,1},{4,6},{5,7},{6,4},{7,5},{8,10},{9,11},{10,... | collective-permute-start | bytes 7077896 | tf_op jit(solution)/shard_map/ppermute | solution.py:188
  233.3 10.1 %collective-permute-start.32 = (bf16[4,16,768]{2,1,0:T(8,128)(2,1)S(1)}, bf16[4,16,768]{2,1,0:T(8,128)(2,1)S(1)}, u32[]{:S(2)}, u32[]{:S(2)}) collective-permute-start(bf16[4,16,768]{2,1,0:T(8,128)(2,1)S(1)} %get-tuple-element.138), channel_id=1, source_target_pairs={{0,4},{1,5},{2,6},{3,7},{4,0},{5,1},{6,2},{7,3},{8,12},{9,13},{10,... | collective-permute-start | bytes 294920 | tf_op jit(solution)/shard_map/ppermute | solution.py:188
  243.5 19.2 %collective-permute-start.40 = (bf16[16,768]{1,0:T(8,128)(2,1)S(1)}, bf16[16,768]{1,0:T(8,128)(2,1)S(1)}, u32[]{:S(2)}, u32[]{:S(2)}) collective-permute-start(bf16[16,768]{1,0:T(8,128)(2,1)S(1)} %get-tuple-element.142), channel_id=1, source_target_pairs={{24,0},{25,1},{26,2},{27,3},{28,4},{29,5},{30,6},{31,7}} | collective-permute-start | bytes 73736 | tf_op jit(solution)/shard_map/ppermute | solution.py:188
  244.8 22.9 %collective-permute-start.39 = (bf16[16,768]{1,0:T(8,128)(2,1)S(1)}, bf16[16,768]{1,0:T(8,128)(2,1)S(1)}, u32[]{:S(2)}, u32[]{:S(2)}) collective-permute-start(bf16[16,768]{1,0:T(8,128)(2,1)S(1)} %get-tuple-element.143), channel_id=1, source_target_pairs={{0,24},{1,25},{2,26},{3,27},{4,28},{5,29},{6,30},{7,31}} | collective-permute-start | bytes 73736 | tf_op jit(solution)/shard_map/ppermute | solution.py:188
  251.2 17.5 %collective-permute-start.38 = (bf16[16,768]{1,0:T(8,128)(2,1)S(1)}, bf16[16,768]{1,0:T(8,128)(2,1)S(1)}, u32[]{:S(2)}, u32[]{:S(2)}) collective-permute-start(bf16[16,768]{1,0:T(8,128)(2,1)S(1)} %get-tuple-element.144), channel_id=1, source_target_pairs={{16,0},{17,1},{18,2},{19,3},{20,4},{21,5},{22,6},{23,7},{24,8},{25... | collective-permute-start | bytes 73736 | tf_op jit(solution)/shard_map/ppermute | solution.py:188
  252.5 17.3 %collective-permute-start.37 = (bf16[16,768]{1,0:T(8,128)(2,1)S(1)}, bf16[16,768]{1,0:T(8,128)(2,1)S(1)}, u32[]{:S(2)}, u32[]{:S(2)}) collective-permute-start(bf16[16,768]{1,0:T(8,128)(2,1)S(1)} %get-tuple-element.145), channel_id=1, source_target_pairs={{0,16},{1,17},{2,18},{3,19},{4,20},{5,21},{6,22},{7,23},{8,24},{9,... | collective-permute-start | bytes 73736 | tf_op jit(solution)/shard_map/ppermute | solution.py:188
  257.9 15.5 %collective-permute-start.36 = (bf16[16,768]{1,0:T(8,128)(2,1)S(1)}, bf16[16,768]{1,0:T(8,128)(2,1)S(1)}, u32[]{:S(2)}, u32[]{:S(2)}) collective-permute-start(bf16[16,768]{1,0:T(8,128)(2,1)S(1)} %get-tuple-element.146), channel_id=1, source_target_pairs={{8,0},{9,1},{10,2},{11,3},{12,4},{13,5},{14,6},{15,7},{16,8},{17,9... | collective-permute-start | bytes 73736 | tf_op jit(solution)/shard_map/ppermute | solution.py:188
  262.8 10.7 %collective-permute-start.35 = (bf16[16,768]{1,0:T(8,128)(2,1)S(1)}, bf16[16,768]{1,0:T(8,128)(2,1)S(1)}, u32[]{:S(2)}, u32[]{:S(2)}) collective-permute-start(bf16[16,768]{1,0:T(8,128)(2,1)S(1)} %get-tuple-element.141), channel_id=1, source_target_pairs={{0,8},{1,9},{2,10},{3,11},{4,12},{5,13},{6,14},{7,15},{8,16},{9,17... | collective-permute-start | bytes 73736 | tf_op jit(solution)/shard_map/ppermute | solution.py:188
  267.7 17.4 %collective-permute-start.23 = (bf16[4,96,768]{2,1,0:T(8,128)(2,1)}, bf16[4,96,768]{2,1,0:T(8,128)(2,1)S(1)}, u32[]{:S(2)}, u32[]{:S(2)}) collective-permute-start(bf16[4,96,768]{2,1,0:T(8,128)(2,1)} %get-tuple-element.120), channel_id=1, source_target_pairs={{0,5},{1,4},{2,7},{3,6},{4,1},{5,0},{6,3},{7,2},{8,13},{9,12},{10,... | collective-permute-start | bytes 1769480 | tf_op jit(solution)/shard_map/ppermute | solution.py:188
  268.7 25.5 %collective-permute-start.22 = (bf16[4,96,768]{2,1,0:T(8,128)(2,1)}, bf16[4,96,768]{2,1,0:T(8,128)(2,1)S(1)}, u32[]{:S(2)}, u32[]{:S(2)}) collective-permute-start(bf16[4,96,768]{2,1,0:T(8,128)(2,1)} %get-tuple-element.121), channel_id=1, source_target_pairs={{0,1},{1,0},{2,3},{3,2},{4,5},{5,4},{6,7},{7,6},{8,9},{9,8},{10,11... | collective-permute-start | bytes 1769480 | tf_op jit(solution)/shard_map/ppermute | solution.py:188
  269.8 24.3 %collective-permute-start.21 = (bf16[4,96,768]{2,1,0:T(8,128)(2,1)}, bf16[4,96,768]{2,1,0:T(8,128)(2,1)}, u32[]{:S(2)}, u32[]{:S(2)}) collective-permute-start(bf16[4,96,768]{2,1,0:T(8,128)(2,1)} %get-tuple-element.119), channel_id=1, source_target_pairs={{0,4},{1,5},{2,6},{3,7},{4,0},{5,1},{6,2},{7,3},{8,12},{9,13},{10,... | collective-permute-start | bytes 1769480 | tf_op jit(solution)/shard_map/ppermute | solution.py:188
  296.8 19.5 %collective-permute-start.29 = (bf16[96,768]{1,0:T(8,128)(2,1)S(1)}, bf16[96,768]{1,0:T(8,128)(2,1)}, u32[]{:S(2)}, u32[]{:S(2)}) collective-permute-start(bf16[96,768]{1,0:T(8,128)(2,1)S(1)} %get-tuple-element.133), channel_id=1, source_target_pairs={{24,0},{25,1},{26,2},{27,3},{28,4},{29,5},{30,6},{31,7}} | collective-permute-start | bytes 442376 | tf_op jit(solution)/shard_map/ppermute | solution.py:188
  299.4 23.7 %collective-permute-start.28 = (bf16[96,768]{1,0:T(8,128)(2,1)}, bf16[96,768]{1,0:T(8,128)(2,1)}, u32[]{:S(2)}, u32[]{:S(2)}) collective-permute-start(bf16[96,768]{1,0:T(8,128)(2,1)} %get-tuple-element.134), channel_id=1, source_target_pairs={{0,24},{1,25},{2,26},{3,27},{4,28},{5,29},{6,30},{7,31}} | collective-permute-start | bytes 442376 | tf_op jit(solution)/shard_map/ppermute | solution.py:188
  307.0 17.4 %collective-permute-start.27 = (bf16[96,768]{1,0:T(8,128)(2,1)}, bf16[96,768]{1,0:T(8,128)(2,1)}, u32[]{:S(2)}, u32[]{:S(2)}) collective-permute-start(bf16[96,768]{1,0:T(8,128)(2,1)} %get-tuple-element.135), channel_id=1, source_target_pairs={{16,0},{17,1},{18,2},{19,3},{20,4},{21,5},{22,6},{23,7},{24,8},{25... | collective-permute-start | bytes 442376 | tf_op jit(solution)/shard_map/ppermute | solution.py:188
  308.3 16.1 %collective-permute-start.26 = (bf16[96,768]{1,0:T(8,128)(2,1)}, bf16[96,768]{1,0:T(8,128)(2,1)}, u32[]{:S(2)}, u32[]{:S(2)}) collective-permute-start(bf16[96,768]{1,0:T(8,128)(2,1)} %get-tuple-element.136), channel_id=1, source_target_pairs={{0,16},{1,17},{2,18},{3,19},{4,20},{5,21},{6,22},{7,23},{8,24},{9,... | collective-permute-start | bytes 442376 | tf_op jit(solution)/shard_map/ppermute | solution.py:188
  315.0 9.4 %collective-permute-start.25 = (bf16[96,768]{1,0:T(8,128)(2,1)}, bf16[96,768]{1,0:T(8,128)(2,1)}, u32[]{:S(2)}, u32[]{:S(2)}) collective-permute-start(bf16[96,768]{1,0:T(8,128)(2,1)} %get-tuple-element.137), channel_id=1, source_target_pairs={{8,0},{9,1},{10,2},{11,3},{12,4},{13,5},{14,6},{15,7},{16,8},{17,9... | collective-permute-start | bytes 442376 | tf_op jit(solution)/shard_map/ppermute | solution.py:188
  (66 other events, 751.0 us)
Sparse Core Ops, SparseCore 0:
  11.5 100.2 all-gather.1
  167.9 113.2 reduce-scatter.1

commit v7 on v6

--- a/solution.py
+++ b/solution.py
@@ -72,7 +72,7 @@
 
 
 def head_view(entries):
-    return entries.reshape(SEQ, HEADS, HDIM)
+    return entries.reshape(SEQ, -1, HDIM)
 
 
 def masked_scores(queries, key_vectors, key_valid):
@@ -126,9 +126,9 @@
         * score_scale
     )
     return (
-        query_grad.reshape(SEQ, D).astype(jnp.bfloat16),
-        key_grad.reshape(SEQ, D).astype(jnp.bfloat16),
-        value_grad.reshape(SEQ, D).astype(jnp.bfloat16),
+        query_grad.reshape(SEQ, -1).astype(jnp.bfloat16),
+        key_grad.reshape(SEQ, -1).astype(jnp.bfloat16),
+        value_grad.reshape(SEQ, -1).astype(jnp.bfloat16),
     )
 
 
@@ -269,10 +269,10 @@
     return attention_full, feed_full, small_full
 
 
-def scatter_gradients(attention_pieces, feed_pieces, small_grad_all, partials, staged):
+def scatter_gradients(attention_parts, feed_pieces, small_grad_all, partials, staged):
     owners = lax.psum(1, ("fsdp", "dp"))
     me = lax.axis_index(("fsdp", "dp"))
-    attention_rows = sum(piece.shape[0] for piece in attention_pieces) // owners
+    attention_rows = sum(piece.shape[0] for piece in attention_parts[0]) // owners
     small_count = small_grad_all.shape[0] // owners
     if staged:
         feed_rows = feed_pieces.shape[0] // owners
@@ -303,11 +303,20 @@
     ).reshape(owners, extra_rows, D)
     block_rows = attention_rows + extra_rows
     if staged:
-        attention_grad_all = jnp.concatenate(attention_pieces, axis=0).astype(jnp.bfloat16)
+        owned_parts = []
+        for index, pieces in enumerate(attention_parts):
+            part_all = jnp.concatenate(pieces, axis=0).astype(jnp.bfloat16)
+            arrays = [part_all.reshape(owners, attention_rows, part_all.shape[1])]
+            if index == len(attention_parts) - 1:
+                arrays.append(extra)
+            owned_parts.append(staged_reduce_scatter(arrays))
         owned = jnp.concatenate(
-            staged_reduce_scatter([attention_grad_all.reshape(owners, attention_rows, D), extra]), axis=0
+            [jnp.concatenate([part[0] for part in owned_parts], axis=1), owned_parts[-1][1]], axis=0
         )
     else:
+        attention_pieces = [
+            jnp.concatenate([pieces[index] for pieces in attention_parts], axis=1) for index in range(4)
+        ]
         packed = jnp.zeros((owners, block_rows, D), jnp.bfloat16)
         packed = lax.dynamic_update_slice(packed, extra, (0, attention_rows, 0))
         owner = 0
@@ -430,25 +439,41 @@
     first_sum_grad, first_gain_grad, first_shift_grad = first_pull(normed_grad)
     branch_grad_low = first_sum_grad.astype(jnp.bfloat16)
     output_bias_grad = column_total(branch_grad_low)
-    output_weight_grad = product_rows(attended, branch_grad_low)
     attended_grad = product_cols(branch_grad_low, output_weight).astype(jnp.bfloat16)
-    query_grad, key_grad, value_grad = lax.map(
-        attend_backward,
-        (
-            queries.reshape(seq_shape),
-            key_vectors.reshape(seq_shape),
-            values.reshape(seq_shape),
-            key_valid,
-            log_total,
-            attended_grad.reshape(seq_shape),
-        ),
-    )
-    query_grad = query_grad.reshape(row_count, D)
-    key_grad = key_grad.reshape(row_count, D)
-    value_grad = value_grad.reshape(row_count, D)
-    query_weight_grad = product_rows(tokens, query_grad)
-    key_weight_grad = product_rows(tokens, key_grad)
-    value_weight_grad = product_rows(tokens, value_grad)
+    parts = 2
+    width = D // parts
+    head_count = HEADS // parts
+    part_grads = []
+    attention_parts = []
+    for part in range(parts):
+        columns = slice(part * width, (part + 1) * width)
+        part_shape = (sequence_count, SEQ, width)
+        query_part, key_part, value_part = lax.map(
+            attend_backward,
+            (
+                queries[:, columns].reshape(part_shape),
+                key_vectors[:, columns].reshape(part_shape),
+                values[:, columns].reshape(part_shape),
+                key_valid,
+                log_total[:, part * head_count : (part + 1) * head_count],
+                attended_grad[:, columns].reshape(part_shape),
+            ),
+        )
+        query_part = query_part.reshape(row_count, width)
+        key_part = key_part.reshape(row_count, width)
+        value_part = value_part.reshape(row_count, width)
+        part_grads.append((query_part, key_part, value_part))
+        attention_parts.append(
+            [
+                product_rows(tokens, query_part),
+                product_rows(tokens, key_part),
+                product_rows(tokens, value_part),
+                product_rows(attended, branch_grad_low[:, columns]),
+            ]
+        )
+    query_grad = jnp.concatenate([grads[0] for grads in part_grads], axis=1)
+    key_grad = jnp.concatenate([grads[1] for grads in part_grads], axis=1)
+    value_grad = jnp.concatenate([grads[2] for grads in part_grads], axis=1)
     query_bias_grad = column_total(query_grad)
     value_bias_grad = column_total(value_grad)
     tokens_grad = (
@@ -471,7 +496,7 @@
         ]
     )
     attention_owned, feed_owned, small_owned, totals = scatter_gradients(
-        [query_weight_grad, key_weight_grad, value_weight_grad, output_weight_grad],
+        attention_parts,
         feed_grad_all,
         small_grad_all,
         partials,

time: 342 us -> 388 us (1.13)
  starting transfers between devices: 92.4 us -> 114 us
  local copies, waits for them, and re-layouts: 25.5 us -> 41.3 us
  waiting for transfers between devices: 72 us -> 62.8 us
  matrix products: 90.9 us -> 99.7 us
  other arithmetic: 39.8 us -> 48.3 us
    ppermute x40 -> x50, starting transfers between devices: 91.1 us -> 112 us  [permute(): return lax.ppermute(tuple(arrays), ('fsdp', 'dp'), pairs)]
    ppermute x40 -> x50, waiting for transfers between devices: 69 us -> 59.7 us  [permute(): return lax.ppermute(tuple(arrays), ('fsdp', 'dp'), pairs)]
    concatenate x0 -> x2, local copies, waits for them, and re-layouts: none -> 7.37 us  [scatter_gradients(): part_all = jnp.concatenate(pieces, axis=0).astype(jnp.bfloat16)]
    dot_general x1 -> x3, matrix products: 3.03 us -> 10.4 us  [masked_scores(): jnp.einsum('qhd,khd->hqk', head_view(queries), head_view(key_vectors), pr...]
    slice x0 -> x6, local copies, waits for them, and re-layouts: none -> 4.91 us  [the longest x3 3.86 us: on_device(): attended_grad[:, columns].reshape(part_shape)]
    dot_general x1 -> x2, matrix products: 10.8 us -> 6.7 us  [attend_backward(): jnp.einsum('qhd,khd->hqk', grad_heads, head_view(values), preferred_eleme...]
    dot_general x4 -> x8, matrix products: 4.5 us -> 7.89 us  [product_rows(): lax.dot_general(left_side, right_side, (((0,), (0,)), ((), ())), preferre...]
    unnamed x119 -> x161, local copies, waits for them, and re-layouts: 10.7 us -> 7.74 us
  transfers between devices with their start and end apart: 43 -> 53, of which waited for: 13 -> 15; matrix products, arithmetic and copies ran while one was open for 29% -> 34% of each run, Pallas kernels for 0% -> 0%
where the time goes in v7:
time: 388 us; the launch traced here: 384 us
  starting transfers between devices  114 us (29%)
  matrix products  99.7 us (26%)
  waiting for transfers between devices  62.8 us (16%)
  other arithmetic  48.3 us (12%)
  local copies, waits for them, and re-layouts  41.3 us (11%)
  between operations  18.2 us (5%)
    ppermute x50, starting transfers between devices, permute(): return lax.ppermute(tuple(arrays), ('fsdp', 'dp'), pairs)  112 us
    ppermute x50, waiting for transfers between devices, permute(): return lax.ppermute(tuple(arrays), ('fsdp', 'dp'), pairs)  59.7 us
    dot_general x6, matrix products, product_cols(): lax.dot_general(left_side, right_side, (((1,), (1,)), ((), ())), preferre...  34.7 us
    dot_general x6, matrix products, product(): return jnp.dot(left_side, right_side, preferred_element_type=jnp.float32)  11.3 us
    dot_general x3, matrix products, masked_scores(): jnp.einsum('qhd,khd->hqk', head_view(queries), head_view(key_vectors), pr...  10.4 us
    dot_general x1, matrix products, on_device(): lax.dot_general(jnp.stack([inner_grad, active]), jnp.stack([normed_low, f...  10.1 us
    dot_general x2, matrix products, attend_backward(): jnp.einsum('hqk,qhd->khd', probability_low, grad_heads, preferred_element...  9.76 us
    convert_element_type x1, other arithmetic, attend_backward(): (probability * (probability_grad - inner_total)).astype(jnp.bfloat16)  7.9 us
  transfers between devices with their start and end apart: 53, of which 15 were waited for; matrix products, arithmetic and copies ran while one was open for 34% of the time, Pallas kernels for 0%

profile of v7, /device:TPU:0, one launch (start us, length us, event | category | flops | bytes accessed | tf_op | source)
XLA Modules:
  0.0 384.1 jit_solution(10664305779657966633)
XLA Ops:
  10.1 5.0 %collective-permute-start.5 = (bf16[96,768]{1,0:T(8,128)(2,1)S(1)}, bf16[96,768]{1,0:T(8,128)(2,1)S(1)}, u32[]{:S(2)}, u32[]{:S(2)}) collective-permute-start(bf16[96,768]{1,0:T(8,128)(2,1)S(1)} %convert_element_type.520), channel_id=1, source_target_pairs={{0,8},{1,9},{2,10},{3,11},{4,12},{5,13},{6,14},{7,15},{8,16},{9,17... | collective-permute-start | bytes 442376 | tf_op jit(solution)/shard_map/ppermute | solution.py:188
  16.4 5.6 %collective-permute-start.3 = (bf16[96,768]{1,0:T(8,128)(2,1)S(1)}, bf16[96,768]{1,0:T(8,128)(2,1)S(1)}, u32[]{:S(2)}, u32[]{:S(2)}) collective-permute-start(bf16[96,768]{1,0:T(8,128)(2,1)S(1)} %convert_element_type.520), channel_id=1, source_target_pairs={{0,16},{1,17},{2,18},{3,19},{4,20},{5,21},{6,22},{7,23},{8,24},{9,... | collective-permute-start | bytes 442376 | tf_op jit(solution)/shard_map/ppermute | solution.py:188
  23.2 6.5 %collective-permute-start.1 = (bf16[96,768]{1,0:T(8,128)(2,1)S(1)}, bf16[96,768]{1,0:T(8,128)(2,1)S(1)}, u32[]{:S(2)}, u32[]{:S(2)}) collective-permute-start(bf16[96,768]{1,0:T(8,128)(2,1)S(1)} %convert_element_type.520), channel_id=1, source_target_pairs={{0,24},{1,25},{2,26},{3,27},{4,28},{5,29},{6,30},{7,31}} | collective-permute-start | bytes 442376 | tf_op jit(solution)/shard_map/ppermute | solution.py:188
  31.2 11.0 %collective-permute-done.2 = bf16[96,768]{1,0:T(8,128)(2,1)S(1)} collective-permute-done((bf16[96,768]{1,0:T(8,128)(2,1)S(1)}, bf16[96,768]{1,0:T(8,128)(2,1)S(1)}, u32[]{:S(2)}, u32[]{:S(2)}) %collective-permute-start.2) | collective-permute-done | bytes 147488 | tf_op jit(solution)/shard_map/ppermute | solution.py:188
  51.9 21.6 %collective-permute-done.6 = bf16[4,96,768]{2,1,0:T(8,128)(2,1)S(1)} collective-permute-done((bf16[4,96,768]{2,1,0:T(8,128)(2,1)S(1)}, bf16[4,96,768]{2,1,0:T(8,128)(2,1)S(1)}, u32[]{:S(2)}, u32[]{:S(2)}) %collective-permute-start.6) | collective-permute-done | bytes 589856 | tf_op jit(solution)/shard_map/ppermute | solution.py:188
  83.5 3.6 collective-permute-start.11
  116.5 3.4 fusion.32
  124.6 3.6 fusion.198
  128.3 3.7 fusion.199
  132.0 20.4 %multiply_convert_fusion.3 = (bf16[512,3072]{1,0:T(8,128)(2,1)S(1)}, f32[512,3072]{1,0:T(8,128)}, f32[512,3072]{1,0:T(8,128)}) fusion(f32[3072]{0:T(1024)S(1)} %slice_convert_fusion, bf16[6144,768]{1,0:T(8,128)(2,1)} %all-gather.2.cloned.1.call-done, f32[512,768]{1,0:T(8,128)S(1)} %get-tuple-element.150, f32[768]{0:T(1024)S(1)} %get-tuple-element.201, ...), kind=kOutput, calls=%fused_computation.18 | convolution fusion | flops 2521694208 | bytes 22042624 | tf_op jit(solution)/shard_map/dot_general | solution.py:37
  152.4 3.7 fusion.186
  159.8 8.1 %fusion.195 = (bf16[3072]{0:T(1024)(128)(2,1)S(1)}, bf16[512,3072]{1,0:T(8,128)(2,1)}) fusion(f32[512,3072]{1,0:T(8,128)} %get-tuple-element.217, f32[3072]{0:T(1024)S(1)} %slice_convert_fusion, f32[512,3072]{1,0:T(8,128)} %get-tuple-element.148, bf16[512,768]{1,0:T(8,128)(2,1)S(1)} %get-tuple-element.130, bf16[6144,768]{1,0:T(8,128)(2,1)S(1)} %copy-done.69), kind=kOutput, calls=%fused_computation.379 | convolution fusion | flops 2434790400 | bytes 21252096 | tf_op jit(solution)/shard_map/dot_general | solution.py:37
  167.9 10.1 %convolution_convert_fusion = bf16[2,3072,768]{2,1,0:T(8,128)(2,1)} fusion(bf16[1,512,3072]{2,1,0:T(8,128)(2,1)} %bitcast.456, bf16[1,512,3072]{2,1,0:T(8,128)(2,1)} %bitcast.457, bf16[1,512,768]{2,1,0:T(8,128)(2,1)S(1)} %bitcast.450, bf16[1,512,768]{2,1,0:T(8,128)(2,1)S(1)} %get-tuple-element.163), kind=kOutput, calls=%fused_computation.6 | convolution fusion | flops 4840488960 | bytes 17301504 | tf_op jit(solution)/shard_map/dot_general | solution.py:427
  178.0 3.1 multiply_reduce_fusion.6
  193.5 5.4 %fusion.47 = bf16[6,64,512]{2,1,0:T(8,128)(2,1)S(1)} fusion(bf16[512,6,64]{0,2,1:T(8,128)(2,1)} %bitcast.435, f32[6,512,512]{1,2,0:T(8,128)} %fusion.199, f32[6,512]{1,0:T(8,128)S(1)} %get-tuple-element.196, pred[512]{0:T(512)(128)(4,1)S(1)} %fusion.113), kind=kOutput, calls=%fused_computation.105 | convolution fusion | flops 207814656 | bytes 7090688 | tf_op jit(solution)/shard_map/while/body/eval_jaxpr/hqk,qhd->khd/dot_general | solution.py:107
  202.2 5.7 %multiply_reduce_fusion.1 = (f32[6,512]{1,0:T(8,128)S(1)}, f32[6,512]{1,0:T(8,128)S(1)}, f32[6,512,512]{1,2,0:T(8,128)}) fusion(f32[6,512,512]{1,2,0:T(8,128)S(1)} %bitcast.393, f32[6,512]{1,0:T(8,128)S(1)} %get-tuple-element.197, pred[512]{0:T(512)(128)(4,1)S(1)} %fusion.113, f32[6,512,512]{1,2,0:T(8,128)S(1)} %fusion.200, ...), kind=kOutput, calls=%fused_computation.15 | convolution fusion | flops 217049088 | bytes 26001920 | tf_op jit(solution)/shard_map/while/body/eval_jaxpr/qhd,khd->hqk/dot_general | solution.py:110
  207.8 7.9 %multiply_convert_fusion.1 = (bf16[6,512,512]{1,2,0:T(8,128)(2,1)}, bf16[6,512,512]{1,2,0:T(8,128)(2,1)}) fusion(f32[6,512,512]{1,2,0:T(8,128)} %get-tuple-element.219, f32[6,512,512]{1,2,0:T(8,128)S(1)} %bitcast.393, f32[6,512]{1,0:T(8,128)S(1)} %get-tuple-element.121, f32[6,512]{1,0:T(8,128)S(1)} %get-tuple-element.197, pred[512]{0:T(512)(128)(4,1)S(1)} %fusion.113, ...), kind=kLoop, calls=%fused_computation.14 | loop fusion | flops 18874368 | bytes 31506944 | tf_op jit(solution)/shard_map/while/body/eval_jaxpr/convert_element_type | solution.py:114
  215.8 3.1 fusion.37
  222.4 4.3 %copy.62 = bf16[3072,384]{1,0:T(8,128)(2,1)} copy(bf16[3072,384]{0,1:T(8,128)(2,1)} %pad_maximum_fusion.1) | data formatting | bytes 4718592 | tf_op jit(solution)/shard_map/concatenate | solution.py:308
  232.3 4.4 %fusion.44 = bf16[6,64,512]{2,1,0:T(8,128)(2,1)S(1)} fusion(bf16[512,6,64]{0,2,1:T(8,128)(2,1)S(1)} %bitcast.442, f32[6,512,512]{1,2,0:T(8,128)} %fusion.198, f32[6,512]{1,0:T(8,128)S(1)} %get-tuple-element.197, pred[512]{0:T(512)(128)(4,1)S(1)} %fusion.113), kind=kOutput, calls=%fused_computation.104 | convolution fusion | flops 207814656 | bytes 7090688 | tf_op jit(solution)/shard_map/while/body/eval_jaxpr/hqk,qhd->khd/dot_general | solution.py:107
  259.2 4.5 %collective-permute-done.44 = bf16[4,16,768]{2,1,0:T(8,128)(2,1)S(1)} collective-permute-done((bf16[4,16,768]{2,1,0:T(8,128)(2,1)S(1)}, bf16[4,16,768]{2,1,0:T(8,128)(2,1)S(1)}, u32[]{:S(2)}, u32[]{:S(2)}) %collective-permute-start.44) | collective-permute-done | bytes 98336 | tf_op jit(solution)/shard_map/ppermute | solution.py:188
  268.2 7.5 %collective-permute-start.49 = (bf16[16,768]{1,0:T(8,128)(2,1)}, bf16[16,768]{1,0:T(8,128)(2,1)}, u32[]{:S(2)}, u32[]{:S(2)}) collective-permute-start(bf16[16,768]{1,0:T(8,128)(2,1)} %get-tuple-element.192), channel_id=1, source_target_pairs={{0,24},{1,25},{2,26},{3,27},{4,28},{5,29},{6,30},{7,31}} | collective-permute-start | bytes 73736 | tf_op jit(solution)/shard_map/ppermute | solution.py:188
  281.9 5.4 %collective-permute-start.47 = (bf16[16,768]{1,0:T(8,128)(2,1)}, bf16[16,768]{1,0:T(8,128)(2,1)S(1)}, u32[]{:S(2)}, u32[]{:S(2)}) collective-permute-start(bf16[16,768]{1,0:T(8,128)(2,1)} %get-tuple-element.194), channel_id=1, source_target_pairs={{0,16},{1,17},{2,18},{3,19},{4,20},{5,21},{6,22},{7,23},{8,24},{9,... | collective-permute-start | bytes 73736 | tf_op jit(solution)/shard_map/ppermute | solution.py:188
  288.6 4.5 %collective-permute-start.45 = (bf16[16,768]{1,0:T(8,128)(2,1)}, bf16[16,768]{1,0:T(8,128)(2,1)S(1)}, u32[]{:S(2)}, u32[]{:S(2)}) collective-permute-start(bf16[16,768]{1,0:T(8,128)(2,1)} %get-tuple-element.190), channel_id=1, source_target_pairs={{0,8},{1,9},{2,10},{3,11},{4,12},{5,13},{6,14},{7,15},{8,16},{9,17... | collective-permute-start | bytes 73736 | tf_op jit(solution)/shard_map/ppermute | solution.py:188
  313.8 3.4 collective-permute-done.33
  317.9 5.7 %collective-permute-done.32 = bf16[4,96,384]{2,1,0:T(8,128)(2,1)S(1)} collective-permute-done((bf16[4,96,384]{2,1,0:T(8,128)(2,1)S(1)}, bf16[4,96,384]{2,1,0:T(8,128)(2,1)S(1)}, u32[]{:S(2)}, u32[]{:S(2)}) %collective-permute-start.32) | collective-permute-done | bytes 294944 | tf_op jit(solution)/shard_map/ppermute | solution.py:188
  325.2 6.3 %collective-permute-start.38 = (bf16[96,384]{1,0:T(8,128)(2,1)S(1)}, bf16[96,384]{1,0:T(8,128)(2,1)S(1)}, u32[]{:S(2)}, u32[]{:S(2)}) collective-permute-start(bf16[96,384]{1,0:T(8,128)(2,1)S(1)} %get-tuple-element.186), channel_id=1, source_target_pairs={{0,24},{1,25},{2,26},{3,27},{4,28},{5,29},{6,30},{7,31}} | collective-permute-start | bytes 221192 | tf_op jit(solution)/shard_map/ppermute | solution.py:188
  335.1 3.2 collective-permute-start.36
  340.0 4.5 %collective-permute-start.34 = (bf16[96,384]{1,0:T(8,128)(2,1)S(1)}, bf16[96,384]{1,0:T(8,128)(2,1)S(1)}, u32[]{:S(2)}, u32[]{:S(2)}) collective-permute-start(bf16[96,384]{1,0:T(8,128)(2,1)S(1)} %get-tuple-element.184), channel_id=1, source_target_pairs={{0,8},{1,9},{2,10},{3,11},{4,12},{5,13},{6,14},{7,15},{8,16},{9,17... | collective-permute-start | bytes 221192 | tf_op jit(solution)/shard_map/ppermute | solution.py:188
  346.6 6.3 %collective-permute-start.28 = (bf16[96,384]{1,0:T(8,128)(2,1)}, bf16[96,384]{1,0:T(8,128)(2,1)S(1)}, u32[]{:S(2)}, u32[]{:S(2)}) collective-permute-start(bf16[96,384]{1,0:T(8,128)(2,1)} %get-tuple-element.180), channel_id=1, source_target_pairs={{0,24},{1,25},{2,26},{3,27},{4,28},{5,29},{6,30},{7,31}} | collective-permute-start | bytes 221192 | tf_op jit(solution)/shard_map/ppermute | solution.py:188
  354.3 6.7 %collective-permute-start.26 = (bf16[96,384]{1,0:T(8,128)(2,1)}, bf16[96,384]{1,0:T(8,128)(2,1)}, u32[]{:S(2)}, u32[]{:S(2)}) collective-permute-start(bf16[96,384]{1,0:T(8,128)(2,1)} %get-tuple-element.182), channel_id=1, source_target_pairs={{0,16},{1,17},{2,18},{3,19},{4,20},{5,21},{6,22},{7,23},{8,24},{9,... | collective-permute-start | bytes 221192 | tf_op jit(solution)/shard_map/ppermute | solution.py:188
  362.3 5.2 %collective-permute-start.24 = (bf16[96,384]{1,0:T(8,128)(2,1)}, bf16[96,384]{1,0:T(8,128)(2,1)}, u32[]{:S(2)}, u32[]{:S(2)}) collective-permute-start(bf16[96,384]{1,0:T(8,128)(2,1)} %get-tuple-element.178), channel_id=1, source_target_pairs={{0,8},{1,9},{2,10},{3,11},{4,12},{5,13},{6,14},{7,15},{8,16},{9,17... | collective-permute-start | bytes 221192 | tf_op jit(solution)/shard_map/ppermute | solution.py:188
  (382 shorter events, 162.5 us)
Async XLA Ops:
  7.2 124.8 %all-gather.2.cloned.1.call-start = ((), (), s32[]{:S(2)}) async-start(), calls=%async_computation.1 | async-start | bytes 9732096 | tf_op jit(solution)/shard_map/all_gather | solution.py:268
  9.1 358.5 %reduce-scatter.2.cloned.1.call-start = ((), (), s32[]{:S(2)}) async-start(), calls=%async_computation.2 | async-start | bytes 10027008 | tf_op jit(solution)/shard_map/reduce_scatter | solution.py:280
  10.1 19.7 %collective-permute-start.5 = (bf16[96,768]{1,0:T(8,128)(2,1)S(1)}, bf16[96,768]{1,0:T(8,128)(2,1)S(1)}, u32[]{:S(2)}, u32[]{:S(2)}) collective-permute-start(bf16[96,768]{1,0:T(8,128)(2,1)S(1)} %convert_element_type.520), channel_id=1, source_target_pairs={{0,8},{1,9},{2,10},{3,11},{4,12},{5,13},{6,14},{7,15},{8,16},{9,17... | collective-permute-start | bytes 442376 | tf_op jit(solution)/shard_map/ppermute | solution.py:188
  15.1 16.1 %collective-permute-start.4 = (bf16[96,768]{1,0:T(8,128)(2,1)S(1)}, bf16[96,768]{1,0:T(8,128)(2,1)S(1)}, u32[]{:S(2)}, u32[]{:S(2)}) collective-permute-start(bf16[96,768]{1,0:T(8,128)(2,1)S(1)} %convert_element_type.520), channel_id=1, source_target_pairs={{8,0},{9,1},{10,2},{11,3},{12,4},{13,5},{14,6},{15,7},{16,8},{17,9... | collective-permute-start | bytes 442376 | tf_op jit(solution)/shard_map/ppermute | solution.py:188
  21.9 20.2 %collective-permute-start.2 = (bf16[96,768]{1,0:T(8,128)(2,1)S(1)}, bf16[96,768]{1,0:T(8,128)(2,1)S(1)}, u32[]{:S(2)}, u32[]{:S(2)}) collective-permute-start(bf16[96,768]{1,0:T(8,128)(2,1)S(1)} %convert_element_type.520), channel_id=1, source_target_pairs={{16,0},{17,1},{18,2},{19,3},{20,4},{21,5},{22,6},{23,7},{24,8},{25... | collective-permute-start | bytes 442376 | tf_op jit(solution)/shard_map/ppermute | solution.py:188
  23.2 18.9 %collective-permute-start.1 = (bf16[96,768]{1,0:T(8,128)(2,1)S(1)}, bf16[96,768]{1,0:T(8,128)(2,1)S(1)}, u32[]{:S(2)}, u32[]{:S(2)}) collective-permute-start(bf16[96,768]{1,0:T(8,128)(2,1)S(1)} %convert_element_type.520), channel_id=1, source_target_pairs={{0,24},{1,25},{2,26},{3,27},{4,28},{5,29},{6,30},{7,31}} | collective-permute-start | bytes 442376 | tf_op jit(solution)/shard_map/ppermute | solution.py:188
  42.5 31.0 %collective-permute-start.6 = (bf16[4,96,768]{2,1,0:T(8,128)(2,1)S(1)}, bf16[4,96,768]{2,1,0:T(8,128)(2,1)S(1)}, u32[]{:S(2)}, u32[]{:S(2)}) collective-permute-start(bf16[4,96,768]{2,1,0:T(8,128)(2,1)S(1)} %select_select_fusion), channel_id=1, source_target_pairs={{0,1},{1,0},{2,3},{3,2},{4,5},{5,4},{6,7},{7,6},{8,9},{9,8},{10,11... | collective-permute-start | bytes 1769480 | tf_op jit(solution)/shard_map/ppermute | solution.py:188
  44.1 31.3 %collective-permute-start.8 = (bf16[4,96,768]{2,1,0:T(8,128)(2,1)S(1)}, bf16[4,96,768]{2,1,0:T(8,128)(2,1)S(1)}, u32[]{:S(2)}, u32[]{:S(2)}) collective-permute-start(bf16[4,96,768]{2,1,0:T(8,128)(2,1)S(1)} %select_select_fusion), channel_id=1, source_target_pairs={{0,5},{1,4},{2,7},{3,6},{4,1},{5,0},{6,3},{7,2},{8,13},{9,12},{10,... | collective-permute-start | bytes 1769480 | tf_op jit(solution)/shard_map/ppermute | solution.py:188
  45.6 33.5 %collective-permute-start.7 = (bf16[4,96,768]{2,1,0:T(8,128)(2,1)S(1)}, bf16[4,96,768]{2,1,0:T(8,128)(2,1)}, u32[]{:S(2)}, u32[]{:S(2)}) collective-permute-start(bf16[4,96,768]{2,1,0:T(8,128)(2,1)S(1)} %select_select_fusion), channel_id=1, source_target_pairs={{0,4},{1,5},{2,6},{3,7},{4,0},{5,1},{6,2},{7,3},{8,12},{9,13},{10,... | collective-permute-start | bytes 1769480 | tf_op jit(solution)/shard_map/ppermute | solution.py:188
  48.0 35.5 %collective-permute-start.15 = (bf16[1,768]{1,0:T(2,128)(2,1)}, bf16[1,768]{1,0:T(2,128)(2,1)}, u32[]{:S(2)}, u32[]{:S(2)}) collective-permute-start(bf16[1,768]{1,0:T(2,128)(2,1)} %get-tuple-element.206), channel_id=1, source_target_pairs={{0,8},{1,9},{2,10},{3,11},{4,12},{5,13},{6,14},{7,15},{8,16},{9,17... | collective-permute-start | bytes 4616 | tf_op jit(solution)/shard_map/ppermute | solution.py:188
  49.9 37.2 %collective-permute-start.14 = (bf16[1,768]{1,0:T(2,128)(2,1)}, bf16[1,768]{1,0:T(2,128)(2,1)}, u32[]{:S(2)}, u32[]{:S(2)}) collective-permute-start(bf16[1,768]{1,0:T(2,128)(2,1)} %get-tuple-element.206), channel_id=1, source_target_pairs={{8,0},{9,1},{10,2},{11,3},{12,4},{13,5},{14,6},{15,7},{16,8},{17,9... | collective-permute-start | bytes 4616 | tf_op jit(solution)/shard_map/ppermute | solution.py:188
  73.5 17.5 %collective-permute-start.13 = (bf16[1,768]{1,0:T(2,128)(2,1)}, bf16[1,768]{1,0:T(2,128)(2,1)}, u32[]{:S(2)}, u32[]{:S(2)}) collective-permute-start(bf16[1,768]{1,0:T(2,128)(2,1)} %get-tuple-element.206), channel_id=1, source_target_pairs={{0,16},{1,17},{2,18},{3,19},{4,20},{5,21},{6,22},{7,23},{8,24},{9,... | collective-permute-start | bytes 4616 | tf_op jit(solution)/shard_map/ppermute | solution.py:188
  75.4 16.3 %collective-permute-start.12 = (bf16[1,768]{1,0:T(2,128)(2,1)}, bf16[1,768]{1,0:T(2,128)(2,1)}, u32[]{:S(2)}, u32[]{:S(2)}) collective-permute-start(bf16[1,768]{1,0:T(2,128)(2,1)} %get-tuple-element.206), channel_id=1, source_target_pairs={{16,0},{17,1},{18,2},{19,3},{20,4},{21,5},{22,6},{23,7},{24,8},{25... | collective-permute-start | bytes 4616 | tf_op jit(solution)/shard_map/ppermute | solution.py:188
  82.7 22.1 %collective-permute-start.9 = (bf16[4,2,2,96,768]{4,3,2,1,0:T(8,128)(2,1)}, bf16[4,2,2,96,768]{4,3,2,1,0:T(8,128)(2,1)}, u32[]{:S(2)}, u32[]{:S(2)}) collective-permute-start(bf16[4,2,2,96,768]{4,3,2,1,0:T(8,128)(2,1)} %broadcast_select_fusion), channel_id=1, source_target_pairs={{0,2},{1,3},{2,0},{3,1},{4,6},{5,7},{6,4},{7,5},{8,10},{9,11},{10,... | collective-permute-start | bytes 7077896 | tf_op jit(solution)/shard_map/ppermute | solution.py:188
  230.9 73.6 %collective-permute-start.30 = (bf16[4,2,2,96,384]{4,3,0,2,1:T(8,128)(2,1)}, bf16[4,2,2,96,384]{4,3,0,2,1:T(8,128)(2,1)}, u32[]{:S(2)}, u32[]{:S(2)}) collective-permute-start(bf16[4,2,2,96,384]{4,3,0,2,1:T(8,128)(2,1)} %bitcast.388), channel_id=1, source_target_pairs={{0,2},{1,3},{2,0},{3,1},{4,6},{5,7},{6,4},{7,5},{8,10},{9,11},{10,... | collective-permute-start | bytes 3538952 | tf_op jit(solution)/shard_map/ppermute | solution.py:188
  266.9 20.4 %collective-permute-start.50 = (bf16[16,768]{1,0:T(8,128)(2,1)}, bf16[16,768]{1,0:T(8,128)(2,1)}, u32[]{:S(2)}, u32[]{:S(2)}) collective-permute-start(bf16[16,768]{1,0:T(8,128)(2,1)} %get-tuple-element.191), channel_id=1, source_target_pairs={{24,0},{25,1},{26,2},{27,3},{28,4},{29,5},{30,6},{31,7}} | collective-permute-start | bytes 73736 | tf_op jit(solution)/shard_map/ppermute | solution.py:188
  268.2 20.5 %collective-permute-start.49 = (bf16[16,768]{1,0:T(8,128)(2,1)}, bf16[16,768]{1,0:T(8,128)(2,1)}, u32[]{:S(2)}, u32[]{:S(2)}) collective-permute-start(bf16[16,768]{1,0:T(8,128)(2,1)} %get-tuple-element.192), channel_id=1, source_target_pairs={{0,24},{1,25},{2,26},{3,27},{4,28},{5,29},{6,30},{7,31}} | collective-permute-start | bytes 73736 | tf_op jit(solution)/shard_map/ppermute | solution.py:188
  294.4 15.4 %collective-permute-start.20 = (bf16[4,2,2,96,384]{4,3,2,1,0:T(8,128)(2,1)}, bf16[4,2,2,96,384]{4,3,2,1,0:T(8,128)(2,1)}, u32[]{:S(2)}, u32[]{:S(2)}) collective-permute-start(bf16[4,2,2,96,384]{4,3,2,1,0:T(8,128)(2,1)} %dynamic-slice_bitcast_fusion), channel_id=1, source_target_pairs={{0,2},{1,3},{2,0},{3,1},{4,6},{5,7},{6,4},{7,5},{8,10},{9,11},{10,... | collective-permute-start | bytes 3538952 | tf_op jit(solution)/shard_map/ppermute | solution.py:188
  307.9 15.6 %collective-permute-start.32 = (bf16[4,96,384]{2,1,0:T(8,128)(2,1)S(1)}, bf16[4,96,384]{2,1,0:T(8,128)(2,1)S(1)}, u32[]{:S(2)}, u32[]{:S(2)}) collective-permute-start(bf16[4,96,384]{2,1,0:T(8,128)(2,1)S(1)} %get-tuple-element.160), channel_id=1, source_target_pairs={{0,1},{1,0},{2,3},{3,2},{4,5},{5,4},{6,7},{7,6},{8,9},{9,8},{10,11... | collective-permute-start | bytes 884744 | tf_op jit(solution)/shard_map/ppermute | solution.py:188
  311.5 20.0 %collective-permute-start.23 = (bf16[4,96,384]{2,1,0:T(8,128)(2,1)S(1)}, bf16[4,96,384]{2,1,0:T(8,128)(2,1)S(1)}, u32[]{:S(2)}, u32[]{:S(2)}) collective-permute-start(bf16[4,96,384]{2,1,0:T(8,128)(2,1)S(1)} %get-tuple-element.156), channel_id=1, source_target_pairs={{0,5},{1,4},{2,7},{3,6},{4,1},{5,0},{6,3},{7,2},{8,13},{9,12},{10,... | collective-permute-start | bytes 884744 | tf_op jit(solution)/shard_map/ppermute | solution.py:188
  313.2 21.9 %collective-permute-start.22 = (bf16[4,96,384]{2,1,0:T(8,128)(2,1)S(1)}, bf16[4,96,384]{2,1,0:T(8,128)(2,1)S(1)}, u32[]{:S(2)}, u32[]{:S(2)}) collective-permute-start(bf16[4,96,384]{2,1,0:T(8,128)(2,1)S(1)} %get-tuple-element.157), channel_id=1, source_target_pairs={{0,1},{1,0},{2,3},{3,2},{4,5},{5,4},{6,7},{7,6},{8,9},{9,8},{10,11... | collective-permute-start | bytes 884744 | tf_op jit(solution)/shard_map/ppermute | solution.py:188
  317.1 21.2 %collective-permute-start.21 = (bf16[4,96,384]{2,1,0:T(8,128)(2,1)S(1)}, bf16[4,96,384]{2,1,0:T(8,128)(2,1)S(1)}, u32[]{:S(2)}, u32[]{:S(2)}) collective-permute-start(bf16[4,96,384]{2,1,0:T(8,128)(2,1)S(1)} %get-tuple-element.155), channel_id=1, source_target_pairs={{0,4},{1,5},{2,6},{3,7},{4,0},{5,1},{6,2},{7,3},{8,12},{9,13},{10,... | collective-permute-start | bytes 884744 | tf_op jit(solution)/shard_map/ppermute | solution.py:188
  323.8 16.2 %collective-permute-start.39 = (bf16[96,384]{1,0:T(8,128)(2,1)S(1)}, bf16[96,384]{1,0:T(8,128)(2,1)S(1)}, u32[]{:S(2)}, u32[]{:S(2)}) collective-permute-start(bf16[96,384]{1,0:T(8,128)(2,1)S(1)} %get-tuple-element.185), channel_id=1, source_target_pairs={{24,0},{25,1},{26,2},{27,3},{28,4},{29,5},{30,6},{31,7}} | collective-permute-start | bytes 221192 | tf_op jit(solution)/shard_map/ppermute | solution.py:188
  325.2 20.1 %collective-permute-start.38 = (bf16[96,384]{1,0:T(8,128)(2,1)S(1)}, bf16[96,384]{1,0:T(8,128)(2,1)S(1)}, u32[]{:S(2)}, u32[]{:S(2)}) collective-permute-start(bf16[96,384]{1,0:T(8,128)(2,1)S(1)} %get-tuple-element.186), channel_id=1, source_target_pairs={{0,24},{1,25},{2,26},{3,27},{4,28},{5,29},{6,30},{7,31}} | collective-permute-start | bytes 221192 | tf_op jit(solution)/shard_map/ppermute | solution.py:188
  331.6 15.0 %collective-permute-start.37 = (bf16[96,384]{1,0:T(8,128)(2,1)S(1)}, bf16[96,384]{1,0:T(8,128)(2,1)S(1)}, u32[]{:S(2)}, u32[]{:S(2)}) collective-permute-start(bf16[96,384]{1,0:T(8,128)(2,1)S(1)} %get-tuple-element.187), channel_id=1, source_target_pairs={{16,0},{17,1},{18,2},{19,3},{20,4},{21,5},{22,6},{23,7},{24,8},{25... | collective-permute-start | bytes 221192 | tf_op jit(solution)/shard_map/ppermute | solution.py:188
  335.1 17.9 %collective-permute-start.36 = (bf16[96,384]{1,0:T(8,128)(2,1)S(1)}, bf16[96,384]{1,0:T(8,128)(2,1)S(1)}, u32[]{:S(2)}, u32[]{:S(2)}) collective-permute-start(bf16[96,384]{1,0:T(8,128)(2,1)S(1)} %get-tuple-element.188), channel_id=1, source_target_pairs={{0,16},{1,17},{2,18},{3,19},{4,20},{5,21},{6,22},{7,23},{8,24},{9,... | collective-permute-start | bytes 221192 | tf_op jit(solution)/shard_map/ppermute | solution.py:188
  338.4 15.9 %collective-permute-start.35 = (bf16[96,384]{1,0:T(8,128)(2,1)S(1)}, bf16[96,384]{1,0:T(8,128)(2,1)S(1)}, u32[]{:S(2)}, u32[]{:S(2)}) collective-permute-start(bf16[96,384]{1,0:T(8,128)(2,1)S(1)} %get-tuple-element.189), channel_id=1, source_target_pairs={{8,0},{9,1},{10,2},{11,3},{12,4},{13,5},{14,6},{15,7},{16,8},{17,9... | collective-permute-start | bytes 221192 | tf_op jit(solution)/shard_map/ppermute | solution.py:188
  340.0 21.0 %collective-permute-start.34 = (bf16[96,384]{1,0:T(8,128)(2,1)S(1)}, bf16[96,384]{1,0:T(8,128)(2,1)S(1)}, u32[]{:S(2)}, u32[]{:S(2)}) collective-permute-start(bf16[96,384]{1,0:T(8,128)(2,1)S(1)} %get-tuple-element.184), channel_id=1, source_target_pairs={{0,8},{1,9},{2,10},{3,11},{4,12},{5,13},{6,14},{7,15},{8,16},{9,17... | collective-permute-start | bytes 221192 | tf_op jit(solution)/shard_map/ppermute | solution.py:188
  345.3 17.0 %collective-permute-start.29 = (bf16[96,384]{1,0:T(8,128)(2,1)S(1)}, bf16[96,384]{1,0:T(8,128)(2,1)S(1)}, u32[]{:S(2)}, u32[]{:S(2)}) collective-permute-start(bf16[96,384]{1,0:T(8,128)(2,1)S(1)} %get-tuple-element.179), channel_id=1, source_target_pairs={{24,0},{25,1},{26,2},{27,3},{28,4},{29,5},{30,6},{31,7}} | collective-permute-start | bytes 221192 | tf_op jit(solution)/shard_map/ppermute | solution.py:188
  346.6 22.0 %collective-permute-start.28 = (bf16[96,384]{1,0:T(8,128)(2,1)}, bf16[96,384]{1,0:T(8,128)(2,1)S(1)}, u32[]{:S(2)}, u32[]{:S(2)}) collective-permute-start(bf16[96,384]{1,0:T(8,128)(2,1)} %get-tuple-element.180), channel_id=1, source_target_pairs={{0,24},{1,25},{2,26},{3,27},{4,28},{5,29},{6,30},{7,31}} | collective-permute-start | bytes 221192 | tf_op jit(solution)/shard_map/ppermute | solution.py:188
  353.0 17.2 %collective-permute-start.27 = (bf16[96,384]{1,0:T(8,128)(2,1)}, bf16[96,384]{1,0:T(8,128)(2,1)}, u32[]{:S(2)}, u32[]{:S(2)}) collective-permute-start(bf16[96,384]{1,0:T(8,128)(2,1)} %get-tuple-element.181), channel_id=1, source_target_pairs={{16,0},{17,1},{18,2},{19,3},{20,4},{21,5},{22,6},{23,7},{24,8},{25... | collective-permute-start | bytes 221192 | tf_op jit(solution)/shard_map/ppermute | solution.py:188
  354.3 15.9 %collective-permute-start.26 = (bf16[96,384]{1,0:T(8,128)(2,1)}, bf16[96,384]{1,0:T(8,128)(2,1)}, u32[]{:S(2)}, u32[]{:S(2)}) collective-permute-start(bf16[96,384]{1,0:T(8,128)(2,1)} %get-tuple-element.182), channel_id=1, source_target_pairs={{0,16},{1,17},{2,18},{3,19},{4,20},{5,21},{6,22},{7,23},{8,24},{9,... | collective-permute-start | bytes 221192 | tf_op jit(solution)/shard_map/ppermute | solution.py:188
  (97 other events, 1056.9 us)
Sparse Core Ops, SparseCore 0:
  11.5 100.2 all-gather.1
  183.3 115.8 reduce-scatter.1

commit v8 on v6

--- a/solution.py
+++ b/solution.py
@@ -188,13 +188,14 @@
     return lax.ppermute(tuple(arrays), ("fsdp", "dp"), pairs)
 
 
-def staged_reduce_scatter(arrays):
+def staged_reduce_scatter(arrays, late=()):
     me, y_place, core, x_place, z_place = flat_coordinates()
-    blocks = [entries.reshape((4, 2, 2, 2) + entries.shape[1:]) for entries in arrays]
-    keep = [lax.dynamic_index_in_dim(b, core, axis=2, keepdims=False) for b in blocks]
-    send = [lax.dynamic_index_in_dim(b, 1 - core, axis=2, keepdims=False).astype(jnp.bfloat16) for b in blocks]
+    blocks = [jnp.moveaxis(entries.reshape((4, 2, 2, 2) + entries.shape[1:]), 2, 0) for entries in arrays]
+    keep = [lax.dynamic_index_in_dim(b, core, axis=0, keepdims=False) for b in blocks]
+    send = [lax.dynamic_index_in_dim(b, 1 - core, axis=0, keepdims=False).astype(jnp.bfloat16) for b in blocks]
     received = permute(send, flipped(2))
     plane = [k.astype(jnp.float32) + r.astype(jnp.float32) for k, r in zip(keep, received)]
+    plane, late = lax.optimization_barrier((plane, late))
 
     def pick(entries, x_index, y_index):
         picked = lax.dynamic_index_in_dim(entries, x_index, axis=1, keepdims=False)
@@ -215,7 +216,7 @@
             shifted(-8 * distance),
         )
         owned = [o + u.astype(jnp.float32) + w.astype(jnp.float32) for o, u, w in zip(owned, up, down)]
-    return owned
+    return owned, late
 
 
 def staged_all_gather(arrays):
@@ -269,7 +270,7 @@
     return attention_full, feed_full, small_full
 
 
-def scatter_gradients(attention_pieces, feed_pieces, small_grad_all, partials, staged):
+def scatter_gradients(attention_pieces, feed_pieces, small_grad_all, partials, staged, late):
     owners = lax.psum(1, ("fsdp", "dp"))
     me = lax.axis_index(("fsdp", "dp"))
     attention_rows = sum(piece.shape[0] for piece in attention_pieces) // owners
@@ -304,9 +305,10 @@
     block_rows = attention_rows + extra_rows
     if staged:
         attention_grad_all = jnp.concatenate(attention_pieces, axis=0).astype(jnp.bfloat16)
-        owned = jnp.concatenate(
-            staged_reduce_scatter([attention_grad_all.reshape(owners, attention_rows, D), extra]), axis=0
-        )
+        owned_parts, late = staged_reduce_scatter(
+            [attention_grad_all.reshape(owners, attention_rows, D), extra], late
+        )
+        owned = jnp.concatenate(owned_parts, axis=0)
     else:
         packed = jnp.zeros((owners, block_rows, D), jnp.bfloat16)
         packed = lax.dynamic_update_slice(packed, extra, (0, attention_rows, 0))
@@ -328,7 +330,7 @@
     totals = gathered_partials[0, :half] + gathered_partials[0, half:]
     for index in range(1, owners):
         totals = totals + (gathered_partials[index, :half] + gathered_partials[index, half:])
-    return attention_owned, feed_owned.astype(jnp.float32), small_owned, totals
+    return attention_owned, feed_owned.astype(jnp.float32), small_owned, totals, late
 
 
 def on_device(
@@ -391,7 +393,6 @@
     gelu_slope = gelu_derivative(inner_sum)
     branch_feed = product(active, feed_full[FF : 2 * FF]) + outer_bias
     residual = normed + branch_feed
-    layer_out = layer_norm(residual, second_gain, second_shift).astype(jnp.bfloat16)
     column = token_valid[:, None]
     partials = jnp.stack(
         [
@@ -424,7 +425,7 @@
         .astype(jnp.bfloat16)
         .reshape(2 * FF, D)
     )
-    feed_grad_all, inner_grad_late = lax.optimization_barrier((feed_grad_all, inner_grad))
+    feed_grad_all, inner_grad_late, partials = lax.optimization_barrier((feed_grad_all, inner_grad, partials))
     normed_grad = residual_grad + product(inner_grad_late, inner_weight)
     first_pull = jax.vjp(layer_norm, first_sum, first_gain, first_shift)[1]
     first_sum_grad, first_gain_grad, first_shift_grad = first_pull(normed_grad)
@@ -451,12 +452,6 @@
     value_weight_grad = product_rows(tokens, value_grad)
     query_bias_grad = column_total(query_grad)
     value_bias_grad = column_total(value_grad)
-    tokens_grad = (
-        first_sum_grad
-        + product_cols(query_grad, query_weight)
-        + product_cols(key_grad, key_weight)
-        + product_cols(value_grad, value_weight)
-    )
     small_grad_all = jnp.concatenate(
         [
             query_bias_grad,
@@ -470,13 +465,22 @@
             second_shift_grad,
         ]
     )
-    attention_owned, feed_owned, small_owned, totals = scatter_gradients(
+    attention_owned, feed_owned, small_owned, totals, late = scatter_gradients(
         [query_weight_grad, key_weight_grad, value_weight_grad, output_weight_grad],
         feed_grad_all,
         small_grad_all,
         partials,
         staged,
-    )
+        (first_sum_grad, query_grad, key_grad, value_grad, residual),
+    )
+    first_sum_grad, query_grad, key_grad, value_grad, residual = late
+    tokens_grad = (
+        first_sum_grad
+        + product_cols(query_grad, query_weight)
+        + product_cols(key_grad, key_weight)
+        + product_cols(value_grad, value_weight)
+    )
+    layer_out = layer_norm(residual, second_gain, second_shift).astype(jnp.bfloat16)
     rms_values = jnp.sqrt(totals[:3] / (totals[3] * D))
     step_float = step_count[0].astype(jnp.float32)
     attention_new, attention_first_new, attention_second_new = adam_step(

time: 342 us -> 334 us (0.977)
  waiting for transfers between devices: 72 us -> 40.6 us
  starting transfers between devices: 92.4 us -> 105 us
  local copies, waits for them, and re-layouts: 25.5 us -> 32.8 us
  other arithmetic: 39.8 us -> 45.7 us
    ppermute x40, waiting for transfers between devices: 69 us -> 40.5 us  [permute(): return lax.ppermute(tuple(arrays), ('fsdp', 'dp'), pairs)]
    ppermute x40, starting transfers between devices: 91.1 us -> 103 us  [permute(): return lax.ppermute(tuple(arrays), ('fsdp', 'dp'), pairs)]
    dot_general x1, matrix products: 8.14 us -> 2.14 us  [attend_backward(): jnp.einsum('hqk,qhd->khd', probability_low, grad_heads, preferred_element...]
    dot_general x1, matrix products: 10.8 us -> 14.4 us  [attend_backward(): jnp.einsum('qhd,khd->hqk', grad_heads, head_view(values), preferred_eleme...]
    unnamed x119 -> x127, local copies, waits for them, and re-layouts: 10.7 us -> 13.4 us
  transfers between devices with their start and end apart: 43 -> 43, of which waited for: 13 -> 13; matrix products, arithmetic and copies ran while one was open for 29% -> 32% of each run, Pallas kernels for 0% -> 0%
where the time goes in v8:
time: 334 us; the launch traced here: 330 us
  starting transfers between devices  105 us (31%)
  matrix products  87.7 us (26%)
  other arithmetic  45.7 us (14%)
  waiting for transfers between devices  40.6 us (12%)
  local copies, waits for them, and re-layouts  32.8 us (10%)
  between operations  17.9 us (5%)
    ppermute x40, starting transfers between devices, permute(): return lax.ppermute(tuple(arrays), ('fsdp', 'dp'), pairs)  103 us
    ppermute x40, waiting for transfers between devices, permute(): return lax.ppermute(tuple(arrays), ('fsdp', 'dp'), pairs)  40.5 us
    dot_general x6, matrix products, product_cols(): lax.dot_general(left_side, right_side, (((1,), (1,)), ((), ())), preferre...  36 us
    dot_general x1, matrix products, attend_backward(): jnp.einsum('qhd,khd->hqk', grad_heads, head_view(values), preferred_eleme...  14.4 us
    dot_general x6, matrix products, product(): return jnp.dot(left_side, right_side, preferred_element_type=jnp.float32)  13.9 us
    unnamed x127, local copies, waits for them, and re-layouts  13.4 us
    dot_general x1, matrix products, on_device(): lax.dot_general(jnp.stack([inner_grad, active]), jnp.stack([normed_low, f...  9.1 us
    convert_element_type x1, other arithmetic, attend_backward(): (probability * (probability_grad - inner_total)).astype(jnp.bfloat16)  7.93 us
  transfers between devices with their start and end apart: 43, of which 13 were waited for; matrix products, arithmetic and copies ran while one was open for 32% of the time, Pallas kernels for 0%

profile of v8, /device:TPU:0, one launch (start us, length us, event | category | flops | bytes accessed | tf_op | source)
XLA Modules:
  0.0 329.9 jit_solution(9495310016781164009)
XLA Ops:
  11.4 7.0 %collective-permute-start.1 = (bf16[96,768]{1,0:T(8,128)(2,1)S(1)}, bf16[96,768]{1,0:T(8,128)(2,1)S(1)}, u32[]{:S(2)}, u32[]{:S(2)}) collective-permute-start(bf16[96,768]{1,0:T(8,128)(2,1)S(1)} %convert_element_type.395), channel_id=1, source_target_pairs={{0,24},{1,25},{2,26},{3,27},{4,28},{5,29},{6,30},{7,31}} | collective-permute-start | bytes 442376 | tf_op jit(solution)/shard_map/ppermute | solution.py:188
  19.7 5.5 %collective-permute-start.3 = (bf16[96,768]{1,0:T(8,128)(2,1)S(1)}, bf16[96,768]{1,0:T(8,128)(2,1)S(1)}, u32[]{:S(2)}, u32[]{:S(2)}) collective-permute-start(bf16[96,768]{1,0:T(8,128)(2,1)S(1)} %convert_element_type.395), channel_id=1, source_target_pairs={{0,16},{1,17},{2,18},{3,19},{4,20},{5,21},{6,22},{7,23},{8,24},{9,... | collective-permute-start | bytes 442376 | tf_op jit(solution)/shard_map/ppermute | solution.py:188
  26.6 4.6 %collective-permute-start.5 = (bf16[96,768]{1,0:T(8,128)(2,1)S(1)}, bf16[96,768]{1,0:T(8,128)(2,1)S(1)}, u32[]{:S(2)}, u32[]{:S(2)}) collective-permute-start(bf16[96,768]{1,0:T(8,128)(2,1)S(1)} %convert_element_type.395), channel_id=1, source_target_pairs={{0,8},{1,9},{2,10},{3,11},{4,12},{5,13},{6,14},{7,15},{8,16},{9,17... | collective-permute-start | bytes 442376 | tf_op jit(solution)/shard_map/ppermute | solution.py:188
  31.2 3.2 collective-permute-done.4
  43.2 7.5 %collective-permute-start.11 = (bf16[1,768]{1,0:T(2,128)(2,1)}, bf16[1,768]{1,0:T(2,128)(2,1)}, u32[]{:S(2)}, u32[]{:S(2)}) collective-permute-start(bf16[1,768]{1,0:T(2,128)(2,1)} %get-tuple-element.165), channel_id=1, source_target_pairs={{0,24},{1,25},{2,26},{3,27},{4,28},{5,29},{6,30},{7,31}} | collective-permute-start | bytes 4616 | tf_op jit(solution)/shard_map/ppermute | solution.py:188
  51.4 4.7 %collective-permute-done.6 = bf16[4,96,768]{2,1,0:T(8,128)(2,1)S(1)} collective-permute-done((bf16[4,96,768]{2,1,0:T(8,128)(2,1)S(1)}, bf16[4,96,768]{2,1,0:T(8,128)(2,1)S(1)}, u32[]{:S(2)}, u32[]{:S(2)}) %collective-permute-start.6) | collective-permute-done | bytes 589856 | tf_op jit(solution)/shard_map/ppermute | solution.py:188
  57.5 4.3 %collective-permute-done.7 = bf16[4,96,768]{2,1,0:T(8,128)(2,1)S(1)} collective-permute-done((bf16[4,96,768]{2,1,0:T(8,128)(2,1)S(1)}, bf16[4,96,768]{2,1,0:T(8,128)(2,1)S(1)}, u32[]{:S(2)}, u32[]{:S(2)}) %collective-permute-start.7) | collective-permute-done | bytes 589856 | tf_op jit(solution)/shard_map/ppermute | solution.py:188
  61.7 8.5 %collective-permute-start.13 = (bf16[1,768]{1,0:T(2,128)(2,1)}, bf16[1,768]{1,0:T(2,128)(2,1)}, u32[]{:S(2)}, u32[]{:S(2)}) collective-permute-start(bf16[1,768]{1,0:T(2,128)(2,1)} %get-tuple-element.165), channel_id=1, source_target_pairs={{0,16},{1,17},{2,18},{3,19},{4,20},{5,21},{6,22},{7,23},{8,24},{9,... | collective-permute-start | bytes 4616 | tf_op jit(solution)/shard_map/ppermute | solution.py:188
  70.3 3.0 collective-permute-done.8
  77.8 7.0 %collective-permute-start.15 = (bf16[1,768]{1,0:T(2,128)(2,1)}, bf16[1,768]{1,0:T(2,128)(2,1)S(1)}, u32[]{:S(2)}, u32[]{:S(2)}) collective-permute-start(bf16[1,768]{1,0:T(2,128)(2,1)} %get-tuple-element.165), channel_id=1, source_target_pairs={{0,8},{1,9},{2,10},{3,11},{4,12},{5,13},{6,14},{7,15},{8,16},{9,17... | collective-permute-start | bytes 4616 | tf_op jit(solution)/shard_map/ppermute | solution.py:188
  105.5 3.0 fusion.143
  110.5 2.6 copy-done
  118.1 20.8 %multiply_convert_fusion.2 = (bf16[512,3072]{1,0:T(8,128)(2,1)S(1)}, f32[512,3072]{1,0:T(8,128)}, f32[512,3072]{1,0:T(8,128)}) fusion(f32[3072]{0:T(1024)S(1)} %slice_convert_fusion, bf16[6144,768]{1,0:T(8,128)(2,1)} %all-gather.2.cloned.1.call-done, f32[512,768]{1,0:T(8,128)S(1)} %get-tuple-element.132, f32[768]{0:T(1024)S(1)} %get-tuple-element.159, ...), kind=kOutput, calls=%fused_computation.16 | convolution fusion | flops 2521694208 | bytes 22042624 | tf_op jit(solution)/shard_map/dot_general | solution.py:37
  138.9 2.6 fusion.16
  147.4 2.7 pad_maximum_fusion.1
  150.1 8.1 %fusion.146 = (bf16[3072]{0:T(1024)(128)(2,1)S(1)}, bf16[512,3072]{1,0:T(8,128)(2,1)}) fusion(f32[512,3072]{1,0:T(8,128)} %get-tuple-element.176, f32[3072]{0:T(1024)S(1)} %slice_convert_fusion, f32[512,3072]{1,0:T(8,128)} %get-tuple-element.130, bf16[512,768]{1,0:T(8,128)(2,1)S(1)} %get-tuple-element.120, bf16[6144,768]{1,0:T(8,128)(2,1)S(1)} %copy-done.55), kind=kOutput, calls=%fused_computation.309 | convolution fusion | flops 2434790400 | bytes 21252096 | tf_op jit(solution)/shard_map/dot_general | solution.py:37
  158.2 9.1 %convolution_convert_fusion = bf16[2,3072,768]{2,1,0:T(8,128)(2,1)} fusion(bf16[1,512,3072]{2,1,0:T(8,128)(2,1)S(1)} %bitcast.327, bf16[1,512,3072]{2,1,0:T(8,128)(2,1)} %bitcast.328, bf16[1,512,768]{2,1,0:T(8,128)(2,1)S(1)} %bitcast.319, bf16[1,512,768]{2,1,0:T(8,128)(2,1)S(1)} %get-tuple-element.142), kind=kOutput, calls=%fused_computation.9 | convolution fusion | flops 4840488960 | bytes 17301504 | tf_op jit(solution)/shard_map/dot_general | solution.py:419
  167.3 6.7 %multiply_reduce_fusion.3 = (bf16[768]{0:T(1024)(128)(2,1)S(1)}, f32[512]{0:T(512)S(1)}, bf16[768]{0:T(1024)(128)(2,1)S(1)}, f32[512,768]{1,0:T(8,128)S(1)}) fusion(f32[512,768]{1,0:T(8,128)S(1)} %get-tuple-element.132, f32[512]{0:T(512)S(1)} %fusion.74, f32[512]{0:T(512)S(1)} %broadcast_multiply_fusion.2, f32[768]{0:T(1024)S(1)} %get-tuple-element.160, ...), kind=kOutput, calls=%fused_computation.55 | convolution fusion | flops 2419849216 | bytes 12597248 | tf_op jit(solution)/shard_map/dot_general | solution.py:27
  180.3 14.4 %multiply_reduce_fusion = (f32[12,512]{1,0:T(8,128)S(1)}, f32[12,512,512]{1,2,0:T(8,128)}) fusion(f32[12,512,512]{1,2,0:T(8,128)} %copy-done, f32[12,512]{1,0:T(8,128)S(1)} %log_add_fusion, bf16[512,12,64]{0,2,1:T(8,128)(2,1)} %bitcast.294, bf16[512,12,64]{0,2,1:T(8,128)(2,1)} %bitcast.318), kind=kOutput, calls=%fused_computation.1 | convolution fusion | flops 412084224 | bytes 26787840 | tf_op jit(solution)/shard_map/while/body/eval_jaxpr/qhd,khd->hqk/dot_general | solution.py:110
  194.8 7.9 %multiply_convert_fusion = bf16[12,512,512]{1,2,0:T(8,128)(2,1)S(1)} fusion(f32[12,512,512]{1,2,0:T(8,128)} %get-tuple-element.179, f32[12,512,512]{1,2,0:T(8,128)S(1)} %bitcast.291, f32[12,512]{1,0:T(8,128)S(1)} %get-tuple-element.178, f32[12,512]{1,0:T(8,128)S(1)} %log_add_fusion), kind=kLoop, calls=%fused_computation | loop fusion | flops 12582912 | bytes 31506432 | tf_op jit(solution)/shard_map/while/body/eval_jaxpr/convert_element_type | solution.py:114
  220.9 2.8 concatenate.19
  229.7 3.2 convert_add_fusion
  233.5 3.1 collective-permute-start.34
  245.8 4.4 %collective-permute-start.35 = (bf16[16,768]{1,0:T(8,128)(2,1)S(1)}, bf16[16,768]{1,0:T(8,128)(2,1)S(1)}, u32[]{:S(2)}, u32[]{:S(2)}) collective-permute-start(bf16[16,768]{1,0:T(8,128)(2,1)S(1)} %get-tuple-element.151), channel_id=1, source_target_pairs={{0,8},{1,9},{2,10},{3,11},{4,12},{5,13},{6,14},{7,15},{8,16},{9,17... | collective-permute-start | bytes 73736 | tf_op jit(solution)/shard_map/ppermute | solution.py:188
  251.6 6.2 %collective-permute-start.37 = (bf16[16,768]{1,0:T(8,128)(2,1)S(1)}, bf16[16,768]{1,0:T(8,128)(2,1)S(1)}, u32[]{:S(2)}, u32[]{:S(2)}) collective-permute-start(bf16[16,768]{1,0:T(8,128)(2,1)S(1)} %get-tuple-element.155), channel_id=1, source_target_pairs={{0,16},{1,17},{2,18},{3,19},{4,20},{5,21},{6,22},{7,23},{8,24},{9,... | collective-permute-start | bytes 73736 | tf_op jit(solution)/shard_map/ppermute | solution.py:188
  261.6 5.8 %collective-permute-start.39 = (bf16[16,768]{1,0:T(8,128)(2,1)S(1)}, bf16[16,768]{1,0:T(8,128)(2,1)S(1)}, u32[]{:S(2)}, u32[]{:S(2)}) collective-permute-start(bf16[16,768]{1,0:T(8,128)(2,1)S(1)} %get-tuple-element.153), channel_id=1, source_target_pairs={{0,24},{1,25},{2,26},{3,27},{4,28},{5,29},{6,30},{7,31}} | collective-permute-start | bytes 73736 | tf_op jit(solution)/shard_map/ppermute | solution.py:188
  269.9 5.7 %collective-permute-done.40 = bf16[16,768]{1,0:T(8,128)(2,1)S(1)} collective-permute-done((bf16[16,768]{1,0:T(8,128)(2,1)S(1)}, bf16[16,768]{1,0:T(8,128)(2,1)S(1)}, u32[]{:S(2)}, u32[]{:S(2)}) %collective-permute-start.40) | collective-permute-done | bytes 24608 | tf_op jit(solution)/shard_map/ppermute | solution.py:188
  278.1 7.4 %collective-permute-done.23 = bf16[4,96,768]{2,1,0:T(8,128)(2,1)S(1)} collective-permute-done((bf16[4,96,768]{2,1,0:T(8,128)(2,1)}, bf16[4,96,768]{2,1,0:T(8,128)(2,1)S(1)}, u32[]{:S(2)}, u32[]{:S(2)}) %collective-permute-start.23) | collective-permute-done | bytes 589856 | tf_op jit(solution)/shard_map/ppermute | solution.py:188
  288.1 2.9 collective-permute-start.25
  293.5 7.5 %collective-permute-start.27 = (bf16[96,768]{1,0:T(8,128)(2,1)}, bf16[96,768]{1,0:T(8,128)(2,1)}, u32[]{:S(2)}, u32[]{:S(2)}) collective-permute-start(bf16[96,768]{1,0:T(8,128)(2,1)} %get-tuple-element.147), channel_id=1, source_target_pairs={{0,16},{1,17},{2,18},{3,19},{4,20},{5,21},{6,22},{7,23},{8,24},{9,... | collective-permute-start | bytes 442376 | tf_op jit(solution)/shard_map/ppermute | solution.py:188
  302.4 7.1 %collective-permute-start.29 = (bf16[96,768]{1,0:T(8,128)(2,1)}, bf16[96,768]{1,0:T(8,128)(2,1)}, u32[]{:S(2)}, u32[]{:S(2)}) collective-permute-start(bf16[96,768]{1,0:T(8,128)(2,1)} %get-tuple-element.145), channel_id=1, source_target_pairs={{0,24},{1,25},{2,26},{3,27},{4,28},{5,29},{6,30},{7,31}} | collective-permute-start | bytes 442376 | tf_op jit(solution)/shard_map/ppermute | solution.py:188
  314.2 4.5 %collective-permute-done.30 = bf16[96,768]{1,0:T(8,128)(2,1)} collective-permute-done((bf16[96,768]{1,0:T(8,128)(2,1)}, bf16[96,768]{1,0:T(8,128)(2,1)}, u32[]{:S(2)}, u32[]{:S(2)}) %collective-permute-start.30) | collective-permute-done | bytes 147488 | tf_op jit(solution)/shard_map/ppermute | solution.py:188
  (308 shorter events, 118.3 us)
Async XLA Ops:
  7.2 110.9 %all-gather.2.cloned.1.call-start = ((), (), s32[]{:S(2)}) async-start(), calls=%async_computation.1 | async-start | bytes 9732096 | tf_op jit(solution)/shard_map/all_gather | solution.py:269
  9.1 302.2 %reduce-scatter.2.cloned.1.call-start = ((), (), s32[]{:S(2)}) async-start(), calls=%async_computation.2 | async-start | bytes 10027008 | tf_op jit(solution)/shard_map/reduce_scatter | solution.py:281
  10.1 16.4 %collective-permute-start = (bf16[96,768]{1,0:T(8,128)(2,1)S(1)}, bf16[96,768]{1,0:T(8,128)(2,1)S(1)}, u32[]{:S(2)}, u32[]{:S(2)}) collective-permute-start(bf16[96,768]{1,0:T(8,128)(2,1)S(1)} %convert_element_type.395), channel_id=1, source_target_pairs={{24,0},{25,1},{26,2},{27,3},{28,4},{29,5},{30,6},{31,7}} | collective-permute-start | bytes 442376 | tf_op jit(solution)/shard_map/ppermute | solution.py:188
  11.4 19.8 %collective-permute-start.1 = (bf16[96,768]{1,0:T(8,128)(2,1)S(1)}, bf16[96,768]{1,0:T(8,128)(2,1)S(1)}, u32[]{:S(2)}, u32[]{:S(2)}) collective-permute-start(bf16[96,768]{1,0:T(8,128)(2,1)S(1)} %convert_element_type.395), channel_id=1, source_target_pairs={{0,24},{1,25},{2,26},{3,27},{4,28},{5,29},{6,30},{7,31}} | collective-permute-start | bytes 442376 | tf_op jit(solution)/shard_map/ppermute | solution.py:188
  18.4 12.8 %collective-permute-start.2 = (bf16[96,768]{1,0:T(8,128)(2,1)S(1)}, bf16[96,768]{1,0:T(8,128)(2,1)S(1)}, u32[]{:S(2)}, u32[]{:S(2)}) collective-permute-start(bf16[96,768]{1,0:T(8,128)(2,1)S(1)} %convert_element_type.395), channel_id=1, source_target_pairs={{16,0},{17,1},{18,2},{19,3},{20,4},{21,5},{22,6},{23,7},{24,8},{25... | collective-permute-start | bytes 442376 | tf_op jit(solution)/shard_map/ppermute | solution.py:188
  19.7 11.5 %collective-permute-start.3 = (bf16[96,768]{1,0:T(8,128)(2,1)S(1)}, bf16[96,768]{1,0:T(8,128)(2,1)S(1)}, u32[]{:S(2)}, u32[]{:S(2)}) collective-permute-start(bf16[96,768]{1,0:T(8,128)(2,1)S(1)} %convert_element_type.395), channel_id=1, source_target_pairs={{0,16},{1,17},{2,18},{3,19},{4,20},{5,21},{6,22},{7,23},{8,24},{9,... | collective-permute-start | bytes 442376 | tf_op jit(solution)/shard_map/ppermute | solution.py:188
  36.5 19.7 %collective-permute-start.6 = (bf16[4,96,768]{2,1,0:T(8,128)(2,1)S(1)}, bf16[4,96,768]{2,1,0:T(8,128)(2,1)S(1)}, u32[]{:S(2)}, u32[]{:S(2)}) collective-permute-start(bf16[4,96,768]{2,1,0:T(8,128)(2,1)S(1)} %select_select_fusion), channel_id=1, source_target_pairs={{0,1},{1,0},{2,3},{3,2},{4,5},{5,4},{6,7},{7,6},{8,9},{9,8},{10,11... | collective-permute-start | bytes 1769480 | tf_op jit(solution)/shard_map/ppermute | solution.py:188
  38.2 23.5 %collective-permute-start.7 = (bf16[4,96,768]{2,1,0:T(8,128)(2,1)S(1)}, bf16[4,96,768]{2,1,0:T(8,128)(2,1)S(1)}, u32[]{:S(2)}, u32[]{:S(2)}) collective-permute-start(bf16[4,96,768]{2,1,0:T(8,128)(2,1)S(1)} %select_select_fusion), channel_id=1, source_target_pairs={{0,4},{1,5},{2,6},{3,7},{4,0},{5,1},{6,2},{7,3},{8,12},{9,13},{10,... | collective-permute-start | bytes 1769480 | tf_op jit(solution)/shard_map/ppermute | solution.py:188
  39.7 33.5 %collective-permute-start.8 = (bf16[4,96,768]{2,1,0:T(8,128)(2,1)S(1)}, bf16[4,96,768]{2,1,0:T(8,128)(2,1)}, u32[]{:S(2)}, u32[]{:S(2)}) collective-permute-start(bf16[4,96,768]{2,1,0:T(8,128)(2,1)S(1)} %select_select_fusion), channel_id=1, source_target_pairs={{0,5},{1,4},{2,7},{3,6},{4,1},{5,0},{6,3},{7,2},{8,13},{9,12},{10,... | collective-permute-start | bytes 1769480 | tf_op jit(solution)/shard_map/ppermute | solution.py:188
  42.0 34.6 %collective-permute-start.10 = (bf16[1,768]{1,0:T(2,128)(2,1)}, bf16[1,768]{1,0:T(2,128)(2,1)}, u32[]{:S(2)}, u32[]{:S(2)}) collective-permute-start(bf16[1,768]{1,0:T(2,128)(2,1)} %get-tuple-element.165), channel_id=1, source_target_pairs={{24,0},{25,1},{26,2},{27,3},{28,4},{29,5},{30,6},{31,7}} | collective-permute-start | bytes 4616 | tf_op jit(solution)/shard_map/ppermute | solution.py:188
  43.2 34.6 %collective-permute-start.11 = (bf16[1,768]{1,0:T(2,128)(2,1)}, bf16[1,768]{1,0:T(2,128)(2,1)}, u32[]{:S(2)}, u32[]{:S(2)}) collective-permute-start(bf16[1,768]{1,0:T(2,128)(2,1)} %get-tuple-element.165), channel_id=1, source_target_pairs={{0,24},{1,25},{2,26},{3,27},{4,28},{5,29},{6,30},{7,31}} | collective-permute-start | bytes 4616 | tf_op jit(solution)/shard_map/ppermute | solution.py:188
  56.2 30.7 %collective-permute-start.12 = (bf16[1,768]{1,0:T(2,128)(2,1)}, bf16[1,768]{1,0:T(2,128)(2,1)}, u32[]{:S(2)}, u32[]{:S(2)}) collective-permute-start(bf16[1,768]{1,0:T(2,128)(2,1)} %get-tuple-element.165), channel_id=1, source_target_pairs={{16,0},{17,1},{18,2},{19,3},{20,4},{21,5},{22,6},{23,7},{24,8},{25... | collective-permute-start | bytes 4616 | tf_op jit(solution)/shard_map/ppermute | solution.py:188
  61.7 25.8 %collective-permute-start.13 = (bf16[1,768]{1,0:T(2,128)(2,1)}, bf16[1,768]{1,0:T(2,128)(2,1)}, u32[]{:S(2)}, u32[]{:S(2)}) collective-permute-start(bf16[1,768]{1,0:T(2,128)(2,1)} %get-tuple-element.165), channel_id=1, source_target_pairs={{0,16},{1,17},{2,18},{3,19},{4,20},{5,21},{6,22},{7,23},{8,24},{9,... | collective-permute-start | bytes 4616 | tf_op jit(solution)/shard_map/ppermute | solution.py:188
  76.5 23.4 %collective-permute-start.9 = (bf16[4,2,2,96,768]{4,3,2,1,0:T(8,128)(2,1)}, bf16[4,2,2,96,768]{4,3,2,1,0:T(8,128)(2,1)}, u32[]{:S(2)}, u32[]{:S(2)}) collective-permute-start(bf16[4,2,2,96,768]{4,3,2,1,0:T(8,128)(2,1)} %broadcast_select_fusion), channel_id=1, source_target_pairs={{0,2},{1,3},{2,0},{3,1},{4,6},{5,7},{6,4},{7,5},{8,10},{9,11},{10,... | collective-permute-start | bytes 7077896 | tf_op jit(solution)/shard_map/ppermute | solution.py:188
  76.5 11.7 %collective-permute-start.14 = (bf16[1,768]{1,0:T(2,128)(2,1)}, bf16[1,768]{1,0:T(2,128)(2,1)S(1)}, u32[]{:S(2)}, u32[]{:S(2)}) collective-permute-start(bf16[1,768]{1,0:T(2,128)(2,1)} %get-tuple-element.165), channel_id=1, source_target_pairs={{8,0},{9,1},{10,2},{11,3},{12,4},{13,5},{14,6},{15,7},{16,8},{17,9... | collective-permute-start | bytes 4616 | tf_op jit(solution)/shard_map/ppermute | solution.py:188
  77.8 10.5 %collective-permute-start.15 = (bf16[1,768]{1,0:T(2,128)(2,1)}, bf16[1,768]{1,0:T(2,128)(2,1)S(1)}, u32[]{:S(2)}, u32[]{:S(2)}) collective-permute-start(bf16[1,768]{1,0:T(2,128)(2,1)} %get-tuple-element.165), channel_id=1, source_target_pairs={{0,8},{1,9},{2,10},{3,11},{4,12},{5,13},{6,14},{7,15},{8,16},{9,17... | collective-permute-start | bytes 4616 | tf_op jit(solution)/shard_map/ppermute | solution.py:188
  217.3 12.4 %collective-permute-start.20 = (bf16[4,2,2,96,768]{4,3,0,2,1:T(8,128)(2,1)}, bf16[4,2,2,96,768]{4,3,0,2,1:T(8,128)(2,1)}, u32[]{:S(2)}, u32[]{:S(2)}) collective-permute-start(bf16[4,2,2,96,768]{4,3,0,2,1:T(8,128)(2,1)} %bitcast.286), channel_id=1, source_target_pairs={{0,2},{1,3},{2,0},{3,1},{4,6},{5,7},{6,4},{7,5},{8,10},{9,11},{10,... | collective-permute-start | bytes 7077896 | tf_op jit(solution)/shard_map/ppermute | solution.py:188
  233.0 11.7 %collective-permute-start.32 = (bf16[4,16,768]{2,1,0:T(8,128)(2,1)S(1)}, bf16[4,16,768]{2,1,0:T(8,128)(2,1)S(1)}, u32[]{:S(2)}, u32[]{:S(2)}) collective-permute-start(bf16[4,16,768]{2,1,0:T(8,128)(2,1)S(1)} %get-tuple-element.149), channel_id=1, source_target_pairs={{0,4},{1,5},{2,6},{3,7},{4,0},{5,1},{6,2},{7,3},{8,12},{9,13},{10,... | collective-permute-start | bytes 294920 | tf_op jit(solution)/shard_map/ppermute | solution.py:188
  233.1 11.6 %collective-permute-start.33 = (bf16[4,16,768]{2,1,0:T(8,128)(2,1)S(1)}, bf16[4,16,768]{2,1,0:T(8,128)(2,1)}, u32[]{:S(2)}, u32[]{:S(2)}) collective-permute-start(bf16[4,16,768]{2,1,0:T(8,128)(2,1)S(1)} %get-tuple-element.150), channel_id=1, source_target_pairs={{0,1},{1,0},{2,3},{3,2},{4,5},{5,4},{6,7},{7,6},{8,9},{9,8},{10,11... | collective-permute-start | bytes 294920 | tf_op jit(solution)/shard_map/ppermute | solution.py:188
  233.5 11.2 %collective-permute-start.34 = (bf16[4,16,768]{2,1,0:T(8,128)(2,1)S(1)}, bf16[4,16,768]{2,1,0:T(8,128)(2,1)}, u32[]{:S(2)}, u32[]{:S(2)}) collective-permute-start(bf16[4,16,768]{2,1,0:T(8,128)(2,1)S(1)} %fusion.57), channel_id=1, source_target_pairs={{0,5},{1,4},{2,7},{3,6},{4,1},{5,0},{6,3},{7,2},{8,13},{9,12},{10,... | collective-permute-start | bytes 294920 | tf_op jit(solution)/shard_map/ppermute | solution.py:188
  237.9 40.2 %collective-permute-start.22 = (bf16[4,96,768]{2,1,0:T(8,128)(2,1)}, bf16[4,96,768]{2,1,0:T(8,128)(2,1)}, u32[]{:S(2)}, u32[]{:S(2)}) collective-permute-start(bf16[4,96,768]{2,1,0:T(8,128)(2,1)} %get-tuple-element.133), channel_id=1, source_target_pairs={{0,4},{1,5},{2,6},{3,7},{4,0},{5,1},{6,2},{7,3},{8,12},{9,13},{10,... | collective-permute-start | bytes 1769480 | tf_op jit(solution)/shard_map/ppermute | solution.py:188
  245.8 13.2 %collective-permute-start.35 = (bf16[16,768]{1,0:T(8,128)(2,1)S(1)}, bf16[16,768]{1,0:T(8,128)(2,1)S(1)}, u32[]{:S(2)}, u32[]{:S(2)}) collective-permute-start(bf16[16,768]{1,0:T(8,128)(2,1)S(1)} %get-tuple-element.151), channel_id=1, source_target_pairs={{0,8},{1,9},{2,10},{3,11},{4,12},{5,13},{6,14},{7,15},{8,16},{9,17... | collective-permute-start | bytes 73736 | tf_op jit(solution)/shard_map/ppermute | solution.py:188
  250.3 9.7 %collective-permute-start.36 = (bf16[16,768]{1,0:T(8,128)(2,1)S(1)}, bf16[16,768]{1,0:T(8,128)(2,1)S(1)}, u32[]{:S(2)}, u32[]{:S(2)}) collective-permute-start(bf16[16,768]{1,0:T(8,128)(2,1)S(1)} %get-tuple-element.156), channel_id=1, source_target_pairs={{8,0},{9,1},{10,2},{11,3},{12,4},{13,5},{14,6},{15,7},{16,8},{17,9... | collective-permute-start | bytes 73736 | tf_op jit(solution)/shard_map/ppermute | solution.py:188
  251.6 10.1 %collective-permute-start.37 = (bf16[16,768]{1,0:T(8,128)(2,1)S(1)}, bf16[16,768]{1,0:T(8,128)(2,1)S(1)}, u32[]{:S(2)}, u32[]{:S(2)}) collective-permute-start(bf16[16,768]{1,0:T(8,128)(2,1)S(1)} %get-tuple-element.155), channel_id=1, source_target_pairs={{0,16},{1,17},{2,18},{3,19},{4,20},{5,21},{6,22},{7,23},{8,24},{9,... | collective-permute-start | bytes 73736 | tf_op jit(solution)/shard_map/ppermute | solution.py:188
  257.7 9.7 %collective-permute-start.38 = (bf16[16,768]{1,0:T(8,128)(2,1)S(1)}, bf16[16,768]{1,0:T(8,128)(2,1)S(1)}, u32[]{:S(2)}, u32[]{:S(2)}) collective-permute-start(bf16[16,768]{1,0:T(8,128)(2,1)S(1)} %get-tuple-element.154), channel_id=1, source_target_pairs={{16,0},{17,1},{18,2},{19,3},{20,4},{21,5},{22,6},{23,7},{24,8},{25... | collective-permute-start | bytes 73736 | tf_op jit(solution)/shard_map/ppermute | solution.py:188
  259.1 26.4 %collective-permute-start.23 = (bf16[4,96,768]{2,1,0:T(8,128)(2,1)}, bf16[4,96,768]{2,1,0:T(8,128)(2,1)S(1)}, u32[]{:S(2)}, u32[]{:S(2)}) collective-permute-start(bf16[4,96,768]{2,1,0:T(8,128)(2,1)} %get-tuple-element.135), channel_id=1, source_target_pairs={{0,1},{1,0},{2,3},{3,2},{4,5},{5,4},{6,7},{7,6},{8,9},{9,8},{10,11... | collective-permute-start | bytes 1769480 | tf_op jit(solution)/shard_map/ppermute | solution.py:188
  259.9 25.6 %collective-permute-start.24 = (bf16[4,96,768]{2,1,0:T(8,128)(2,1)}, bf16[4,96,768]{2,1,0:T(8,128)(2,1)S(1)}, u32[]{:S(2)}, u32[]{:S(2)}) collective-permute-start(bf16[4,96,768]{2,1,0:T(8,128)(2,1)} %get-tuple-element.134), channel_id=1, source_target_pairs={{0,5},{1,4},{2,7},{3,6},{4,1},{5,0},{6,3},{7,2},{8,13},{9,12},{10,... | collective-permute-start | bytes 1769480 | tf_op jit(solution)/shard_map/ppermute | solution.py:188
  288.1 21.4 %collective-permute-start.25 = (bf16[96,768]{1,0:T(8,128)(2,1)S(1)}, bf16[96,768]{1,0:T(8,128)(2,1)}, u32[]{:S(2)}, u32[]{:S(2)}) collective-permute-start(bf16[96,768]{1,0:T(8,128)(2,1)S(1)} %get-tuple-element.143), channel_id=1, source_target_pairs={{0,8},{1,9},{2,10},{3,11},{4,12},{5,13},{6,14},{7,15},{8,16},{9,17... | collective-permute-start | bytes 442376 | tf_op jit(solution)/shard_map/ppermute | solution.py:188
  292.2 20.1 %collective-permute-start.26 = (bf16[96,768]{1,0:T(8,128)(2,1)}, bf16[96,768]{1,0:T(8,128)(2,1)}, u32[]{:S(2)}, u32[]{:S(2)}) collective-permute-start(bf16[96,768]{1,0:T(8,128)(2,1)} %get-tuple-element.148), channel_id=1, source_target_pairs={{8,0},{9,1},{10,2},{11,3},{12,4},{13,5},{14,6},{15,7},{16,8},{17,9... | collective-permute-start | bytes 442376 | tf_op jit(solution)/shard_map/ppermute | solution.py:188
  293.5 20.6 %collective-permute-start.27 = (bf16[96,768]{1,0:T(8,128)(2,1)}, bf16[96,768]{1,0:T(8,128)(2,1)}, u32[]{:S(2)}, u32[]{:S(2)}) collective-permute-start(bf16[96,768]{1,0:T(8,128)(2,1)} %get-tuple-element.147), channel_id=1, source_target_pairs={{0,16},{1,17},{2,18},{3,19},{4,20},{5,21},{6,22},{7,23},{8,24},{9,... | collective-permute-start | bytes 442376 | tf_op jit(solution)/shard_map/ppermute | solution.py:188
  301.1 13.1 %collective-permute-start.28 = (bf16[96,768]{1,0:T(8,128)(2,1)}, bf16[96,768]{1,0:T(8,128)(2,1)}, u32[]{:S(2)}, u32[]{:S(2)}) collective-permute-start(bf16[96,768]{1,0:T(8,128)(2,1)} %get-tuple-element.146), channel_id=1, source_target_pairs={{16,0},{17,1},{18,2},{19,3},{20,4},{21,5},{22,6},{23,7},{24,8},{25... | collective-permute-start | bytes 442376 | tf_op jit(solution)/shard_map/ppermute | solution.py:188
  302.4 11.8 %collective-permute-start.29 = (bf16[96,768]{1,0:T(8,128)(2,1)}, bf16[96,768]{1,0:T(8,128)(2,1)}, u32[]{:S(2)}, u32[]{:S(2)}) collective-permute-start(bf16[96,768]{1,0:T(8,128)(2,1)} %get-tuple-element.145), channel_id=1, source_target_pairs={{0,24},{1,25},{2,26},{3,27},{4,28},{5,29},{6,30},{7,31}} | collective-permute-start | bytes 442376 | tf_op jit(solution)/shard_map/ppermute | solution.py:188
  (70 other events, 669.2 us)
Sparse Core Ops, SparseCore 0:
  11.5 97.1 all-gather.1
  167.5 126.0 reduce-scatter.1

commit v9 on v8

--- a/solution.py
+++ b/solution.py
@@ -305,10 +305,8 @@
     block_rows = attention_rows + extra_rows
     if staged:
         attention_grad_all = jnp.concatenate(attention_pieces, axis=0).astype(jnp.bfloat16)
-        owned_parts, late = staged_reduce_scatter(
-            [attention_grad_all.reshape(owners, attention_rows, D), extra], late
-        )
-        owned = jnp.concatenate(owned_parts, axis=0)
+        packed = jnp.concatenate([attention_grad_all.reshape(owners, attention_rows, D), extra], axis=1)
+        (owned,), late = staged_reduce_scatter([packed], late)
     else:
         packed = jnp.zeros((owners, block_rows, D), jnp.bfloat16)
         packed = lax.dynamic_update_slice(packed, extra, (0, attention_rows, 0))

time: 334 us -> 340 us (1.018)
  starting transfers between devices: 105 us -> 80.4 us
  waiting for transfers between devices: 40.6 us -> 63.8 us
  matrix products: 87.7 us -> 98.9 us
    ppermute x40 -> x30, starting transfers between devices: 103 us -> 78.6 us  [permute(): return lax.ppermute(tuple(arrays), ('fsdp', 'dp'), pairs)]
    ppermute x40 -> x30, waiting for transfers between devices: 40.5 us -> 61.3 us  [permute(): return lax.ppermute(tuple(arrays), ('fsdp', 'dp'), pairs)]
    dot_general x1, matrix products: 2.14 us -> 7.86 us  [attend_backward(): jnp.einsum('hqk,qhd->khd', probability_low, grad_heads, preferred_element...]
    unnamed x127 -> x120, local copies, waits for them, and re-layouts: 13.4 us -> 15.9 us
  transfers between devices with their start and end apart: 43 -> 33, of which waited for: 13 -> 15; matrix products, arithmetic and copies ran while one was open for 32% -> 33% of each run, Pallas kernels for 0% -> 0%
where the time goes in v9:
time: 340 us; the launch traced here: 337 us
  matrix products  98.9 us (29%)
  starting transfers between devices  80.4 us (24%)
  waiting for transfers between devices  63.8 us (19%)
  other arithmetic  45.7 us (13%)
  local copies, waits for them, and re-layouts  30.2 us (9%)
  between operations  17.7 us (5%)
    ppermute x30, starting transfers between devices, permute(): return lax.ppermute(tuple(arrays), ('fsdp', 'dp'), pairs)  78.6 us
    ppermute x30, waiting for transfers between devices, permute(): return lax.ppermute(tuple(arrays), ('fsdp', 'dp'), pairs)  61.3 us
    dot_general x6, matrix products, product_cols(): lax.dot_general(left_side, right_side, (((1,), (1,)), ((), ())), preferre...  36 us
    unnamed x120, local copies, waits for them, and re-layouts  15.9 us
    dot_general x1, matrix products, attend_backward(): jnp.einsum('qhd,khd->hqk', grad_heads, head_view(values), preferred_eleme...  14.5 us
    dot_general x6, matrix products, product(): return jnp.dot(left_side, right_side, preferred_element_type=jnp.float32)  13.9 us
    dot_general x1, matrix products, on_device(): lax.dot_general(jnp.stack([inner_grad, active]), jnp.stack([normed_low, f...  9.13 us
    dot_general x1, matrix products, attend_backward(): jnp.einsum('hqk,qhd->khd', probability_low, grad_heads, preferred_element...  7.86 us
  transfers between devices with their start and end apart: 33, of which 15 were waited for; matrix products, arithmetic and copies ran while one was open for 33% of the time, Pallas kernels for 0%

profile of v9, /device:TPU:0, one launch (start us, length us, event | category | flops | bytes accessed | tf_op | source)
XLA Modules:
  0.0 336.7 jit_solution(5681322170441652858)
XLA Ops:
  11.4 7.0 %collective-permute-start.1 = (bf16[96,768]{1,0:T(8,128)(2,1)S(1)}, bf16[96,768]{1,0:T(8,128)(2,1)S(1)}, u32[]{:S(2)}, u32[]{:S(2)}) collective-permute-start(bf16[96,768]{1,0:T(8,128)(2,1)S(1)} %convert_element_type.306), channel_id=1, source_target_pairs={{0,24},{1,25},{2,26},{3,27},{4,28},{5,29},{6,30},{7,31}} | collective-permute-start | bytes 442376 | tf_op jit(solution)/shard_map/ppermute | solution.py:188
  19.7 5.5 %collective-permute-start.3 = (bf16[96,768]{1,0:T(8,128)(2,1)S(1)}, bf16[96,768]{1,0:T(8,128)(2,1)S(1)}, u32[]{:S(2)}, u32[]{:S(2)}) collective-permute-start(bf16[96,768]{1,0:T(8,128)(2,1)S(1)} %convert_element_type.306), channel_id=1, source_target_pairs={{0,16},{1,17},{2,18},{3,19},{4,20},{5,21},{6,22},{7,23},{8,24},{9,... | collective-permute-start | bytes 442376 | tf_op jit(solution)/shard_map/ppermute | solution.py:188
  26.6 4.6 %collective-permute-start.5 = (bf16[96,768]{1,0:T(8,128)(2,1)S(1)}, bf16[96,768]{1,0:T(8,128)(2,1)S(1)}, u32[]{:S(2)}, u32[]{:S(2)}) collective-permute-start(bf16[96,768]{1,0:T(8,128)(2,1)S(1)} %convert_element_type.306), channel_id=1, source_target_pairs={{0,8},{1,9},{2,10},{3,11},{4,12},{5,13},{6,14},{7,15},{8,16},{9,17... | collective-permute-start | bytes 442376 | tf_op jit(solution)/shard_map/ppermute | solution.py:188
  31.2 3.2 collective-permute-done.4
  43.2 7.5 %collective-permute-start.11 = (bf16[1,768]{1,0:T(2,128)(2,1)}, bf16[1,768]{1,0:T(2,128)(2,1)}, u32[]{:S(2)}, u32[]{:S(2)}) collective-permute-start(bf16[1,768]{1,0:T(2,128)(2,1)} %get-tuple-element.155), channel_id=1, source_target_pairs={{0,24},{1,25},{2,26},{3,27},{4,28},{5,29},{6,30},{7,31}} | collective-permute-start | bytes 4616 | tf_op jit(solution)/shard_map/ppermute | solution.py:188
  51.4 4.7 %collective-permute-done.6 = bf16[4,96,768]{2,1,0:T(8,128)(2,1)S(1)} collective-permute-done((bf16[4,96,768]{2,1,0:T(8,128)(2,1)S(1)}, bf16[4,96,768]{2,1,0:T(8,128)(2,1)S(1)}, u32[]{:S(2)}, u32[]{:S(2)}) %collective-permute-start.6) | collective-permute-done | bytes 589856 | tf_op jit(solution)/shard_map/ppermute | solution.py:188
  57.5 4.3 %collective-permute-done.7 = bf16[4,96,768]{2,1,0:T(8,128)(2,1)S(1)} collective-permute-done((bf16[4,96,768]{2,1,0:T(8,128)(2,1)S(1)}, bf16[4,96,768]{2,1,0:T(8,128)(2,1)S(1)}, u32[]{:S(2)}, u32[]{:S(2)}) %collective-permute-start.7) | collective-permute-done | bytes 589856 | tf_op jit(solution)/shard_map/ppermute | solution.py:188
  61.7 8.5 %collective-permute-start.13 = (bf16[1,768]{1,0:T(2,128)(2,1)}, bf16[1,768]{1,0:T(2,128)(2,1)}, u32[]{:S(2)}, u32[]{:S(2)}) collective-permute-start(bf16[1,768]{1,0:T(2,128)(2,1)} %get-tuple-element.155), channel_id=1, source_target_pairs={{0,16},{1,17},{2,18},{3,19},{4,20},{5,21},{6,22},{7,23},{8,24},{9,... | collective-permute-start | bytes 4616 | tf_op jit(solution)/shard_map/ppermute | solution.py:188
  70.3 3.0 collective-permute-done.8
  77.8 7.0 %collective-permute-start.15 = (bf16[1,768]{1,0:T(2,128)(2,1)}, bf16[1,768]{1,0:T(2,128)(2,1)S(1)}, u32[]{:S(2)}, u32[]{:S(2)}) collective-permute-start(bf16[1,768]{1,0:T(2,128)(2,1)} %get-tuple-element.155), channel_id=1, source_target_pairs={{0,8},{1,9},{2,10},{3,11},{4,12},{5,13},{6,14},{7,15},{8,16},{9,17... | collective-permute-start | bytes 4616 | tf_op jit(solution)/shard_map/ppermute | solution.py:188
  105.5 3.0 fusion.129
  110.5 2.6 copy-done
  118.2 20.8 %multiply_convert_fusion.2 = (bf16[512,3072]{1,0:T(8,128)(2,1)S(1)}, f32[512,3072]{1,0:T(8,128)}, f32[512,3072]{1,0:T(8,128)}) fusion(f32[3072]{0:T(1024)S(1)} %slice_convert_fusion, bf16[6144,768]{1,0:T(8,128)(2,1)} %all-gather.2.cloned.1.call-done, f32[512,768]{1,0:T(8,128)S(1)} %get-tuple-element.130, f32[768]{0:T(1024)S(1)} %get-tuple-element.149, ...), kind=kOutput, calls=%fused_computation.18 | convolution fusion | flops 2521694208 | bytes 22042624 | tf_op jit(solution)/shard_map/dot_general | solution.py:37
  138.9 2.6 fusion.16
  147.5 2.7 pad_maximum_fusion.1
  150.1 8.2 %fusion.132 = (bf16[3072]{0:T(1024)(128)(2,1)S(1)}, bf16[512,3072]{1,0:T(8,128)(2,1)}) fusion(f32[512,3072]{1,0:T(8,128)} %get-tuple-element.166, f32[3072]{0:T(1024)S(1)} %slice_convert_fusion, f32[512,3072]{1,0:T(8,128)} %get-tuple-element.128, bf16[512,768]{1,0:T(8,128)(2,1)S(1)} %get-tuple-element.118, bf16[6144,768]{1,0:T(8,128)(2,1)S(1)} %copy-done.51), kind=kOutput, calls=%fused_computation.284 | convolution fusion | flops 2434790400 | bytes 21252096 | tf_op jit(solution)/shard_map/dot_general | solution.py:37
  158.3 9.1 %convolution_convert_fusion = bf16[2,3072,768]{2,1,0:T(8,128)(2,1)} fusion(bf16[1,512,3072]{2,1,0:T(8,128)(2,1)S(1)} %bitcast.285, bf16[1,512,3072]{2,1,0:T(8,128)(2,1)} %bitcast.286, bf16[1,512,768]{2,1,0:T(8,128)(2,1)S(1)} %bitcast.277, bf16[1,512,768]{2,1,0:T(8,128)(2,1)S(1)} %get-tuple-element.140), kind=kOutput, calls=%fused_computation.11 | convolution fusion | flops 4840488960 | bytes 17301504 | tf_op jit(solution)/shard_map/dot_general | solution.py:417
  167.5 6.7 %multiply_reduce_fusion.3 = (bf16[768]{0:T(1024)(128)(2,1)S(1)}, f32[512]{0:T(512)S(1)}, bf16[768]{0:T(1024)(128)(2,1)S(1)}, f32[512,768]{1,0:T(8,128)S(1)}) fusion(f32[512,768]{1,0:T(8,128)S(1)} %get-tuple-element.130, f32[512]{0:T(512)S(1)} %fusion.60, f32[512]{0:T(512)S(1)} %broadcast_multiply_fusion.2, f32[768]{0:T(1024)S(1)} %get-tuple-element.150, ...), kind=kOutput, calls=%fused_computation.61 | convolution fusion | flops 2419849216 | bytes 12597248 | tf_op jit(solution)/shard_map/dot_general | solution.py:27
  180.4 14.5 %multiply_reduce_fusion = (f32[12,512]{1,0:T(8,128)S(1)}, f32[12,512,512]{1,2,0:T(8,128)}) fusion(f32[12,512,512]{1,2,0:T(8,128)} %copy-done, f32[12,512]{1,0:T(8,128)S(1)} %log_add_fusion, bf16[512,12,64]{0,2,1:T(8,128)(2,1)} %bitcast.253, bf16[512,12,64]{0,2,1:T(8,128)(2,1)} %bitcast.276), kind=kOutput, calls=%fused_computation.1 | convolution fusion | flops 412084224 | bytes 26787840 | tf_op jit(solution)/shard_map/while/body/eval_jaxpr/qhd,khd->hqk/dot_general | solution.py:110
  194.9 7.7 %multiply_convert_fusion = bf16[12,512,512]{1,2,0:T(8,128)(2,1)S(1)} fusion(f32[12,512,512]{1,2,0:T(8,128)} %get-tuple-element.169, f32[12,512,512]{1,2,0:T(8,128)S(1)} %bitcast.250, f32[12,512]{1,0:T(8,128)S(1)} %get-tuple-element.168, f32[12,512]{1,0:T(8,128)S(1)} %log_add_fusion), kind=kLoop, calls=%fused_computation | loop fusion | flops 12582912 | bytes 31506432 | tf_op jit(solution)/shard_map/while/body/eval_jaxpr/convert_element_type | solution.py:114
  205.6 7.9 %fusion.131 = (bf16[12,64]{1,0:T(8,128)(2,1)S(1)}, bf16[12,64,512]{2,1,0:T(8,128)(2,1)}) fusion(bf16[512,12,64]{0,2,1:T(8,128)(2,1)} %bitcast.254, f32[12,512,512]{1,2,0:T(8,128)} %copy-done, f32[12,512]{1,0:T(8,128)S(1)} %log_add_fusion), kind=kOutput, calls=%fused_computation.283 | convolution fusion | flops 409730304 | bytes 14181888 | tf_op jit(solution)/shard_map/while/body/eval_jaxpr/hqk,qhd->khd/dot_general | solution.py:107
  223.1 4.9 %multiply_convert_fusion.3 = bf16[12,64,512]{2,1,0:T(8,128)(2,1)S(1)} fusion(bf16[512,12,64]{0,2,1:T(8,128)(2,1)S(1)} %bitcast.266, bf16[12,512,512]{1,2,0:T(8,128)(2,1)} %copy-done.1), kind=kOutput, calls=%fused_computation.62 | convolution fusion | flops 403439616 | bytes 7864320 | tf_op jit(solution)/shard_map/while/body/eval_jaxpr/hqk,qhd->khd/dot_general | solution.py:123
  236.1 4.4 %collective-permute-done.20 = bf16[4,2,2,112,768]{4,3,0,2,1:T(8,128)(2,1)} collective-permute-done((bf16[4,2,2,112,768]{4,3,0,2,1:T(8,128)(2,1)}, bf16[4,2,2,112,768]{4,3,0,2,1:T(8,128)(2,1)}, u32[]{:S(2)}, u32[]{:S(2)}) %collective-permute-start.20) | collective-permute-done | bytes 2752544 | tf_op jit(solution)/shard_map/ppermute | solution.py:188
  240.5 3.5 %convert_add_fusion = f32[4,2,2,112,768]{4,3,0,2,1:T(8,128)S(1)} fusion(bf16[4,2,2,112,768]{4,3,0,2,1:T(8,128)(2,1)} %collective-permute-done.20, bf16[4,2,1,2,112,768]{5,4,3,2,1,0:T(8,128)(2,1)} %get-tuple-element.134), kind=kLoop, calls=%fused_computation.34 | loop fusion | flops 4128768 | bytes 11010048 | tf_op jit(solution)/shard_map/add | solution.py:197
  248.2 3.1 collective-permute-start.23
  257.9 14.9 %collective-permute-done.21 = bf16[4,112,768]{2,1,0:T(8,128)(2,1)} collective-permute-done((bf16[4,112,768]{2,1,0:T(8,128)(2,1)}, bf16[4,112,768]{2,1,0:T(8,128)(2,1)}, u32[]{:S(2)}, u32[]{:S(2)}) %collective-permute-start.21) | collective-permute-done | bytes 688160 | tf_op jit(solution)/shard_map/ppermute | solution.py:188
  272.8 13.3 %collective-permute-done.23 = bf16[4,112,768]{2,1,0:T(8,128)(2,1)} collective-permute-done((bf16[4,112,768]{2,1,0:T(8,128)(2,1)}, bf16[4,112,768]{2,1,0:T(8,128)(2,1)}, u32[]{:S(2)}, u32[]{:S(2)}) %collective-permute-start.23) | collective-permute-done | bytes 688160 | tf_op jit(solution)/shard_map/ppermute | solution.py:188
  288.5 4.7 %collective-permute-start.24 = (bf16[112,768]{1,0:T(8,128)(2,1)S(1)}, bf16[112,768]{1,0:T(8,128)(2,1)S(1)}, u32[]{:S(2)}, u32[]{:S(2)}) collective-permute-start(bf16[112,768]{1,0:T(8,128)(2,1)S(1)} %get-tuple-element.141), channel_id=1, source_target_pairs={{0,8},{1,9},{2,10},{3,11},{4,12},{5,13},{6,14},{7,15},{8,16},{9,17... | collective-permute-start | bytes 516104 | tf_op jit(solution)/shard_map/ppermute | solution.py:188
  294.5 6.2 %collective-permute-start.26 = (bf16[112,768]{1,0:T(8,128)(2,1)S(1)}, bf16[112,768]{1,0:T(8,128)(2,1)S(1)}, u32[]{:S(2)}, u32[]{:S(2)}) collective-permute-start(bf16[112,768]{1,0:T(8,128)(2,1)S(1)} %get-tuple-element.145), channel_id=1, source_target_pairs={{0,16},{1,17},{2,18},{3,19},{4,20},{5,21},{6,22},{7,23},{8,24},{9,... | collective-permute-start | bytes 516104 | tf_op jit(solution)/shard_map/ppermute | solution.py:188
  302.0 5.2 %collective-permute-start.28 = (bf16[112,768]{1,0:T(8,128)(2,1)S(1)}, bf16[112,768]{1,0:T(8,128)(2,1)S(1)}, u32[]{:S(2)}, u32[]{:S(2)}) collective-permute-start(bf16[112,768]{1,0:T(8,128)(2,1)S(1)} %get-tuple-element.143), channel_id=1, source_target_pairs={{0,24},{1,25},{2,26},{3,27},{4,28},{5,29},{6,30},{7,31}} | collective-permute-start | bytes 516104 | tf_op jit(solution)/shard_map/ppermute | solution.py:188
  309.7 3.9 %collective-permute-done.27 = bf16[112,768]{1,0:T(8,128)(2,1)S(1)} collective-permute-done((bf16[112,768]{1,0:T(8,128)(2,1)S(1)}, bf16[112,768]{1,0:T(8,128)(2,1)S(1)}, u32[]{:S(2)}, u32[]{:S(2)}) %collective-permute-start.27) | collective-permute-done | bytes 172064 | tf_op jit(solution)/shard_map/ppermute | solution.py:188
  313.6 2.7 collective-permute-done.29
  (275 shorter events, 111.4 us)
Async XLA Ops:
  7.2 110.9 %all-gather.2.cloned.1.call-start = ((), (), s32[]{:S(2)}) async-start(), calls=%async_computation.1 | async-start | bytes 9732096 | tf_op jit(solution)/shard_map/all_gather | solution.py:269
  9.1 311.1 %reduce-scatter.2.cloned.1.call-start = ((), (), s32[]{:S(2)}) async-start(), calls=%async_computation.2 | async-start | bytes 10027008 | tf_op jit(solution)/shard_map/reduce_scatter | solution.py:281
  10.1 16.4 %collective-permute-start = (bf16[96,768]{1,0:T(8,128)(2,1)S(1)}, bf16[96,768]{1,0:T(8,128)(2,1)S(1)}, u32[]{:S(2)}, u32[]{:S(2)}) collective-permute-start(bf16[96,768]{1,0:T(8,128)(2,1)S(1)} %convert_element_type.306), channel_id=1, source_target_pairs={{24,0},{25,1},{26,2},{27,3},{28,4},{29,5},{30,6},{31,7}} | collective-permute-start | bytes 442376 | tf_op jit(solution)/shard_map/ppermute | solution.py:188
  11.4 19.8 %collective-permute-start.1 = (bf16[96,768]{1,0:T(8,128)(2,1)S(1)}, bf16[96,768]{1,0:T(8,128)(2,1)S(1)}, u32[]{:S(2)}, u32[]{:S(2)}) collective-permute-start(bf16[96,768]{1,0:T(8,128)(2,1)S(1)} %convert_element_type.306), channel_id=1, source_target_pairs={{0,24},{1,25},{2,26},{3,27},{4,28},{5,29},{6,30},{7,31}} | collective-permute-start | bytes 442376 | tf_op jit(solution)/shard_map/ppermute | solution.py:188
  18.4 12.8 %collective-permute-start.2 = (bf16[96,768]{1,0:T(8,128)(2,1)S(1)}, bf16[96,768]{1,0:T(8,128)(2,1)S(1)}, u32[]{:S(2)}, u32[]{:S(2)}) collective-permute-start(bf16[96,768]{1,0:T(8,128)(2,1)S(1)} %convert_element_type.306), channel_id=1, source_target_pairs={{16,0},{17,1},{18,2},{19,3},{20,4},{21,5},{22,6},{23,7},{24,8},{25... | collective-permute-start | bytes 442376 | tf_op jit(solution)/shard_map/ppermute | solution.py:188
  19.7 11.5 %collective-permute-start.3 = (bf16[96,768]{1,0:T(8,128)(2,1)S(1)}, bf16[96,768]{1,0:T(8,128)(2,1)S(1)}, u32[]{:S(2)}, u32[]{:S(2)}) collective-permute-start(bf16[96,768]{1,0:T(8,128)(2,1)S(1)} %convert_element_type.306), channel_id=1, source_target_pairs={{0,16},{1,17},{2,18},{3,19},{4,20},{5,21},{6,22},{7,23},{8,24},{9,... | collective-permute-start | bytes 442376 | tf_op jit(solution)/shard_map/ppermute | solution.py:188
  25.2 9.3 %collective-permute-start.4 = (bf16[96,768]{1,0:T(8,128)(2,1)S(1)}, bf16[96,768]{1,0:T(8,128)(2,1)S(1)}, u32[]{:S(2)}, u32[]{:S(2)}) collective-permute-start(bf16[96,768]{1,0:T(8,128)(2,1)S(1)} %convert_element_type.306), channel_id=1, source_target_pairs={{8,0},{9,1},{10,2},{11,3},{12,4},{13,5},{14,6},{15,7},{16,8},{17,9... | collective-permute-start | bytes 442376 | tf_op jit(solution)/shard_map/ppermute | solution.py:188
  26.6 9.6 %collective-permute-start.5 = (bf16[96,768]{1,0:T(8,128)(2,1)S(1)}, bf16[96,768]{1,0:T(8,128)(2,1)S(1)}, u32[]{:S(2)}, u32[]{:S(2)}) collective-permute-start(bf16[96,768]{1,0:T(8,128)(2,1)S(1)} %convert_element_type.306), channel_id=1, source_target_pairs={{0,8},{1,9},{2,10},{3,11},{4,12},{5,13},{6,14},{7,15},{8,16},{9,17... | collective-permute-start | bytes 442376 | tf_op jit(solution)/shard_map/ppermute | solution.py:188
  36.5 19.7 %collective-permute-start.6 = (bf16[4,96,768]{2,1,0:T(8,128)(2,1)S(1)}, bf16[4,96,768]{2,1,0:T(8,128)(2,1)S(1)}, u32[]{:S(2)}, u32[]{:S(2)}) collective-permute-start(bf16[4,96,768]{2,1,0:T(8,128)(2,1)S(1)} %select_select_fusion), channel_id=1, source_target_pairs={{0,1},{1,0},{2,3},{3,2},{4,5},{5,4},{6,7},{7,6},{8,9},{9,8},{10,11... | collective-permute-start | bytes 1769480 | tf_op jit(solution)/shard_map/ppermute | solution.py:188
  38.2 23.5 %collective-permute-start.7 = (bf16[4,96,768]{2,1,0:T(8,128)(2,1)S(1)}, bf16[4,96,768]{2,1,0:T(8,128)(2,1)S(1)}, u32[]{:S(2)}, u32[]{:S(2)}) collective-permute-start(bf16[4,96,768]{2,1,0:T(8,128)(2,1)S(1)} %select_select_fusion), channel_id=1, source_target_pairs={{0,4},{1,5},{2,6},{3,7},{4,0},{5,1},{6,2},{7,3},{8,12},{9,13},{10,... | collective-permute-start | bytes 1769480 | tf_op jit(solution)/shard_map/ppermute | solution.py:188
  39.7 33.5 %collective-permute-start.8 = (bf16[4,96,768]{2,1,0:T(8,128)(2,1)S(1)}, bf16[4,96,768]{2,1,0:T(8,128)(2,1)}, u32[]{:S(2)}, u32[]{:S(2)}) collective-permute-start(bf16[4,96,768]{2,1,0:T(8,128)(2,1)S(1)} %select_select_fusion), channel_id=1, source_target_pairs={{0,5},{1,4},{2,7},{3,6},{4,1},{5,0},{6,3},{7,2},{8,13},{9,12},{10,... | collective-permute-start | bytes 1769480 | tf_op jit(solution)/shard_map/ppermute | solution.py:188
  42.0 34.6 %collective-permute-start.10 = (bf16[1,768]{1,0:T(2,128)(2,1)}, bf16[1,768]{1,0:T(2,128)(2,1)}, u32[]{:S(2)}, u32[]{:S(2)}) collective-permute-start(bf16[1,768]{1,0:T(2,128)(2,1)} %get-tuple-element.155), channel_id=1, source_target_pairs={{24,0},{25,1},{26,2},{27,3},{28,4},{29,5},{30,6},{31,7}} | collective-permute-start | bytes 4616 | tf_op jit(solution)/shard_map/ppermute | solution.py:188
  43.2 34.6 %collective-permute-start.11 = (bf16[1,768]{1,0:T(2,128)(2,1)}, bf16[1,768]{1,0:T(2,128)(2,1)}, u32[]{:S(2)}, u32[]{:S(2)}) collective-permute-start(bf16[1,768]{1,0:T(2,128)(2,1)} %get-tuple-element.155), channel_id=1, source_target_pairs={{0,24},{1,25},{2,26},{3,27},{4,28},{5,29},{6,30},{7,31}} | collective-permute-start | bytes 4616 | tf_op jit(solution)/shard_map/ppermute | solution.py:188
  56.2 30.7 %collective-permute-start.12 = (bf16[1,768]{1,0:T(2,128)(2,1)}, bf16[1,768]{1,0:T(2,128)(2,1)}, u32[]{:S(2)}, u32[]{:S(2)}) collective-permute-start(bf16[1,768]{1,0:T(2,128)(2,1)} %get-tuple-element.155), channel_id=1, source_target_pairs={{16,0},{17,1},{18,2},{19,3},{20,4},{21,5},{22,6},{23,7},{24,8},{25... | collective-permute-start | bytes 4616 | tf_op jit(solution)/shard_map/ppermute | solution.py:188
  61.7 25.8 %collective-permute-start.13 = (bf16[1,768]{1,0:T(2,128)(2,1)}, bf16[1,768]{1,0:T(2,128)(2,1)}, u32[]{:S(2)}, u32[]{:S(2)}) collective-permute-start(bf16[1,768]{1,0:T(2,128)(2,1)} %get-tuple-element.155), channel_id=1, source_target_pairs={{0,16},{1,17},{2,18},{3,19},{4,20},{5,21},{6,22},{7,23},{8,24},{9,... | collective-permute-start | bytes 4616 | tf_op jit(solution)/shard_map/ppermute | solution.py:188
  76.5 23.4 %collective-permute-start.9 = (bf16[4,2,2,96,768]{4,3,2,1,0:T(8,128)(2,1)}, bf16[4,2,2,96,768]{4,3,2,1,0:T(8,128)(2,1)}, u32[]{:S(2)}, u32[]{:S(2)}) collective-permute-start(bf16[4,2,2,96,768]{4,3,2,1,0:T(8,128)(2,1)} %broadcast_select_fusion), channel_id=1, source_target_pairs={{0,2},{1,3},{2,0},{3,1},{4,6},{5,7},{6,4},{7,5},{8,10},{9,11},{10,... | collective-permute-start | bytes 7077896 | tf_op jit(solution)/shard_map/ppermute | solution.py:188
  76.5 11.7 %collective-permute-start.14 = (bf16[1,768]{1,0:T(2,128)(2,1)}, bf16[1,768]{1,0:T(2,128)(2,1)S(1)}, u32[]{:S(2)}, u32[]{:S(2)}) collective-permute-start(bf16[1,768]{1,0:T(2,128)(2,1)} %get-tuple-element.155), channel_id=1, source_target_pairs={{8,0},{9,1},{10,2},{11,3},{12,4},{13,5},{14,6},{15,7},{16,8},{17,9... | collective-permute-start | bytes 4616 | tf_op jit(solution)/shard_map/ppermute | solution.py:188
  77.8 10.5 %collective-permute-start.15 = (bf16[1,768]{1,0:T(2,128)(2,1)}, bf16[1,768]{1,0:T(2,128)(2,1)S(1)}, u32[]{:S(2)}, u32[]{:S(2)}) collective-permute-start(bf16[1,768]{1,0:T(2,128)(2,1)} %get-tuple-element.155), channel_id=1, source_target_pairs={{0,8},{1,9},{2,10},{3,11},{4,12},{5,13},{6,14},{7,15},{8,16},{9,17... | collective-permute-start | bytes 4616 | tf_op jit(solution)/shard_map/ppermute | solution.py:188
  88.5 3.9 %collective-permute-start.16 = (bf16[4,1,768]{2,0,1:T(4,128)(2,1)S(1)}, bf16[4,1,768]{2,0,1:T(4,128)(2,1)S(1)}, u32[]{:S(2)}, u32[]{:S(2)}) collective-permute-start(bf16[4,1,768]{2,0,1:T(4,128)(2,1)S(1)} %select_select_fusion.1), channel_id=1, source_target_pairs={{0,1},{1,0},{2,3},{3,2},{4,5},{5,4},{6,7},{7,6},{8,9},{9,8},{10,11... | collective-permute-start | bytes 18440 | tf_op jit(solution)/shard_map/ppermute | solution.py:188
  90.2 3.9 %collective-permute-start.17 = (bf16[4,1,768]{2,0,1:T(4,128)(2,1)S(1)}, bf16[4,1,768]{2,0,1:T(4,128)(2,1)S(1)}, u32[]{:S(2)}, u32[]{:S(2)}) collective-permute-start(bf16[4,1,768]{2,0,1:T(4,128)(2,1)S(1)} %select_select_fusion.1), channel_id=1, source_target_pairs={{0,4},{1,5},{2,6},{3,7},{4,0},{5,1},{6,2},{7,3},{8,12},{9,13},{10,... | collective-permute-start | bytes 18440 | tf_op jit(solution)/shard_map/ppermute | solution.py:188
  91.7 4.5 %collective-permute-start.18 = (bf16[4,1,768]{2,0,1:T(4,128)(2,1)S(1)}, bf16[4,1,768]{2,0,1:T(4,128)(2,1)S(1)}, u32[]{:S(2)}, u32[]{:S(2)}) collective-permute-start(bf16[4,1,768]{2,0,1:T(4,128)(2,1)S(1)} %select_select_fusion.1), channel_id=1, source_target_pairs={{0,5},{1,4},{2,7},{3,6},{4,1},{5,0},{6,3},{7,2},{8,13},{9,12},{10,... | collective-permute-start | bytes 18440 | tf_op jit(solution)/shard_map/ppermute | solution.py:188
  235.1 5.4 %collective-permute-start.20 = (bf16[4,2,2,112,768]{4,3,0,2,1:T(8,128)(2,1)}, bf16[4,2,2,112,768]{4,3,0,2,1:T(8,128)(2,1)}, u32[]{:S(2)}, u32[]{:S(2)}) collective-permute-start(bf16[4,2,2,112,768]{4,3,0,2,1:T(8,128)(2,1)} %bitcast.245), channel_id=1, source_target_pairs={{0,2},{1,3},{2,0},{3,1},{4,6},{5,7},{6,4},{7,5},{8,10},{9,11},{10,... | collective-permute-start | bytes 8257544 | tf_op jit(solution)/shard_map/ppermute | solution.py:188
  247.8 24.9 %collective-permute-start.21 = (bf16[4,112,768]{2,1,0:T(8,128)(2,1)}, bf16[4,112,768]{2,1,0:T(8,128)(2,1)}, u32[]{:S(2)}, u32[]{:S(2)}) collective-permute-start(bf16[4,112,768]{2,1,0:T(8,128)(2,1)} %get-tuple-element.131), channel_id=1, source_target_pairs={{0,4},{1,5},{2,6},{3,7},{4,0},{5,1},{6,2},{7,3},{8,12},{9,13},{10,... | collective-permute-start | bytes 2064392 | tf_op jit(solution)/shard_map/ppermute | solution.py:188
  247.8 24.9 %collective-permute-start.22 = (bf16[4,112,768]{2,1,0:T(8,128)(2,1)}, bf16[4,112,768]{2,1,0:T(8,128)(2,1)}, u32[]{:S(2)}, u32[]{:S(2)}) collective-permute-start(bf16[4,112,768]{2,1,0:T(8,128)(2,1)} %get-tuple-element.133), channel_id=1, source_target_pairs={{0,1},{1,0},{2,3},{3,2},{4,5},{5,4},{6,7},{7,6},{8,9},{9,8},{10,11... | collective-permute-start | bytes 2064392 | tf_op jit(solution)/shard_map/ppermute | solution.py:188
  248.2 37.9 %collective-permute-start.23 = (bf16[4,112,768]{2,1,0:T(8,128)(2,1)}, bf16[4,112,768]{2,1,0:T(8,128)(2,1)}, u32[]{:S(2)}, u32[]{:S(2)}) collective-permute-start(bf16[4,112,768]{2,1,0:T(8,128)(2,1)} %get-tuple-element.132), channel_id=1, source_target_pairs={{0,5},{1,4},{2,7},{3,6},{4,1},{5,0},{6,3},{7,2},{8,13},{9,12},{10,... | collective-permute-start | bytes 2064392 | tf_op jit(solution)/shard_map/ppermute | solution.py:188
  288.5 18.7 %collective-permute-start.24 = (bf16[112,768]{1,0:T(8,128)(2,1)S(1)}, bf16[112,768]{1,0:T(8,128)(2,1)S(1)}, u32[]{:S(2)}, u32[]{:S(2)}) collective-permute-start(bf16[112,768]{1,0:T(8,128)(2,1)S(1)} %get-tuple-element.141), channel_id=1, source_target_pairs={{0,8},{1,9},{2,10},{3,11},{4,12},{5,13},{6,14},{7,15},{8,16},{9,17... | collective-permute-start | bytes 516104 | tf_op jit(solution)/shard_map/ppermute | solution.py:188
  293.2 16.5 %collective-permute-start.25 = (bf16[112,768]{1,0:T(8,128)(2,1)S(1)}, bf16[112,768]{1,0:T(8,128)(2,1)S(1)}, u32[]{:S(2)}, u32[]{:S(2)}) collective-permute-start(bf16[112,768]{1,0:T(8,128)(2,1)S(1)} %get-tuple-element.146), channel_id=1, source_target_pairs={{8,0},{9,1},{10,2},{11,3},{12,4},{13,5},{14,6},{15,7},{16,8},{17,9... | collective-permute-start | bytes 516104 | tf_op jit(solution)/shard_map/ppermute | solution.py:188
  294.5 15.2 %collective-permute-start.26 = (bf16[112,768]{1,0:T(8,128)(2,1)S(1)}, bf16[112,768]{1,0:T(8,128)(2,1)S(1)}, u32[]{:S(2)}, u32[]{:S(2)}) collective-permute-start(bf16[112,768]{1,0:T(8,128)(2,1)S(1)} %get-tuple-element.145), channel_id=1, source_target_pairs={{0,16},{1,17},{2,18},{3,19},{4,20},{5,21},{6,22},{7,23},{8,24},{9,... | collective-permute-start | bytes 516104 | tf_op jit(solution)/shard_map/ppermute | solution.py:188
  300.7 12.9 %collective-permute-start.27 = (bf16[112,768]{1,0:T(8,128)(2,1)S(1)}, bf16[112,768]{1,0:T(8,128)(2,1)S(1)}, u32[]{:S(2)}, u32[]{:S(2)}) collective-permute-start(bf16[112,768]{1,0:T(8,128)(2,1)S(1)} %get-tuple-element.144), channel_id=1, source_target_pairs={{16,0},{17,1},{18,2},{19,3},{20,4},{21,5},{22,6},{23,7},{24,8},{25... | collective-permute-start | bytes 516104 | tf_op jit(solution)/shard_map/ppermute | solution.py:188
  302.0 11.6 %collective-permute-start.28 = (bf16[112,768]{1,0:T(8,128)(2,1)S(1)}, bf16[112,768]{1,0:T(8,128)(2,1)S(1)}, u32[]{:S(2)}, u32[]{:S(2)}) collective-permute-start(bf16[112,768]{1,0:T(8,128)(2,1)S(1)} %get-tuple-element.143), channel_id=1, source_target_pairs={{0,24},{1,25},{2,26},{3,27},{4,28},{5,29},{6,30},{7,31}} | collective-permute-start | bytes 516104 | tf_op jit(solution)/shard_map/ppermute | solution.py:188
  307.2 9.1 %collective-permute-start.29 = (bf16[112,768]{1,0:T(8,128)(2,1)S(1)}, bf16[112,768]{1,0:T(8,128)(2,1)S(1)}, u32[]{:S(2)}, u32[]{:S(2)}) collective-permute-start(bf16[112,768]{1,0:T(8,128)(2,1)S(1)} %get-tuple-element.142), channel_id=1, source_target_pairs={{24,0},{25,1},{26,2},{27,3},{28,4},{29,5},{30,6},{31,7}} | collective-permute-start | bytes 516104 | tf_op jit(solution)/shard_map/ppermute | solution.py:188
  321.3 6.8 %collective-permute-start.30 = (bf16[192,768]{1,0:T(8,128)(2,1)S(1)}, bf16[192,768]{1,0:T(8,128)(2,1)S(1)}, u32[]{:S(2)}, u32[]{:S(2)}) collective-permute-start(bf16[192,768]{1,0:T(8,128)(2,1)S(1)} %dynamic-slice_bitcast_fusion), channel_id=1, source_target_pairs={{0,1},{1,0},{2,3},{3,2},{4,5},{5,4},{6,7},{7,6},{8,9},{9,8},{10,11... | collective-permute-start | bytes 884744 | tf_op jit(solution)/shard_map/ppermute | solution.py:286
  (56 other events, 577.7 us)
Sparse Core Ops, SparseCore 0:
  11.5 97.1 all-gather.1
  167.6 115.7 reduce-scatter.1
